TPU v7x, 32 devices: a whole 2x2x4 slice. The times are simulated.
32 devices in a mesh: seq: 16 (over z, y, x), tp: 2 (over core).
Axes of the slice: x: 2, y: 2, z: 4, core: 2. Of those that a mesh axis runs over, the one named last changes fastest.
Arguments:
- prefill_hidden: bfloat16 [2048, 5120], P('seq', 'tp'), may hold values from -14 to 14
- prefill_query_rows: bfloat16 [2048, 5120], P('seq', 'tp'), may hold values from -250 to 250
- prefill_key_value: bfloat16 [2, 2048, 1024], P(None, 'seq', 'tp'), may hold values from -5 to 5
- request_prefix_cache: bfloat16 [2, 16, 768, 1024], P(None, 'seq', None, 'tp'), may hold values from -5 to 5
- prefix_lengths: int32 [16], replicated, may hold values from 0 to 768, as said below
- decode_hidden: bfloat16 [4, 5120], P(None, 'tp'), may hold values from -14 to 14
- decode_query_rows: bfloat16 [4, 5120], P(None, 'tp'), may hold values from -250 to 250
- decode_kv: bfloat16 [2, 4, 1024], P(None, None, 'tp'), may hold values from -5 to 5
- decode_slot_cache: bfloat16 [2, 5, 2048, 1024], P(None, None, 'seq', 'tp'), may hold values from -5 to 5
- cache_lengths: int32 [4], replicated, may hold values from 512 to 2048, as said below
- slot_table: int32 [4], replicated, may hold values from 0 to 4, as said below
- out_weight: bfloat16 [5120, 5120], P('tp', 'seq'), may hold values from -0.078125 to 0.078125
- final_gain: bfloat16 [5120], replicated, may hold values from 0.5 to 1.5
- head_weight: bfloat16 [5120, 152064], P(None, ('seq', 'tp')), may hold values from -4 to 4
Outputs:
- prefill_out: bfloat16 [2048, 5120], P('seq', 'tp')
- decode_out: bfloat16 [4, 5120], P(None, 'tp')
- log_probs: float32 [20, 152064], P(None, ('seq', 'tp'))
Inputs may be any that keep to these rules, and one draw needn't show every extreme that they name: `prefix_lengths`: some request has no cached prefix and some has exactly 768 cached tokens. `cache_lengths`: some request has exactly 2048 cached tokens. `slot_table`: distinct slots.
All inputs are finite; a program needn't handle non-finite values.
Results may differ from a plain program's by a relative error of at most 0.0035.
Values may be sent and summed in bfloat16 or wider, within the bound.
No kernel may reach another device: no remote copies, remote signals or barrier semaphores. Data moves between devices by JAX's collectives and lax.ppermute only.
A program may use at most 128 MiB of HBM per device.

v0:
```python
import math

import jax
import jax.numpy as jnp
from jax import lax
from jax.sharding import PartitionSpec as P

QUERY_HEADS = 40
KEY_HEADS = 8
HEAD_SIZE = 128


neg_large = -1e30
exact = lax.Precision.HIGHEST
norm_eps = 1e-06


def merged(value, axis, join):
    pieces = jax.tree.map(lambda part: lax.all_gather(part, axis), value)
    head = jax.tree.map(lambda part: part[0], pieces)
    tail = jax.tree.map(lambda part: part[1:], pieces)
    subtotal, _ = lax.scan(lambda subtotal, piece: (join(subtotal, piece), None), head, tail)
    return subtotal


def join_parts(earlier, later):
    row_max = jnp.maximum(earlier[0], later[0])
    factor_one = jnp.exp(earlier[0] - row_max)
    factor_two = jnp.exp(later[0] - row_max)
    return (
        row_max,
        earlier[1] * factor_one + later[1] * factor_two,
        earlier[2] * factor_one[..., None] + later[2] * factor_two[..., None],
    )


def join_totals(earlier, later):
    row_max = jnp.maximum(earlier[0], later[0])
    return (
        row_max,
        earlier[1] * jnp.exp(earlier[0] - row_max) + later[1] * jnp.exp(later[0] - row_max),
    )


def local(
    prefill_hidden,
    prefill_query_rows,
    prefill_key_value,
    request_prefix_cache,
    prefix_lengths,
    decode_hidden,
    decode_query_rows,
    decode_kv,
    decode_slot_cache,
    cache_lengths,
    slot_table,
    out_weight,
    final_gain,
    head_weight,
):
    query_group_width = QUERY_HEADS // KEY_HEADS
    score_scale = 1.0 / math.sqrt(HEAD_SIZE)
    kv_local = prefill_key_value.shape[2] // HEAD_SIZE
    seq_index = lax.axis_index("seq")
    span_len = prefill_query_rows.shape[0]
    prefix_len = request_prefix_cache.shape[2]
    prefix_end = lax.dynamic_slice_in_dim(prefix_lengths, seq_index, 1)[0]
    query_matrix = prefill_query_rows.reshape(span_len, kv_local, query_group_width, HEAD_SIZE)
    joined_keys = jnp.concatenate([request_prefix_cache[0, 0], prefill_key_value[0]], 0).reshape(
        prefix_len + span_len, kv_local, HEAD_SIZE
    )
    value_matrix = jnp.concatenate([request_prefix_cache[1, 0], prefill_key_value[1]], 0).reshape(
        prefix_len + span_len, kv_local, HEAD_SIZE
    )
    key_place = jnp.arange(prefix_len + span_len)
    query_place = jnp.arange(span_len)
    live_mask = jnp.where(
        key_place[None, :] < prefix_len,
        key_place[None, :] < prefix_end,
        key_place[None, :] - prefix_len <= query_place[:, None],
    )
    scores = (
        jnp.einsum("rkgh,skh->kgrs", query_matrix, joined_keys, preferred_element_type=jnp.float32)
        * score_scale
    )
    masked = jnp.where(live_mask, scores, neg_large)
    row_max = jnp.max(masked, axis=-1, keepdims=True)
    weights = jnp.where(live_mask, jnp.exp(masked - row_max), 0.0)
    row_sum = jnp.sum(weights, axis=-1)
    weights_low = weights.astype(jnp.bfloat16)
    mixed = jnp.einsum(
        "kgrs,skh->rkgh", weights_low, value_matrix, preferred_element_type=jnp.float32
    )
    prefill_attention = (
        (mixed / jnp.transpose(row_sum, (2, 0, 1))[..., None])
        .astype(jnp.bfloat16)
        .reshape(span_len, -1)
    )
    decode_count = decode_query_rows.shape[0]
    ctx_local = decode_slot_cache.shape[2]
    chosen = jnp.take(decode_slot_cache, slot_table, axis=1)
    positions = seq_index * ctx_local + jnp.arange(ctx_local)
    decode_live = (positions[None, :] < cache_lengths[:, None])[:, None, None, :]
    decode_token_rows = decode_query_rows.reshape(
        decode_count, kv_local, query_group_width, HEAD_SIZE
    )
    cache_keys = chosen[0].reshape(decode_count, ctx_local, kv_local, HEAD_SIZE)
    cache_values = chosen[1].reshape(decode_count, ctx_local, kv_local, HEAD_SIZE)
    decode_scores = (
        jnp.einsum(
            "bkgh,bskh->bkgs", decode_token_rows, cache_keys, preferred_element_type=jnp.float32
        )
        * score_scale
    )
    decode_masked = jnp.where(decode_live, decode_scores, neg_large)
    decode_max = jnp.max(decode_masked, axis=-1)
    decode_weights = jnp.where(decode_live, jnp.exp(decode_masked - decode_max[..., None]), 0.0)
    decode_sum = jnp.sum(decode_weights, axis=-1)
    decode_mixed = jnp.einsum(
        "bkgs,bskh->bkgh", decode_weights, cache_values.astype(jnp.float32), precision=exact
    )
    best = lax.pmax(decode_max, "seq")
    factors = jnp.exp(decode_max - best)
    totals, mixtures = lax.psum((decode_sum * factors, decode_mixed * factors[..., None]), "seq")
    combined = (best, totals, mixtures)
    own_keys = decode_kv[0].reshape(decode_count, kv_local, HEAD_SIZE)
    own_values = decode_kv[1].reshape(decode_count, kv_local, HEAD_SIZE).astype(jnp.float32)
    own_scores = (
        jnp.einsum("bkgh,bkh->bkg", decode_token_rows, own_keys, preferred_element_type=jnp.float32)
        * score_scale
    )
    own_mixed = jnp.broadcast_to(own_values[:, :, None, :], combined[2].shape)
    final_max, final_sum, final_mixed = join_parts(
        combined, (own_scores, jnp.ones_like(own_scores), own_mixed)
    )
    decode_attention = (
        (final_mixed / final_sum[..., None]).astype(jnp.bfloat16).reshape(decode_count, -1)
    )
    attention_all = jnp.concatenate([prefill_attention, decode_attention], 0)
    every_row = lax.all_gather(attention_all, "seq", axis=0, tiled=True)
    column_block = jnp.dot(every_row, out_weight, preferred_element_type=jnp.float32)
    partial_terms = lax.all_to_all(column_block, "seq", split_axis=0, concat_axis=1, tiled=True)
    summed = lax.psum_scatter(partial_terms, "tp", scatter_dimension=1, tiled=True)
    residual = jnp.concatenate([prefill_hidden, decode_hidden], 0).astype(jnp.float32)
    updated = (residual + summed).astype(jnp.bfloat16)
    prefill_out = updated[:span_len]
    decode_out = updated[span_len:]
    gathered = lax.all_gather(prefill_out[span_len - 1 :], ("seq", "tp"), axis=0, tiled=True)
    decode_full = lax.all_gather(decode_out, "tp", axis=1, tiled=True)
    n_seq = lax.axis_size("seq")
    n_tp = lax.axis_size("tp")
    feature_width = prefill_out.shape[1]
    prefill_full = gathered.reshape(n_seq, n_tp * feature_width)
    head_input = jnp.concatenate([decode_full, prefill_full], 0).astype(jnp.float32)
    mean_square = jnp.mean(head_input * head_input, axis=-1, keepdims=True)
    normed = (
        head_input * lax.rsqrt(mean_square + norm_eps) * final_gain.astype(jnp.float32)
    ).astype(jnp.bfloat16)
    logits = jnp.dot(normed, head_weight, preferred_element_type=jnp.float32)
    local_max = jnp.max(logits, axis=-1)
    local_sum = jnp.sum(jnp.exp(logits - local_max[:, None]), axis=-1)
    global_max, global_sum = merged((local_max, local_sum), ("seq", "tp"), join_totals)
    log_probs = logits - (global_max + jnp.log(global_sum))[:, None]
    return (prefill_out, decode_out, log_probs)


def solution(mesh):
    return jax.shard_map(
        local,
        mesh=mesh,
        in_specs=(
            P("seq", "tp"),
            P("seq", "tp"),
            P(None, "seq", "tp"),
            P(None, "seq", None, "tp"),
            P(),
            P(None, "tp"),
            P(None, "tp"),
            P(None, None, "tp"),
            P(None, None, "seq", "tp"),
            P(),
            P(),
            P("tp", "seq"),
            P(),
            P(None, ("seq", "tp")),
        ),
        out_specs=(P("seq", "tp"), P(None, "tp"), P(None, ("seq", "tp"))),
        check_vma=False,
    )
```

profile of v0, /device:TPU:0, one launch (start us, length us, event | category | flops | bytes accessed | tf_op | source)
XLA Modules:
  0.0 530.6 jit_solution(17046051987952885032)
XLA Ops:
  7.2 0.8 compare_select_fusion
  8.0 0.7 compare_and_fusion
  8.7 1.9 gather_fusion
  10.9 0.3 copy.61
  11.3 0.3 fusion.58
  11.7 44.0 %pmax.7 = f32[4,4,5]{2,1,0:T(4,128)S(1)} all-reduce(f32[4,4,5]{2,1,0:T(4,128)S(1)} %get-tuple-element.62), channel_id=1, replica_groups=mesh['seq'=16,'tp'=2] {'seq'}, use_global_device_ids=true, to_apply=%region_3.4 | all-reduce | flops 80 | bytes 640 | tf_op jit(solution)/shard_map/pmax | solution.py:122
  55.7 0.2 fusion.36
  55.9 0.3 copy.63
  56.4 1.0 convolution_multiply_fusion.1
  57.3 72.6 %all-reduce.3 = (f32[4,4,5,128]{3,2,1,0:T(8,128)S(1)}, f32[4,4,5]{2,1,0:T(4,128)S(1)}) all-reduce(f32[4,4,5,128]{3,2,1,0:T(8,128)S(1)} %convolution_multiply_fusion.1, f32[4,4,5]{2,1,0:T(4,128)S(1)} %bitcast.100), channel_id=1, replica_groups=mesh['seq'=16,'tp'=2] {'seq'}, use_global_device_ids=true, to_apply=%region_4.5 | all-reduce | flops 10320 | bytes 82560 | tf_op jit(solution)/shard_map/psum | solution.py:124
  130.1 0.6 dynamic_slice.10
  130.7 0.6 iota_compare_fusion.1
  131.3 2.4 fusion.55
  133.7 1.4 copy.77
  135.1 1.2 copy.56
  136.2 1.7 fusion.57
  138.0 1.0 copy.78
  139.0 0.8 copy.57
  139.8 2.2 copy.58
  142.0 1.2 copy.52
  143.1 0.8 copy.53
  143.9 1.4 fusion.31
  145.3 7.5 %fusion.59 = (f32[4,5,128]{2,1,0:T(8,128)S(1)}, bf16[4,5,128,896]{2,3,1,0:T(8,128)(2,1)}) fusion(pred[128,896]{0,1:T(8,128)(4,1)} %fusion.31, bf16[128,4,5,128]{0,3,2,1:T(8,128)(2,1)} %bitcast.92, bf16[128,4,128]{2,0,1:T(8,128)(2,1)S(1)} %copy-done.5, bf16[768,4,128]{2,0,1:T(8,128)(2,1)S(1)} %copy-done.2), kind=kOutput, calls=%fused_computation.82 | convolution fusion | flops 602801024 | bytes 6285312 | tf_op jit(solution)/shard_map/sub | solution.py:88
  152.7 4.1 fusion.18
  156.9 1.3 copy.65
  158.2 0.9 maximum_bitcast_fusion.3
  159.1 0.2 reduce-scatter.2.cloned.1.call-start
  159.3 135.4 %all-gather.6.cloned.1.call-done = bf16[16,132,2560]{2,1,0:T(8,128)(2,1)} async-done(((bf16[1,132,2560]{2,1,0:T(8,128)(2,1)}), bf16[16,132,2560]{2,1,0:T(8,128)(2,1)}) %all-gather.6.cloned.1.call-update) | async-done | bytes 10813456 | tf_op jit(solution)/shard_map/all_gather | solution.py:140
  294.8 11.0 %reshape.134 = bf16[2112,2560]{1,0:T(8,128)(2,1)} reshape(bf16[16,132,2560]{2,1,0:T(8,128)(2,1)} %all-gather.6.cloned.1.call-done) | data formatting | bytes 21626880
  305.8 10.3 %fusion.62 = f32[2112,320]{1,0:T(8,128)} fusion(bf16[2112,2560]{1,0:T(8,128)(2,1)} %reshape.134, bf16[2560,320]{0,1:T(8,128)(2,1)S(1)} %copy-done), kind=kOutput, calls=%fused_computation.85 | convolution fusion | flops 3460300800 | bytes 15155200 | tf_op jit(solution)/shard_map/dot_general | solution.py:141
  316.1 4.2 all_to_all.14
  320.3 80.0 %all_to_all.19 = f32[16,132,320]{2,1,0:T(8,128)S(1)} all-to-all(f32[16,132,320]{2,1,0:T(8,128)} %all_to_all.14), channel_id=1, replica_groups=mesh['seq'=16,'tp'=2] {'seq'}, dimensions={0} | all-to-all | bytes 5406720 | tf_op jit(solution)/shard_map/all_to_all | solution.py:142
  400.3 2.3 copy.67
  402.5 4.8 all_to_all.17
  407.4 8.2 %reduce-scatter.2.cloned.1.call-done = f32[132,2560]{1,0:T(8,128)} async-done(((f32[132,5120]{1,0:T(8,128)}), f32[132,2560]{1,0:T(8,128)}) %reduce-scatter.2.cloned.1.call-update) | async-done | bytes 1351696 | tf_op jit(solution)/shard_map/reduce_scatter | solution.py:143
  415.6 1.5 add_convert_fusion
  417.1 42.7 %all-gather.3 = bf16[32,1,2560]{2,1,0:T(2,128)(2,1)S(1)} all-gather(bf16[1,1,2560]{2,1,0:T(2,128)(2,1)S(1)} %slice_bitcast_fusion), channel_id=1, replica_groups=mesh['seq'=16,'tp'=2] {'seq','tp'}, dimensions={0}, use_global_device_ids=true | all-gather | bytes 168960 | tf_op jit(solution)/shard_map/all_gather | solution.py:148
  459.8 0.9 reduce
  460.9 1.8 all_gather.22
  462.7 0.2 fusion.28
  462.9 19.8 %fusion.60 = (f32[20]{0:T(128)S(1)}, f32[20,4752]{1,0:T(8,128)S(1)}) fusion(bf16[5120,4752]{0,1:T(8,128)(2,1)} %param.29, f32[5120]{0:T(1024)S(1)} %convert_element_type.43, f32[20]{0:T(128)S(1)} %add_rsqrt_fusion, bf16[16,5120]{1,0:T(8,128)(2,1)S(1)} %reshape.110, bf16[4,5120]{1,0:T(4,128)(2,1)S(1)} %all_gather.22), kind=kOutput, calls=%fused_computation.83 | convolution fusion | flops 974021440 | bytes 49266080 | tf_op jit(solution)/shard_map/dot_general | solution.py:159
  482.7 0.3 exponential_reduce_fusion
  483.0 0.2 dynamic-update-slice
  483.2 0.2 dynamic-update-slice.1
  483.5 36.9 %all-reduce.2 = (f32[640]{0:T(1024)S(1)}, f32[640]{0:T(1024)S(1)}) all-reduce(f32[640]{0:T(1024)S(1)} %dynamic-update-slice, f32[640]{0:T(1024)S(1)} %dynamic-update-slice.1), channel_id=2, replica_groups=mesh['seq'=16,'tp'=2] {'seq','tp'}, use_global_device_ids=true, to_apply=%add | all-reduce | flops 1280 | bytes 10240
  520.5 0.9 slice.69
  521.6 1.3 while.12
  522.9 0.9 broadcast_subtract_fusion
  (91 shorter events, 2.2 us)
Async XLA Ops:
  7.2 298.6 %copy-start = (bf16[2560,320]{0,1:T(8,128)(2,1)S(1)}, bf16[2560,320]{0,1:T(8,128)(2,1)}, u32[]{:S(2)}) copy-start(bf16[2560,320]{0,1:T(8,128)(2,1)} %param.27) | copy-start | bytes 4915204
  7.2 287.6 %all-gather.6.cloned.1.call-start = ((), (), s32[]{:S(2)}) async-start(), calls=%async_computation.3 | async-start | bytes 11837440 | tf_op jit(solution)/shard_map/all_gather | solution.py:140
  8.7 2.5 copy-start.9
  8.7 2.6 copy-start.12
  10.7 45.5 %copy-start.11 = (bf16[2,4,512]{2,1,0:T(4,128)(2,1)S(1)}, bf16[2,4,512]{2,1,0:T(4,128)(2,1)}, u32[]{:S(2)}) copy-start(bf16[2,4,512]{2,1,0:T(4,128)(2,1)} %param.23) | copy-start | bytes 24580
  10.8 119.2 %copy-start.13 = (s32[16]{0:T(128)S(1)}, s32[16]{0:T(128)}, u32[]{:S(2)}) copy-start(s32[16]{0:T(128)} %param.20) | copy-start | bytes 196
  136.2 9.0 %copy-start.2 = (bf16[768,4,128]{2,0,1:T(8,128)(2,1)S(1)}, bf16[768,4,128]{2,0,1:T(8,128)(2,1)}, u32[]{:S(2)}) copy-start(bf16[768,4,128]{2,0,1:T(8,128)(2,1)} %copy.56) | copy-start | bytes 2359300
  139.8 5.5 %copy-start.5 = (bf16[128,4,128]{2,0,1:T(8,128)(2,1)S(1)}, bf16[128,4,128]{2,0,1:T(8,128)(2,1)}, u32[]{:S(2)}) copy-start(bf16[128,4,128]{2,0,1:T(8,128)(2,1)} %copy.57) | copy-start | bytes 393220
  145.3 7.5 %copy-start.3 = (bf16[1,1,768,512]{2,3,1,0:T(8,128)(2,1)S(1)}, bf16[1,1,768,512]{2,3,1,0:T(8,128)(2,1)}, u32[]{:S(2)}) copy-start(bf16[1,1,768,512]{2,3,1,0:T(8,128)(2,1)} %copy.52) | copy-start | bytes 2359300
  145.3 7.5 %copy-start.6 = (bf16[1,128,512]{1,2,0:T(8,128)(2,1)S(1)}, bf16[1,128,512]{1,2,0:T(8,128)(2,1)}, u32[]{:S(2)}) copy-start(bf16[1,128,512]{1,2,0:T(8,128)(2,1)} %copy.53) | copy-start | bytes 393220
  159.1 256.5 %reduce-scatter.2.cloned.1.call-start = ((), (), s32[]{:S(2)}) async-start(), calls=%async_computation.2 | async-start | bytes 4177920 | tf_op jit(solution)/shard_map/reduce_scatter | solution.py:143
  402.5 4.8 copy-start.10
  402.5 13.1 %copy-start.4 = (bf16[128,2560]{1,0:T(8,128)(2,1)S(1)}, bf16[128,2560]{1,0:T(8,128)(2,1)}, u32[]{:S(2)}) copy-start(bf16[128,2560]{1,0:T(8,128)(2,1)} %param.16) | copy-start | bytes 1966084
  402.5 13.1 %copy-start.8 = (bf16[4,2560]{1,0:T(4,128)(2,1)S(1)}, bf16[4,2560]{1,0:T(4,128)(2,1)}, u32[]{:S(2)}) copy-start(bf16[4,2560]{1,0:T(4,128)(2,1)} %param.21) | copy-start | bytes 61444
  417.1 65.6 %copy-start.7 = (bf16[4,2560]{1,0:T(4,128)(2,1)}, bf16[4,2560]{1,0:T(4,128)(2,1)S(1)}, u32[]{:S(2)}) copy-start(bf16[4,2560]{1,0:T(4,128)(2,1)S(1)} %slice.70) | copy-start | bytes 61444
  462.9 60.9 %copy-start.1 = (bf16[2560,320]{0,1:T(8,128)(2,1)S(1)}, bf16[2560,320]{0,1:T(8,128)(2,1)}, u32[]{:S(2)}) copy-start(bf16[2560,320]{0,1:T(8,128)(2,1)} %param.27) | copy-start | bytes 4915204
Sparse Core Ops, SparseCore 0:
  159.2 135.4 all-gather.5
  407.5 8.1 reduce-scatter.1
where the time goes:
time: 532 us; the launch traced here: 531 us
  blocking collectives  278 us (52%)
  waiting for transfers between devices  144 us (27%)
  matrix products  43.1 us (8%)
  local copies, waits for them, and re-layouts  41.2 us (8%)
  between operations  14.4 us (3%)
  other arithmetic  9.66 us (2%)
    all_gather x1, waiting for transfers between devices, local(): every_row = lax.all_gather(attention_all, 'seq', axis=0, tiled=True)  135 us
    all_to_all x1, blocking collectives, local(): lax.all_to_all(column_block, 'seq', split_axis=0, concat_axis=1, tiled=True)  80 us
    psum x1, blocking collectives, local(): lax.psum((decode_sum * factors, decode_mixed * factors[..., None]), 'seq')  72.6 us
    pmax x1, blocking collectives, local(): best = lax.pmax(decode_max, 'seq')  44 us
    all_gather x1, blocking collectives, local(): lax.all_gather(prefill_out[span_len - 1:], ('seq', 'tp'), axis=0, tiled=T...  42.7 us
    unnamed x1, blocking collectives  36.9 us
    dot_general x1, matrix products, local(): logits = jnp.dot(normed, head_weight, preferred_element_type=jnp.float32)  19.8 us
    unnamed x37, local copies, waits for them, and re-layouts  16.2 us
  transfers between devices with their start and end apart: 2, of which 2 were waited for; matrix products, arithmetic and copies ran while one was open for 0% of the time, Pallas kernels for 0%

commit v1 on v0

v1 whole, which is shorter than its diff:
```python
import math

import jax
import jax.numpy as jnp
from jax import lax
from jax.sharding import PartitionSpec as P

QUERY_HEADS = 40
KEY_HEADS = 8
HEAD_SIZE = 128


neg_large = -1e30
exact = lax.Precision.HIGHEST
norm_eps = 1e-06


def local(
    prefill_hidden,
    prefill_query_rows,
    prefill_key_value,
    request_prefix_cache,
    prefix_lengths,
    decode_hidden,
    decode_query_rows,
    decode_kv,
    decode_slot_cache,
    cache_lengths,
    slot_table,
    out_weight,
    final_gain,
    head_weight,
):
    query_group_width = QUERY_HEADS // KEY_HEADS
    score_scale = 1.0 / math.sqrt(HEAD_SIZE)
    kv_local = prefill_key_value.shape[2] // HEAD_SIZE
    seq_index = lax.axis_index("seq")
    tp_index = lax.axis_index("tp")
    n_seq = lax.axis_size("seq")
    n_tp = lax.axis_size("tp")
    span_len = prefill_query_rows.shape[0]
    prefix_len = request_prefix_cache.shape[2]
    feature_width = prefill_hidden.shape[1]
    model_width = feature_width * n_tp
    column_width = out_weight.shape[1]
    decode_count = decode_query_rows.shape[0]

    ctx_local = decode_slot_cache.shape[2]
    chosen = jnp.take(decode_slot_cache, slot_table, axis=1)
    positions = seq_index * ctx_local + jnp.arange(ctx_local)
    decode_live = (positions[None, :] < cache_lengths[:, None])[:, None, None, :]
    decode_token_rows = decode_query_rows.reshape(
        decode_count, kv_local, query_group_width, HEAD_SIZE
    )
    cache_keys = chosen[0].reshape(decode_count, ctx_local, kv_local, HEAD_SIZE)
    cache_values = chosen[1].reshape(decode_count, ctx_local, kv_local, HEAD_SIZE)
    decode_scores = (
        jnp.einsum(
            "bkgh,bskh->bkgs", decode_token_rows, cache_keys, preferred_element_type=jnp.float32
        )
        * score_scale
    )
    decode_masked = jnp.where(decode_live, decode_scores, neg_large)
    decode_max = jnp.max(decode_masked, axis=-1)
    decode_weights = jnp.where(decode_live, jnp.exp(decode_masked - decode_max[..., None]), 0.0)
    decode_sum = jnp.sum(decode_weights, axis=-1)
    decode_mixed = jnp.einsum(
        "bkgs,bskh->bkgh", decode_weights, cache_values.astype(jnp.float32), precision=exact
    )
    packed = jnp.concatenate([decode_max[..., None], decode_sum[..., None], decode_mixed], -1)
    every_part = lax.all_gather(packed, "seq", axis=0)

    prefix_end = lax.dynamic_slice_in_dim(prefix_lengths, seq_index, 1)[0]
    query_matrix = prefill_query_rows.reshape(span_len, kv_local, query_group_width, HEAD_SIZE)
    joined_keys = jnp.concatenate([request_prefix_cache[0, 0], prefill_key_value[0]], 0).reshape(
        prefix_len + span_len, kv_local, HEAD_SIZE
    )
    value_matrix = jnp.concatenate([request_prefix_cache[1, 0], prefill_key_value[1]], 0).reshape(
        prefix_len + span_len, kv_local, HEAD_SIZE
    )
    key_place = jnp.arange(prefix_len + span_len)
    query_place = jnp.arange(span_len)
    live_mask = jnp.where(
        key_place[None, :] < prefix_len,
        key_place[None, :] < prefix_end,
        key_place[None, :] - prefix_len <= query_place[:, None],
    )
    scores = (
        jnp.einsum("rkgh,skh->kgrs", query_matrix, joined_keys, preferred_element_type=jnp.float32)
        * score_scale
    )
    masked = jnp.where(live_mask, scores, neg_large)
    row_max = jnp.max(masked, axis=-1, keepdims=True)
    weights = jnp.where(live_mask, jnp.exp(masked - row_max), 0.0)
    row_sum = jnp.sum(weights, axis=-1)
    weights_low = weights.astype(jnp.bfloat16)
    mixed = jnp.einsum(
        "kgrs,skh->rkgh", weights_low, value_matrix, preferred_element_type=jnp.float32
    )
    prefill_attention = (
        (mixed / jnp.transpose(row_sum, (2, 0, 1))[..., None])
        .astype(jnp.bfloat16)
        .reshape(span_len, -1)
    )
    every_row = lax.all_gather(prefill_attention, "seq", axis=0, tiled=True)

    part_max = every_part[..., 0]
    part_sum = every_part[..., 1]
    part_mixed = every_part[..., 2:]
    best = jnp.max(part_max, axis=0)
    factors = jnp.exp(part_max - best[None])
    totals = jnp.sum(part_sum * factors, axis=0)
    mixtures = jnp.sum(part_mixed * factors[..., None], axis=0)
    own_keys = decode_kv[0].reshape(decode_count, kv_local, HEAD_SIZE)
    own_values = decode_kv[1].reshape(decode_count, kv_local, HEAD_SIZE).astype(jnp.float32)
    own_scores = (
        jnp.einsum("bkgh,bkh->bkg", decode_token_rows, own_keys, preferred_element_type=jnp.float32)
        * score_scale
    )
    final_max = jnp.maximum(best, own_scores)
    factor_one = jnp.exp(best - final_max)
    factor_two = jnp.exp(own_scores - final_max)
    final_sum = totals * factor_one + factor_two
    final_mixed = mixtures * factor_one[..., None] + own_values[:, :, None, :] * factor_two[..., None]
    decode_attention = (
        (final_mixed / final_sum[..., None]).astype(jnp.bfloat16).reshape(decode_count, -1)
    )

    attention_all = jnp.concatenate([every_row, decode_attention], 0)
    column_block = jnp.dot(attention_all, out_weight, preferred_element_type=jnp.float32)
    prefill_block = column_block[: n_seq * span_len].reshape(n_seq, span_len, column_width)

    head_part = jnp.concatenate(
        [column_block[n_seq * span_len :], prefill_block[:, span_len - 1]], 0
    )
    hidden_piece = jnp.concatenate([prefill_hidden[span_len - 1 :], decode_hidden], 0)
    payload = jnp.concatenate(
        [head_part.reshape(-1), hidden_piece.astype(jnp.float32).reshape(-1)]
    )
    head_all = lax.all_gather(payload, ("seq", "tp"), axis=0).reshape(n_seq, n_tp, -1)
    head_rows_count = decode_count + n_seq
    head_partials = head_all[..., : head_rows_count * column_width].reshape(
        n_seq, n_tp, head_rows_count, column_width
    )
    head_projected = jnp.sum(head_partials, axis=1)
    head_projected = jnp.transpose(head_projected, (1, 0, 2)).reshape(head_rows_count, model_width)
    hidden_all = head_all[..., head_rows_count * column_width :].reshape(
        n_seq, n_tp, 1 + decode_count, feature_width
    )
    prefill_last = hidden_all[:, :, 0].reshape(n_seq, model_width)
    decode_full_hidden = jnp.transpose(hidden_all[0, :, 1:], (1, 0, 2)).reshape(
        decode_count, model_width
    )
    head_hidden = jnp.concatenate([decode_full_hidden, prefill_last], 0)
    head_updated = (head_hidden + head_projected).astype(jnp.bfloat16)
    decode_out = lax.dynamic_slice_in_dim(
        head_updated[:decode_count], tp_index * feature_width, feature_width, axis=1
    )

    rows_part = span_len // n_tp
    summed_rows = lax.psum_scatter(prefill_block, "tp", scatter_dimension=1, tiled=True)
    by_source = lax.all_to_all(summed_rows, "seq", split_axis=0, concat_axis=0, tiled=True)
    own_columns = lax.all_to_all(by_source, "tp", split_axis=0, concat_axis=1, tiled=True)
    projected = jnp.transpose(own_columns, (1, 0, 2)).reshape(span_len, feature_width)
    del rows_part
    prefill_out = (prefill_hidden.astype(jnp.float32) + projected).astype(jnp.bfloat16)

    head_input = head_updated.astype(jnp.float32)
    mean_square = jnp.mean(head_input * head_input, axis=-1, keepdims=True)
    normed = (
        head_input * lax.rsqrt(mean_square + norm_eps) * final_gain.astype(jnp.float32)
    ).astype(jnp.bfloat16)
    logits = jnp.dot(normed, head_weight, preferred_element_type=jnp.float32)
    local_max = jnp.max(logits, axis=-1)
    local_sum = jnp.sum(jnp.exp(logits - local_max[:, None]), axis=-1)
    stats = lax.all_gather(jnp.stack([local_max, local_sum], -1), ("seq", "tp"), axis=0)
    global_max = jnp.max(stats[..., 0], axis=0)
    global_sum = jnp.sum(stats[..., 1] * jnp.exp(stats[..., 0] - global_max[None]), axis=0)
    log_probs = logits - (global_max + jnp.log(global_sum))[:, None]
    return (prefill_out, decode_out, log_probs)


def solution(mesh):
    return jax.shard_map(
        local,
        mesh=mesh,
        in_specs=(
            P("seq", "tp"),
            P("seq", "tp"),
            P(None, "seq", "tp"),
            P(None, "seq", None, "tp"),
            P(),
            P(None, "tp"),
            P(None, "tp"),
            P(None, None, "tp"),
            P(None, None, "seq", "tp"),
            P(),
            P(),
            P("tp", "seq"),
            P(),
            P(None, ("seq", "tp")),
        ),
        out_specs=(P("seq", "tp"), P(None, "tp"), P(None, ("seq", "tp"))),
        check_vma=False,
    )
```

time: 532 us -> 401 us (0.75)
  blocking collectives: 278 us -> 108 us
  waiting for transfers between devices: 144 us -> 159 us
  local copies, waits for them, and re-layouts: 41.2 us -> 52.9 us
  other arithmetic: 9.66 us -> 19.6 us
    all_to_all x1, blocking collectives: 80 us -> 4.99 us  [local(): lax.all_to_all(by_source, 'tp', split_axis=0, concat_axis=1, tiled=True)]
    psum x1 -> x0, blocking collectives: 72.6 us -> none  [local(): lax.psum((decode_sum * factors, decode_mixed * factors[..., None]), 'seq')]
    all_gather x2, blocking collectives: 44.5 us -> 103 us  [the longest x1 61.5 us: local(): every_part = lax.all_gather(packed, 'seq', axis=0)]
    pmax x1 -> x0, blocking collectives: 44 us -> none  [local(): best = lax.pmax(decode_max, 'seq')]
    unnamed x1 -> x0, blocking collectives: 36.9 us -> none
    all_gather x1 -> x2, waiting for transfers between devices: 135 us -> 159 us  [the longest x1 110 us: local(): every_row = lax.all_gather(prefill_attention, 'seq', axis=0, tiled=True)]
    all_to_all x3 -> x1, local copies, waits for them, and re-layouts: 11.2 us -> 0.14 us  [local(): lax.all_to_all(by_source, 'tp', split_axis=0, concat_axis=1, tiled=True)]
    reduce_scatter x1, waiting for transfers between devices: 8.25 us -> 0.02 us  [local(): lax.psum_scatter(prefill_block, 'tp', scatter_dimension=1, tiled=True)]
  transfers between devices with their start and end apart: 2 -> 4, of which waited for: 2 -> 2; matrix products, arithmetic and copies ran while one was open for 0% -> 15% of each run, Pallas kernels for 0% -> 0%
where the time goes in v1:
time: 401 us; the launch traced here: 400 us
  waiting for transfers between devices  159 us (40%)
  blocking collectives  108 us (27%)
  local copies, waits for them, and re-layouts  52.9 us (13%)
  matrix products  40.4 us (10%)
  other arithmetic  19.6 us (5%)
  between operations  14.2 us (4%)
  starting transfers between devices  5.25 us (1%)
    all_gather x1, waiting for transfers between devices, local(): every_row = lax.all_gather(prefill_attention, 'seq', axis=0, tiled=True)  110 us
    all_gather x1, blocking collectives, local(): every_part = lax.all_gather(packed, 'seq', axis=0)  61.5 us
    all_gather x1, waiting for transfers between devices, local(): lax.all_gather(payload, ('seq', 'tp'), axis=0).reshape(n_seq, n_tp, -1)  49.6 us
    all_gather x1, blocking collectives, local(): lax.all_gather(jnp.stack([local_max, local_sum], -1), ('seq', 'tp'), axis=0)  41.9 us
    dot_general x1, matrix products, local(): logits = jnp.dot(normed, head_weight, preferred_element_type=jnp.float32)  19.8 us
    unnamed x41, local copies, waits for them, and re-layouts  17 us
    all_gather x1, other arithmetic, local(): lax.all_gather(payload, ('seq', 'tp'), axis=0).reshape(n_seq, n_tp, -1)  9.01 us
  transfers between devices with their start and end apart: 4, of which 2 were waited for; matrix products, arithmetic and copies ran while one was open for 15% of the time, Pallas kernels for 0%

profile of v1, /device:TPU:0, one launch (start us, length us, event | category | flops | bytes accessed | tf_op | source)
XLA Modules:
  0.0 400.2 jit_solution(18177792709383280548)
XLA Ops:
  7.2 1.4 dynamic_slice.6
  8.6 0.6 iota_compare_fusion.1
  9.3 2.4 fusion.59
  11.6 1.4 copy.332
  13.0 1.2 copy.284
  14.2 1.7 fusion.62
  15.9 1.0 copy.333
  16.9 0.8 copy.285
  17.7 2.2 copy.286
  19.9 1.2 copy.280
  21.0 0.8 copy.281
  21.8 1.4 fusion.31
  23.2 7.4 %fusion.65 = (f32[4,5,128]{2,1,0:T(8,128)S(1)}, bf16[4,5,128,896]{2,3,1,0:T(8,128)(2,1)}) fusion(pred[128,896]{0,1:T(8,128)(4,1)} %fusion.31, bf16[128,4,5,128]{0,3,2,1:T(8,128)(2,1)} %bitcast.138, bf16[128,4,128]{2,0,1:T(8,128)(2,1)S(1)} %copy-done.7, bf16[768,4,128]{2,0,1:T(8,128)(2,1)S(1)} %copy-done.4), kind=kOutput, calls=%fused_computation.101 | convolution fusion | flops 602801024 | bytes 6285312 | tf_op jit(solution)/shard_map/sub | solution.py:94
  30.6 4.2 %fusion.17 = bf16[128,4,5,128]{0,3,2,1:T(8,128)(2,1)} fusion(bf16[4,5,128,896]{2,3,1,0:T(8,128)(2,1)} %get-tuple-element.49, bf16[128,4,128]{0,2,1:T(8,128)(2,1)S(1)} %bitcast.143, bf16[768,4,128]{0,2,1:T(8,128)(2,1)S(1)} %bitcast.136, f32[128,4,5]{0,2,1:T(8,128)S(1)} %bitcast.150), kind=kOutput, calls=%fused_computation.17 | convolution fusion | flops 589692928 | bytes 6170624 | tf_op jit(solution)/shard_map/kgrs,skh->rkgh/dot_general | solution.py:97
  34.9 1.9 gather_fusion
  39.0 1.0 fusion.38
  40.1 61.5 %all-gather = f32[64,4,5,130]{3,1,2,0:T(4,128)S(1)} all-gather(f32[4,4,5,130]{3,1,2,0:T(4,128)S(1)} %copy.295), channel_id=2, replica_groups=mesh['seq'=16,'tp'=2] {'seq'}, dimensions={0}, use_global_device_ids=true | all-gather | bytes 707200 | tf_op jit(solution)/shard_map/all_gather | solution.py:71
  101.7 1.5 fusion.60
  103.2 1.6 copy.331
  104.8 1.6 copy.302
  107.7 0.8 fusion.27
  109.0 0.8 slice.81
  109.9 109.8 %all-gather.8.cloned.1.call-done = bf16[2048,2560]{0,1:T(8,128)(2,1)} async-done(((bf16[128,2560]{0,1:T(8,128)(2,1)}), bf16[2048,2560]{0,1:T(8,128)(2,1)}) %all-gather.8.cloned.1.call-update) | async-done | bytes 10485776 | tf_op jit(solution)/shard_map/all_gather | solution.py:105
  219.7 7.6 %fusion.1 = f32[2052,320]{0,1:T(8,128)S(1)} fusion(bf16[2560,320]{0,1:T(8,128)(2,1)S(1)} %copy-done, bf16[4,2560]{0,1:T(8,128)(2,1)S(1)} %bitcast.139, bf16[2048,2560]{0,1:T(8,128)(2,1)} %all-gather.8.cloned.1.call-done), kind=kOutput, calls=%fused_computation.2 | convolution fusion | flops 3383009280 | bytes 14771200 | tf_op jit(solution)/shard_map/dot_general | solution.py:130
  227.7 1.2 copy-done.3
  229.5 1.5 copy-done.2
  231.0 2.2 slice.98
  233.2 3.0 copy.334
  236.4 0.7 reshape.170
  237.4 3.5 copy.305
  240.9 1.1 copy-done.6
  241.9 1.1 copy.279
  243.0 49.6 %all-gather.10.cloned.1.call-done = f32[32,1,19200]{2,1,0:T(1,128)} async-done(((f32[1,1,19200]{2,1,0:T(1,128)}), f32[32,1,19200]{2,1,0:T(1,128)}) %all-gather.10.cloned.1.call-update) | async-done | bytes 2457616 | tf_op jit(solution)/shard_map/all_gather | solution.py:140
  292.6 9.0 %reduce.4 = f32[32,19200]{1,0:T(8,128)} reduce(f32[32,1,19200]{2,1,0:T(1,128)} %all-gather.10.cloned.1.call-done, f32[]{:T(128)} %constant.54), dimensions={1}, to_apply=%all-gather.3.reduce_sub_computation | reduce | bytes 4915204 | tf_op jit(solution)/shard_map/all_gather | solution.py:140
  301.6 3.8 reshape.151
  305.5 1.4 slice-done
  307.2 2.0 reshape.152
  309.2 2.0 slice.101
  311.8 0.9 slice_bitcast_fusion.1
  313.0 1.9 slice_reduce_fusion
  315.9 4.9 %all-to-all-start = ((f32[16,64,320]{2,1,0:T(8,128)}), f32[16,64,320]{2,1,0:T(8,128)S(1)}, u32[]{:S(2)}, u32[]{:S(2)}) async-start(f32[16,64,320]{2,1,0:T(8,128)} %reduce-scatter.2.cloned.1.call-done), calls=%async_computation.1 | async-start | bytes 3145728 | tf_op jit(solution)/shard_map/all_to_all | solution.py:162
  320.8 19.8 %fusion.66 = (f32[20]{0:T(128)S(1)}, f32[20,4752]{1,0:T(8,128)S(1)}) fusion(bf16[5120,4752]{0,1:T(8,128)(2,1)} %param.27, bf16[20,5120]{1,0:T(8,128)(2,1)S(1)} %fusion.30, f32[5120]{0:T(1024)S(1)} %convert_element_type.69, f32[20]{0:T(128)S(1)} %add_rsqrt_fusion), kind=kOutput, calls=%fused_computation.102 | convolution fusion | flops 973714240 | bytes 49266080 | tf_op jit(solution)/shard_map/dot_general | solution.py:173
  340.8 41.9 %all-gather.4 = f32[32,20,2]{1,2,0:T(2,128)S(1)} all-gather(f32[1,20,2]{1,2,0:T(2,128)S(1)} %maximum_bitcast_fusion.9), channel_id=4, replica_groups=mesh['seq'=16,'tp'=2] {'seq','tp'}, dimensions={0}, use_global_device_ids=true | all-gather | bytes 5280 | tf_op jit(solution)/shard_map/all_gather | solution.py:176
  383.5 0.9 broadcast_subtract_fusion
  384.3 5.0 %all_to_all.23 = f32[16,64,320]{2,1,0:T(8,128)S(1)} all-to-all(f32[16,64,320]{2,1,0:T(8,128)S(1)} %all-to-all-done), channel_id=1, replica_groups=mesh['seq'=16,'tp'=2] {'tp'}, dimensions={0} | all-to-all | bytes 2621440 | tf_op jit(solution)/shard_map/all_to_all | solution.py:163
  389.5 1.5 copy.307
  391.0 1.6 fusion.20
  392.6 1.1 copy.318
  (100 shorter events, 8.7 us)
Async XLA Ops:
  7.2 212.6 %copy-start = (bf16[2560,320]{0,1:T(8,128)(2,1)S(1)}, bf16[2560,320]{0,1:T(8,128)(2,1)}, u32[]{:S(2)}) copy-start(bf16[2560,320]{0,1:T(8,128)(2,1)} %param.25) | copy-start | bytes 4915204
  7.2 212.5 %all-gather.8.cloned.1.call-start = ((), (), s32[]{:S(2)}) async-start(), calls=%async_computation.3 | async-start | bytes 11141120 | tf_op jit(solution)/shard_map/all_gather | solution.py:105
  14.2 9.0 %copy-start.4 = (bf16[768,4,128]{2,0,1:T(8,128)(2,1)S(1)}, bf16[768,4,128]{2,0,1:T(8,128)(2,1)}, u32[]{:S(2)}) copy-start(bf16[768,4,128]{2,0,1:T(8,128)(2,1)} %copy.284) | copy-start | bytes 2359300
  17.7 5.5 %copy-start.7 = (bf16[128,4,128]{2,0,1:T(8,128)(2,1)S(1)}, bf16[128,4,128]{2,0,1:T(8,128)(2,1)}, u32[]{:S(2)}) copy-start(bf16[128,4,128]{2,0,1:T(8,128)(2,1)} %copy.285) | copy-start | bytes 393220
  23.2 7.5 %copy-start.5 = (bf16[1,1,768,512]{2,3,1,0:T(8,128)(2,1)S(1)}, bf16[1,1,768,512]{2,3,1,0:T(8,128)(2,1)}, u32[]{:S(2)}) copy-start(bf16[1,1,768,512]{2,3,1,0:T(8,128)(2,1)} %copy.280) | copy-start | bytes 2359300
  23.2 7.5 %copy-start.8 = (bf16[1,128,512]{1,2,0:T(8,128)(2,1)S(1)}, bf16[1,128,512]{1,2,0:T(8,128)(2,1)}, u32[]{:S(2)}) copy-start(bf16[1,128,512]{1,2,0:T(8,128)(2,1)} %copy.281) | copy-start | bytes 393220
  30.6 4.3 %copy-start.13 = (s32[4]{0:T(128)S(1)}, s32[4]{0:T(128)}, u32[]{:S(2)}) copy-start(s32[4]{0:T(128)} %param.24) | copy-start | bytes 52
  34.8 257.8 %all-gather.10.cloned.1.call-start = ((), (), s32[]{:S(2)}) async-start(), calls=%async_computation.5 | async-start | bytes 2534400 | tf_op jit(solution)/shard_map/all_gather | solution.py:140
  36.9 0.7 copy-start.10
  37.1 0.9 copy-start.14
  40.1 66.4 %copy-start.12 = (bf16[2,4,512]{2,1,0:T(4,128)(2,1)S(1)}, bf16[2,4,512]{2,1,0:T(4,128)(2,1)}, u32[]{:S(2)}) copy-start(bf16[2,4,512]{2,1,0:T(4,128)(2,1)} %param.21) | copy-start | bytes 24580
  103.2 6.6 %copy-start.9 = (bf16[4,2560]{1,0:T(4,128)(2,1)S(1)}, bf16[4,2560]{1,0:T(4,128)(2,1)}, u32[]{:S(2)}) copy-start(bf16[4,2560]{1,0:T(4,128)(2,1)} %param.19) | copy-start | bytes 61444
  227.4 1.6 copy-start.3
  229.4 1.5 copy-start.2
  233.2 3.0 slice-start.1
  237.1 78.7 %reduce-scatter.2.cloned.1.call-start = ((), (), s32[]{:S(2)}) async-start(), calls=%async_computation.4 | async-start | bytes 4718592 | tf_op jit(solution)/shard_map/reduce_scatter | solution.py:161
  240.9 1.1 copy-start.6
  240.9 2.2 copy-start.11
  305.5 1.4 slice-start
  315.9 68.5 %all-to-all-start = ((f32[16,64,320]{2,1,0:T(8,128)}), f32[16,64,320]{2,1,0:T(8,128)S(1)}, u32[]{:S(2)}, u32[]{:S(2)}) async-start(f32[16,64,320]{2,1,0:T(8,128)} %reduce-scatter.2.cloned.1.call-done), calls=%async_computation.1 | async-start | bytes 3145728 | tf_op jit(solution)/shard_map/all_to_all | solution.py:162
  389.5 4.2 %copy-start.1 = (bf16[2560,320]{0,1:T(8,128)(2,1)S(1)}, bf16[2560,320]{0,1:T(8,128)(2,1)}, u32[]{:S(2)}) copy-start(bf16[2560,320]{0,1:T(8,128)(2,1)} %param.25) | copy-start | bytes 4915204
Sparse Core Ops, SparseCore 0:
  35.0 184.7 all-gather.7
  237.2 55.3 all-gather.9
  294.9 9.8 reduce-scatter.1

commit v2 on v1

--- a/solution.py
+++ b/solution.py
@@ -61,15 +61,12 @@
         * score_scale
     )
     decode_masked = jnp.where(decode_live, decode_scores, neg_large)
-    decode_max = jnp.max(decode_masked, axis=-1)
+    decode_max = jnp.max(decode_masked, axis=-1).astype(jnp.bfloat16).astype(jnp.float32)
     decode_weights = jnp.where(decode_live, jnp.exp(decode_masked - decode_max[..., None]), 0.0)
     decode_sum = jnp.sum(decode_weights, axis=-1)
     decode_mixed = jnp.einsum(
         "bkgs,bskh->bkgh", decode_weights, cache_values.astype(jnp.float32), precision=exact
     )
-    packed = jnp.concatenate([decode_max[..., None], decode_sum[..., None], decode_mixed], -1)
-    every_part = lax.all_gather(packed, "seq", axis=0)
-
     prefix_end = lax.dynamic_slice_in_dim(prefix_lengths, seq_index, 1)[0]
     query_matrix = prefill_query_rows.reshape(span_len, kv_local, query_group_width, HEAD_SIZE)
     joined_keys = jnp.concatenate([request_prefix_cache[0, 0], prefill_key_value[0]], 0).reshape(
@@ -102,11 +99,45 @@
         .astype(jnp.bfloat16)
         .reshape(span_len, -1)
     )
-    every_row = lax.all_gather(prefill_attention, "seq", axis=0, tiled=True)
-
-    part_max = every_part[..., 0]
-    part_sum = every_part[..., 1]
-    part_mixed = every_part[..., 2:]
+    sum_high = decode_sum.astype(jnp.bfloat16)
+    sum_low = (decode_sum - sum_high.astype(jnp.float32)).astype(jnp.bfloat16)
+    mixed_high = decode_mixed.astype(jnp.bfloat16)
+    mixed_low = (decode_mixed - mixed_high.astype(jnp.float32)).astype(jnp.bfloat16)
+    stat_count = decode_sum.size
+    decode_flat = jnp.concatenate(
+        [
+            decode_max.astype(jnp.bfloat16).reshape(-1),
+            sum_high.reshape(-1),
+            sum_low.reshape(-1),
+            mixed_high.reshape(-1),
+            mixed_low.reshape(-1),
+        ]
+    )
+    extra_rows = -(-decode_flat.size // feature_width)
+    decode_flat = jnp.pad(decode_flat, (0, extra_rows * feature_width - decode_flat.size))
+    payload_rows = jnp.concatenate(
+        [
+            prefill_attention,
+            prefill_hidden[span_len - 1 :],
+            decode_flat.reshape(extra_rows, feature_width),
+        ],
+        0,
+    )
+    gathered = lax.all_gather(payload_rows, "seq", axis=0)
+    every_row = gathered[:, :span_len].reshape(n_seq * span_len, feature_width)
+    last_hidden = gathered[:, span_len].astype(jnp.float32)
+    every_flat = gathered[:, span_len + 1 :].reshape(n_seq, -1).astype(jnp.float32)
+    mixed_count = decode_mixed.size
+    part_max = every_flat[:, :stat_count].reshape((n_seq,) + decode_sum.shape)
+    part_sum = (
+        every_flat[:, stat_count : 2 * stat_count] + every_flat[:, 2 * stat_count : 3 * stat_count]
+    ).reshape((n_seq,) + decode_sum.shape)
+    mixed_at = 3 * stat_count
+    part_mixed = (
+        every_flat[:, mixed_at : mixed_at + mixed_count]
+        + every_flat[:, mixed_at + mixed_count : mixed_at + 2 * mixed_count]
+    ).reshape((n_seq,) + decode_mixed.shape)
+
     best = jnp.max(part_max, axis=0)
     factors = jnp.exp(part_max - best[None])
     totals = jnp.sum(part_sum * factors, axis=0)
@@ -130,29 +161,24 @@
     column_block = jnp.dot(attention_all, out_weight, preferred_element_type=jnp.float32)
     prefill_block = column_block[: n_seq * span_len].reshape(n_seq, span_len, column_width)
 
+    blocks_per_tp = n_seq // n_tp
+    owner_tp = seq_index // blocks_per_tp
+    column_start = (seq_index % blocks_per_tp) * column_width
+    decode_hidden_cols = lax.dynamic_slice_in_dim(
+        decode_hidden, column_start, column_width, axis=1
+    ).astype(jnp.float32)
+    last_hidden_cols = lax.dynamic_slice_in_dim(last_hidden, column_start, column_width, axis=1)
+    head_hidden_cols = jnp.concatenate([decode_hidden_cols, last_hidden_cols], 0)
     head_part = jnp.concatenate(
         [column_block[n_seq * span_len :], prefill_block[:, span_len - 1]], 0
     )
-    hidden_piece = jnp.concatenate([prefill_hidden[span_len - 1 :], decode_hidden], 0)
-    payload = jnp.concatenate(
-        [head_part.reshape(-1), hidden_piece.astype(jnp.float32).reshape(-1)]
-    )
-    head_all = lax.all_gather(payload, ("seq", "tp"), axis=0).reshape(n_seq, n_tp, -1)
+    head_part = jnp.where(owner_tp == tp_index, head_part + head_hidden_cols, head_part)
+    head_all = lax.all_gather(head_part, ("seq", "tp"), axis=0)
     head_rows_count = decode_count + n_seq
-    head_partials = head_all[..., : head_rows_count * column_width].reshape(
-        n_seq, n_tp, head_rows_count, column_width
-    )
-    head_projected = jnp.sum(head_partials, axis=1)
-    head_projected = jnp.transpose(head_projected, (1, 0, 2)).reshape(head_rows_count, model_width)
-    hidden_all = head_all[..., head_rows_count * column_width :].reshape(
-        n_seq, n_tp, 1 + decode_count, feature_width
-    )
-    prefill_last = hidden_all[:, :, 0].reshape(n_seq, model_width)
-    decode_full_hidden = jnp.transpose(hidden_all[0, :, 1:], (1, 0, 2)).reshape(
-        decode_count, model_width
-    )
-    head_hidden = jnp.concatenate([decode_full_hidden, prefill_last], 0)
-    head_updated = (head_hidden + head_projected).astype(jnp.bfloat16)
+    head_all = head_all.reshape(n_seq, n_tp, head_rows_count, column_width)
+    head_sum = jnp.sum(head_all, axis=1)
+    head_sum = jnp.transpose(head_sum, (1, 0, 2)).reshape(head_rows_count, model_width)
+    head_updated = head_sum.astype(jnp.bfloat16)
     decode_out = lax.dynamic_slice_in_dim(
         head_updated[:decode_count], tp_index * feature_width, feature_width, axis=1
     )

time: 401 us -> 358 us (0.89)
  blocking collectives: 108 us -> 88.8 us
  waiting for transfers between devices: 159 us -> 146 us
  other arithmetic: 19.6 us -> 11.7 us
    all_gather x1, blocking collectives: 61.5 us -> 42.1 us  [local(): head_all = lax.all_gather(head_part, ('seq', 'tp'), axis=0)]
    all_gather x2 -> x1, waiting for transfers between devices: 159 us -> 146 us  [local(): gathered = lax.all_gather(payload_rows, 'seq', axis=0)]
    all_gather x1 -> x0, other arithmetic: 9.01 us -> none  [local(): lax.all_gather(payload, ('seq', 'tp'), axis=0).reshape(n_seq, n_tp, -1)]
    reshape x4 -> x5, local copies, waits for them, and re-layouts: 6.07 us -> 0.38 us  [the longest x1 0.25 us: local(): prefill_attention = (mixed / jnp.transpose(row_sum, (2, 0, 1))[..., None]...]
    slice x9 -> x3, local copies, waits for them, and re-layouts: 5.7 us -> 10.1 us  [the longest x1 8.78 us: local(): every_row = gathered[:, :span_len].reshape(n_seq * span_len, feature_width)]
    unnamed x41 -> x31, local copies, waits for them, and re-layouts: 17 us -> 13.5 us
  transfers between devices with their start and end apart: 4 -> 3, of which waited for: 2 -> 1; matrix products, arithmetic and copies ran while one was open for 15% -> 10% of each run, Pallas kernels for 0% -> 0%
where the time goes in v2:
time: 358 us; the launch traced here: 357 us
  waiting for transfers between devices  146 us (41%)
  blocking collectives  88.8 us (25%)
  local copies, waits for them, and re-layouts  50.5 us (14%)
  matrix products  40.8 us (11%)
  between operations  14.5 us (4%)
  other arithmetic  11.7 us (3%)
  starting transfers between devices  4.2 us (1%)
    all_gather x1, waiting for transfers between devices, local(): gathered = lax.all_gather(payload_rows, 'seq', axis=0)  146 us
    all_gather x1, blocking collectives, local(): head_all = lax.all_gather(head_part, ('seq', 'tp'), axis=0)  42.1 us
    all_gather x1, blocking collectives, local(): lax.all_gather(jnp.stack([local_max, local_sum], -1), ('seq', 'tp'), axis=0)  41.7 us
    dot_general x1, matrix products, local(): logits = jnp.dot(normed, head_weight, preferred_element_type=jnp.float32)  19.8 us
    unnamed x31, local copies, waits for them, and re-layouts  13.5 us
    slice x1, local copies, waits for them, and re-layouts, local(): every_row = gathered[:, :span_len].reshape(n_seq * span_len, feature_width)  8.78 us
    dot_general x1, matrix products, local(): jnp.dot(attention_all, out_weight, preferred_element_type=jnp.float32)  8.67 us
    sub x1, matrix products, local(): weights = jnp.where(live_mask, jnp.exp(masked - row_max), 0.0)  7.59 us
  transfers between devices with their start and end apart: 3, of which 1 were waited for; matrix products, arithmetic and copies ran while one was open for 10% of the time, Pallas kernels for 0%

profile of v2, /device:TPU:0, one launch (start us, length us, event | category | flops | bytes accessed | tf_op | source)
XLA Modules:
  0.0 356.8 jit_solution(4179541137310845090)
XLA Ops:
  7.2 0.8 compare_select_fusion
  8.0 0.7 compare_and_fusion
  8.7 1.9 gather_fusion
  11.5 0.3 fusion.61
  12.5 1.0 subtract_convert_fusion
  13.8 0.8 slice.77
  14.6 0.6 dynamic_slice.12
  15.2 0.6 iota_compare_fusion.1
  15.8 1.1 copy.150
  16.9 1.0 fusion.59
  18.0 0.8 copy.149
  18.8 2.3 fusion.56
  21.2 1.4 copy.177
  22.6 1.2 copy.148
  23.7 0.8 copy.145
  24.8 0.8 fusion.30
  25.6 7.6 %fusion.62 = (f32[4,5,128]{2,1,0:T(8,128)S(1)}, bf16[4,5,128,896]{2,3,1,0:T(8,128)(2,1)}) fusion(pred[128,896]{0,1:T(8,128)(4,1)S(1)} %fusion.30, bf16[128,4,5,128]{0,3,2,1:T(8,128)(2,1)} %bitcast.120, bf16[128,4,128]{2,0,1:T(8,128)(2,1)} %copy.149, bf16[768,4,128]{2,0,1:T(8,128)(2,1)} %copy.148), kind=kOutput, calls=%fused_computation.101 | convolution fusion | flops 602801024 | bytes 6285312 | tf_op jit(solution)/shard_map/sub | solution.py:91
  33.2 3.3 fusion.17
  36.7 0.9 maximum_bitcast_fusion.3
  38.1 146.3 %all-gather.6.cloned.1.call-done = bf16[16,138,2560]{2,1,0:T(8,128)(2,1)} async-done(((bf16[1,138,2560]{2,1,0:T(8,128)(2,1)}), bf16[16,138,2560]{2,1,0:T(8,128)(2,1)}) %all-gather.6.cloned.1.call-update) | async-done | bytes 11304976 | tf_op jit(solution)/shard_map/all_gather | solution.py:126
  184.4 1.7 slice_convert_fusion
  186.1 0.9 copy.183
  187.9 1.3 mul.107
  189.2 2.3 mul.108
  191.5 1.5 fusion.28
  193.2 8.8 %slice.101 = bf16[16,128,2560]{2,1,0:T(8,128)(2,1)} slice(bf16[16,138,2560]{2,1,0:T(8,128)(2,1)} %all-gather.6.cloned.1.call-done), slice={[0:16], [0:128], [0:2560]} | slice | bytes 20971520 | tf_op jit(solution)/shard_map/slice | solution.py:127
  202.0 8.7 %fusion.1 = f32[2052,320]{0,1:T(8,128)S(1)} fusion(bf16[2560,320]{0,1:T(8,128)(2,1)S(1)} %copy-done, bf16[4,2560]{1,0:T(4,128)(2,1)S(1)} %fusion.37, bf16[2048,2560]{1,0:T(8,128)(2,1)} %bitcast.107), kind=kOutput, calls=%fused_computation.2 | convolution fusion | flops 3383009280 | bytes 14771200 | tf_op jit(solution)/shard_map/dot_general | solution.py:161
  210.7 0.3 slice_bitcast_fusion
  211.0 1.2 copy-done.2
  212.2 2.0 copy.184
  214.1 3.5 copy.160
  217.7 1.1 copy-done.3
  218.8 1.1 copy.143
  219.8 0.8 bitcast_convert_fusion
  220.6 4.4 %slice.110 = f32[16,1,320]{1,0,2:T(8,128)} slice(f32[16,128,320]{1,0,2:T(8,128)} %bitcast.106), slice={[0:16], [127:128], [0:320]} | slice | bytes 40960 | tf_op jit(solution)/shard_map/slice | solution.py:173
  225.0 3.1 copy.179
  228.1 0.9 slice_bitcast_fusion.1
  229.1 1.2 slice.111
  230.5 42.1 %all_gather.18 = f32[32,20,320]{2,1,0:T(8,128)S(1)} all-gather(f32[1,20,320]{2,1,0:T(8,128)S(1)} %add_select_fusion), channel_id=1, replica_groups=mesh['seq'=16,'tp'=2] {'seq','tp'}, dimensions={0}, use_global_device_ids=true | all-gather | bytes 844800 | tf_op jit(solution)/shard_map/all_gather | solution.py:176
  273.2 3.9 %all-to-all-start = ((f32[16,64,320]{2,1,0:T(8,128)}), f32[16,64,320]{2,1,0:T(8,128)S(1)}, u32[]{:S(2)}, u32[]{:S(2)}) async-start(f32[16,64,320]{2,1,0:T(8,128)} %reduce-scatter.2.cloned.1.call-done), calls=%async_computation.1 | async-start | bytes 3145728 | tf_op jit(solution)/shard_map/all_to_all | solution.py:188
  277.1 19.8 %fusion.63 = (f32[20]{0:T(128)S(1)}, f32[20,4752]{1,0:T(8,128)S(1)}) fusion(bf16[5120,4752]{0,1:T(8,128)(2,1)} %param.27, f32[20,5120]{1,0:T(8,128)S(1)} %reshape.269, f32[5120]{0:T(1024)S(1)} %convert_element_type.130, f32[20]{0:T(128)S(1)} %add_rsqrt_fusion), kind=kOutput, calls=%fused_computation.102 | convolution fusion | flops 973611840 | bytes 49470880 | tf_op jit(solution)/shard_map/dot_general | solution.py:199
  297.3 41.7 %all-gather.3 = f32[32,20,2]{1,2,0:T(2,128)S(1)} all-gather(f32[1,20,2]{1,2,0:T(2,128)S(1)} %maximum_bitcast_fusion.10), channel_id=3, replica_groups=mesh['seq'=16,'tp'=2] {'seq','tp'}, dimensions={0}, use_global_device_ids=true | all-gather | bytes 5280 | tf_op jit(solution)/shard_map/all_gather | solution.py:202
  339.1 0.6 constant_dynamic-slice_fusion
  339.7 0.9 broadcast_subtract_fusion
  340.6 5.0 %all_to_all.23 = f32[16,64,320]{2,1,0:T(8,128)S(1)} all-to-all(f32[16,64,320]{2,1,0:T(8,128)S(1)} %all-to-all-done), channel_id=1, replica_groups=mesh['seq'=16,'tp'=2] {'tp'}, dimensions={0} | all-to-all | bytes 2621440 | tf_op jit(solution)/shard_map/all_to_all | solution.py:189
  345.7 1.5 copy.162
  347.3 1.6 fusion.20
  348.9 1.1 copy.168
  (87 shorter events, 5.3 us)
Async XLA Ops:
  7.2 194.8 %copy-start = (bf16[2560,320]{0,1:T(8,128)(2,1)S(1)}, bf16[2560,320]{0,1:T(8,128)(2,1)}, u32[]{:S(2)}) copy-start(bf16[2560,320]{0,1:T(8,128)(2,1)} %param.25) | copy-start | bytes 4915204
  7.2 177.2 %all-gather.6.cloned.1.call-start = ((), (), s32[]{:S(2)}) async-start(), calls=%async_computation.4 | async-start | bytes 12533760 | tf_op jit(solution)/shard_map/all_gather | solution.py:126
  10.6 0.7 copy-start.6
  10.6 0.8 copy-start.9
  10.8 3.8 %copy-start.10 = (s32[16]{0:T(128)S(1)}, s32[16]{0:T(128)}, u32[]{:S(2)}) copy-start(s32[16]{0:T(128)} %param.18) | copy-start | bytes 196
  11.3 4.5 %copy-start.4 = (bf16[128,2560]{1,0:T(8,128)(2,1)S(1)}, bf16[128,2560]{1,0:T(8,128)(2,1)}, u32[]{:S(2)}) copy-start(bf16[128,2560]{1,0:T(8,128)(2,1)} %param.15) | copy-start | bytes 1966084
  25.6 7.6 %copy-start.5 = (bf16[1,128,512]{1,2,0:T(8,128)(2,1)S(1)}, bf16[1,128,512]{1,2,0:T(8,128)(2,1)}, u32[]{:S(2)}) copy-start(bf16[1,128,512]{1,2,0:T(8,128)(2,1)} %copy.145) | copy-start | bytes 393220
  36.5 1.4 copy-start.8
  37.7 235.5 %reduce-scatter.2.cloned.1.call-start = ((), (), s32[]{:S(2)}) async-start(), calls=%async_computation.3 | async-start | bytes 4718592 | tf_op jit(solution)/shard_map/reduce_scatter | solution.py:187
  210.7 1.5 copy-start.2
  217.7 1.1 copy-start.3
  217.7 2.2 copy-start.7
  273.2 67.4 %all-to-all-start = ((f32[16,64,320]{2,1,0:T(8,128)}), f32[16,64,320]{2,1,0:T(8,128)S(1)}, u32[]{:S(2)}, u32[]{:S(2)}) async-start(f32[16,64,320]{2,1,0:T(8,128)} %reduce-scatter.2.cloned.1.call-done), calls=%async_computation.1 | async-start | bytes 3145728 | tf_op jit(solution)/shard_map/all_to_all | solution.py:188
  345.7 4.2 %copy-start.1 = (bf16[2560,320]{0,1:T(8,128)(2,1)S(1)}, bf16[2560,320]{0,1:T(8,128)(2,1)}, u32[]{:S(2)}) copy-start(bf16[2560,320]{0,1:T(8,128)(2,1)} %param.25) | copy-start | bytes 4915204
Sparse Core Ops, SparseCore 0:
  37.8 146.5 all-gather.5
  217.8 9.2 reduce-scatter.1

commit v3 on v2

--- a/solution.py
+++ b/solution.py
@@ -115,18 +115,19 @@
     )
     extra_rows = -(-decode_flat.size // feature_width)
     decode_flat = jnp.pad(decode_flat, (0, extra_rows * feature_width - decode_flat.size))
-    payload_rows = jnp.concatenate(
+    small_rows = jnp.concatenate(
         [
-            prefill_attention,
+            prefill_attention[span_len - 1 :],
             prefill_hidden[span_len - 1 :],
             decode_flat.reshape(extra_rows, feature_width),
         ],
         0,
     )
-    gathered = lax.all_gather(payload_rows, "seq", axis=0)
-    every_row = gathered[:, :span_len].reshape(n_seq * span_len, feature_width)
-    last_hidden = gathered[:, span_len].astype(jnp.float32)
-    every_flat = gathered[:, span_len + 1 :].reshape(n_seq, -1).astype(jnp.float32)
+    small_gathered = lax.all_gather(small_rows, "seq", axis=0)
+    every_row = lax.all_gather(prefill_attention, "seq", axis=0).reshape(n_seq * span_len, feature_width)
+    last_attention = small_gathered[:, 0]
+    last_hidden = small_gathered[:, 1].astype(jnp.float32)
+    every_flat = small_gathered[:, 2:].reshape(n_seq, -1).astype(jnp.float32)
     mixed_count = decode_mixed.size
     part_max = every_flat[:, :stat_count].reshape((n_seq,) + decode_sum.shape)
     part_sum = (
@@ -157,10 +158,6 @@
         (final_mixed / final_sum[..., None]).astype(jnp.bfloat16).reshape(decode_count, -1)
     )
 
-    attention_all = jnp.concatenate([every_row, decode_attention], 0)
-    column_block = jnp.dot(attention_all, out_weight, preferred_element_type=jnp.float32)
-    prefill_block = column_block[: n_seq * span_len].reshape(n_seq, span_len, column_width)
-
     blocks_per_tp = n_seq // n_tp
     owner_tp = seq_index // blocks_per_tp
     column_start = (seq_index % blocks_per_tp) * column_width
@@ -169,9 +166,8 @@
     ).astype(jnp.float32)
     last_hidden_cols = lax.dynamic_slice_in_dim(last_hidden, column_start, column_width, axis=1)
     head_hidden_cols = jnp.concatenate([decode_hidden_cols, last_hidden_cols], 0)
-    head_part = jnp.concatenate(
-        [column_block[n_seq * span_len :], prefill_block[:, span_len - 1]], 0
-    )
+    head_attention = jnp.concatenate([decode_attention, last_attention], 0)
+    head_part = jnp.dot(head_attention, out_weight, preferred_element_type=jnp.float32)
     head_part = jnp.where(owner_tp == tp_index, head_part + head_hidden_cols, head_part)
     head_all = lax.all_gather(head_part, ("seq", "tp"), axis=0)
     head_rows_count = decode_count + n_seq
@@ -182,14 +178,6 @@
     decode_out = lax.dynamic_slice_in_dim(
         head_updated[:decode_count], tp_index * feature_width, feature_width, axis=1
     )
-
-    rows_part = span_len // n_tp
-    summed_rows = lax.psum_scatter(prefill_block, "tp", scatter_dimension=1, tiled=True)
-    by_source = lax.all_to_all(summed_rows, "seq", split_axis=0, concat_axis=0, tiled=True)
-    own_columns = lax.all_to_all(by_source, "tp", split_axis=0, concat_axis=1, tiled=True)
-    projected = jnp.transpose(own_columns, (1, 0, 2)).reshape(span_len, feature_width)
-    del rows_part
-    prefill_out = (prefill_hidden.astype(jnp.float32) + projected).astype(jnp.bfloat16)
 
     head_input = head_updated.astype(jnp.float32)
     mean_square = jnp.mean(head_input * head_input, axis=-1, keepdims=True)
@@ -203,6 +191,17 @@
     global_max = jnp.max(stats[..., 0], axis=0)
     global_sum = jnp.sum(stats[..., 1] * jnp.exp(stats[..., 0] - global_max[None]), axis=0)
     log_probs = logits - (global_max + jnp.log(global_sum))[:, None]
+    every_row, decode_out, log_probs = lax.optimization_barrier((every_row, decode_out, log_probs))
+
+    column_block = jnp.dot(every_row, out_weight, preferred_element_type=jnp.float32)
+    prefill_block = column_block.reshape(n_seq, span_len, column_width)
+
+    summed_rows = lax.psum_scatter(prefill_block, "tp", scatter_dimension=1, tiled=True)
+    by_source = lax.all_to_all(summed_rows, "seq", split_axis=0, concat_axis=0, tiled=True)
+    own_columns = lax.all_to_all(by_source, "tp", split_axis=0, concat_axis=1, tiled=True)
+    projected = jnp.transpose(own_columns, (1, 0, 2)).reshape(span_len, feature_width)
+    prefill_out = (prefill_hidden.astype(jnp.float32) + projected).astype(jnp.bfloat16)
+
     return (prefill_out, decode_out, log_probs)
 
 

time: 358 us -> 303 us (0.85)
  waiting for transfers between devices: 146 us -> 39.4 us
  blocking collectives: 88.8 us -> 155 us
  local copies, waits for them, and re-layouts: 50.5 us -> 31.5 us
    all_gather x1, waiting for transfers between devices: 146 us -> 0.01 us  [local(): lax.all_gather(prefill_attention, 'seq', axis=0)]
    all_gather x0 -> x1, blocking collectives: none -> 64 us  [local(): small_gathered = lax.all_gather(small_rows, 'seq', axis=0)]
    all_to_all x1, waiting for transfers between devices: 0.01 us -> 32.1 us  [local(): lax.all_to_all(summed_rows, 'seq', split_axis=0, concat_axis=0, tiled=True)]
    slice x3, local copies, waits for them, and re-layouts: 14.4 us -> 0.73 us  [the longest x2 0.51 us: local(): prefill_attention[span_len - 1:]]
    reshape x0 -> x1, matrix products: none -> 10.1 us  [local(): prefill_block = column_block.reshape(n_seq, span_len, column_width)]
    dot_general x1, matrix products: 8.67 us -> 0.55 us  [local(): jnp.dot(head_attention, out_weight, preferred_element_type=jnp.float32)]
    reduce_scatter x1, waiting for transfers between devices: 0.01 us -> 7.3 us  [local(): lax.psum_scatter(prefill_block, 'tp', scatter_dimension=1, tiled=True)]
    all_gather x1, blocking collectives: 42.1 us -> 47.5 us  [local(): head_all = lax.all_gather(head_part, ('seq', 'tp'), axis=0)]
  transfers between devices with their start and end apart: 3 -> 3, of which waited for: 1 -> 2; matrix products, arithmetic and copies ran while one was open for 10% -> 14% of each run, Pallas kernels for 0% -> 0%
where the time goes in v3:
time: 303 us; the launch traced here: 300 us
  blocking collectives  155 us (51%)
  matrix products  42.6 us (14%)
  waiting for transfers between devices  39.4 us (13%)
  local copies, waits for them, and re-layouts  31.5 us (10%)
  between operations  14.6 us (5%)
  other arithmetic  9.42 us (3%)
  starting transfers between devices  6.98 us (2%)
    all_gather x1, blocking collectives, local(): small_gathered = lax.all_gather(small_rows, 'seq', axis=0)  64 us
    all_gather x1, blocking collectives, local(): head_all = lax.all_gather(head_part, ('seq', 'tp'), axis=0)  47.5 us
    all_gather x1, blocking collectives, local(): lax.all_gather(jnp.stack([local_max, local_sum], -1), ('seq', 'tp'), axis=0)  39 us
    all_to_all x1, waiting for transfers between devices, local(): lax.all_to_all(summed_rows, 'seq', split_axis=0, concat_axis=0, tiled=True)  32.1 us
    dot_general x1, matrix products, local(): logits = jnp.dot(normed, head_weight, preferred_element_type=jnp.float32)  19.8 us
    reshape x1, matrix products, local(): prefill_block = column_block.reshape(n_seq, span_len, column_width)  10.1 us
    unnamed x26, local copies, waits for them, and re-layouts  9.01 us
    reduce_scatter x1, waiting for transfers between devices, local(): lax.psum_scatter(prefill_block, 'tp', scatter_dimension=1, tiled=True)  7.3 us
  transfers between devices with their start and end apart: 3, of which 2 were waited for; matrix products, arithmetic and copies ran while one was open for 14% of the time, Pallas kernels for 0%

profile of v3, /device:TPU:0, one launch (start us, length us, event | category | flops | bytes accessed | tf_op | source)
XLA Modules:
  0.0 299.8 jit_solution(17854747300477261836)
XLA Ops:
  7.2 1.4 dynamic_slice.14
  8.6 0.6 iota_compare_fusion.1
  9.3 2.4 fusion.61
  11.6 1.4 copy.165
  13.0 1.2 copy.136
  14.2 1.0 fusion.65
  15.3 0.8 copy.137
  16.1 2.2 copy.138
  18.3 1.2 copy.132
  19.5 0.8 fusion.26
  20.4 7.2 %fusion.68 = (f32[4,5,128]{2,1,0:T(8,128)S(1)}, bf16[4,5,128,896]{2,3,1,0:T(8,128)(2,1)}) fusion(pred[128,896]{0,1:T(8,128)(4,1)S(1)} %fusion.26, bf16[128,4,5,128]{0,3,2,1:T(8,128)(2,1)} %bitcast.117, bf16[128,4,128]{2,0,1:T(8,128)(2,1)S(1)} %copy-done.3, bf16[768,4,128]{2,0,1:T(8,128)(2,1)S(1)} %copy-done.2), kind=kOutput, calls=%fused_computation.103 | convolution fusion | flops 602801024 | bytes 6285312 | tf_op jit(solution)/shard_map/sub | solution.py:91
  27.6 3.5 %fusion.13 = bf16[128,4,5,128]{0,3,2,1:T(8,128)(2,1)S(1)} fusion(bf16[4,5,128,896]{2,3,1,0:T(8,128)(2,1)} %get-tuple-element.52, bf16[128,4,128]{0,2,1:T(8,128)(2,1)S(1)} %bitcast.120, bf16[768,4,128]{0,2,1:T(8,128)(2,1)} %bitcast.116, f32[128,4,5]{0,2,1:T(8,128)S(1)} %bitcast.128), kind=kOutput, calls=%fused_computation.12 | convolution fusion | flops 589692928 | bytes 6170624 | tf_op jit(solution)/shard_map/kgrs,skh->rkgh/dot_general | solution.py:94
  31.1 1.1 copy.141
  32.3 1.9 gather_fusion
  34.5 0.9 fusion.64
  35.4 1.3 copy.142
  36.9 0.3 fusion.67
  37.3 0.3 copy.144
  37.6 1.0 subtract_convert_fusion
  39.2 0.5 slice_reduce_fusion
  39.7 0.8 slice.76
  40.5 64.0 %all-gather.3 = bf16[16,11,2560]{2,1,0:T(8,128)(2,1)S(1)} all-gather(bf16[1,11,2560]{2,1,0:T(8,128)(2,1)S(1)} %maximum_bitcast_fusion.9), channel_id=2, replica_groups=mesh['seq'=16,'tp'=2] {'seq'}, dimensions={0}, use_global_device_ids=true | all-gather | bytes 957440 | tf_op jit(solution)/shard_map/all_gather | solution.py:126
  104.5 0.4 slice_convert_fusion
  104.9 0.9 copy.169
  105.7 1.1 copy-done.1
  107.4 1.3 mul.107
  108.7 2.3 mul.108
  111.0 1.9 fusion.24
  113.0 0.9 fusion.49
  114.5 0.2 fusion.63
  114.9 0.8 dynamic-slice_convert_fusion.1
  115.7 0.6 fusion.36
  116.3 47.5 %all-gather.4 = f32[32,20,320]{2,1,0:T(8,128)S(1)} all-gather(f32[1,20,320]{2,1,0:T(8,128)S(1)} %fusion.36), channel_id=3, replica_groups=mesh['seq'=16,'tp'=2] {'seq','tp'}, dimensions={0}, use_global_device_ids=true | all-gather | bytes 844800 | tf_op jit(solution)/shard_map/all_gather | solution.py:172
  164.2 0.2 multiply_reduce_fusion
  164.5 19.8 %fusion.69 = (f32[20]{0:T(128)S(1)}, f32[20,4752]{1,0:T(8,128)S(1)}) fusion(bf16[5120,4752]{0,1:T(8,128)(2,1)} %param.27, f32[20,5120]{1,0:T(8,128)S(1)} %reshape.181, f32[5120]{0:T(1024)S(1)} %convert_element_type.132, f32[20]{0:T(128)S(1)} %add_rsqrt_fusion), kind=kOutput, calls=%fused_computation.104 | convolution fusion | flops 973611840 | bytes 49470880 | tf_op jit(solution)/shard_map/dot_general | solution.py:187
  184.3 0.3 exponential_reduce_fusion
  184.5 39.0 %all-gather.5 = f32[32,20,2]{1,2,0:T(2,128)S(1)} all-gather(f32[1,20,2]{1,2,0:T(2,128)S(1)} %maximum_bitcast_fusion.10), channel_id=4, replica_groups=mesh['seq'=16,'tp'=2] {'seq','tp'}, dimensions={0}, use_global_device_ids=true | all-gather | bytes 5280 | tf_op jit(solution)/shard_map/all_gather | solution.py:190
  223.6 0.6 constant_dynamic-slice_fusion
  224.2 0.9 broadcast_subtract_fusion
  225.1 10.1 %fusion.71 = f32[2048,320]{1,0:T(8,128)} fusion(bf16[2048,2560]{1,0:T(8,128)(2,1)} %bitcast.127, bf16[2560,320]{0,1:T(8,128)(2,1)S(1)} %copy-done), kind=kOutput, calls=%fused_computation.106 | convolution fusion | flops 3355443200 | bytes 14745600 | tf_op jit(solution)/shard_map/reshape | solution.py:197
  235.2 7.3 %reduce-scatter.2.cloned.1.call-done = f32[16,64,320]{2,1,0:T(8,128)} async-done(((f32[16,128,320]{2,1,0:T(8,128)}), f32[16,64,320]{2,1,0:T(8,128)}) %reduce-scatter.2.cloned.1.call-update) | async-done | bytes 1310736 | tf_op jit(solution)/shard_map/reduce_scatter | solution.py:199
  242.5 6.9 %all-to-all-start = ((f32[16,64,320]{2,1,0:T(8,128)}), f32[16,64,320]{2,1,0:T(8,128)S(1)}, u32[]{:S(2)}, u32[]{:S(2)}) async-start(f32[16,64,320]{2,1,0:T(8,128)} %reduce-scatter.2.cloned.1.call-done), calls=%async_computation.1 | async-start | bytes 3145728 | tf_op jit(solution)/shard_map/all_to_all | solution.py:200
  249.4 2.2 copy.131
  251.6 32.1 %all-to-all-done = f32[16,64,320]{2,1,0:T(8,128)S(1)} async-done(((f32[16,64,320]{2,1,0:T(8,128)}), f32[16,64,320]{2,1,0:T(8,128)S(1)}, u32[]{:S(2)}, u32[]{:S(2)}) %all-to-all-start) | async-done | bytes 1310752 | tf_op jit(solution)/shard_map/all_to_all | solution.py:200
  283.6 5.0 %all_to_all.23 = f32[16,64,320]{2,1,0:T(8,128)S(1)} all-to-all(f32[16,64,320]{2,1,0:T(8,128)S(1)} %all-to-all-done), channel_id=1, replica_groups=mesh['seq'=16,'tp'=2] {'tp'}, dimensions={0} | all-to-all | bytes 2621440 | tf_op jit(solution)/shard_map/all_to_all | solution.py:201
  288.8 1.5 copy.153
  290.3 1.6 fusion.16
  291.9 1.1 copy.154
  (79 shorter events, 3.4 us)
Async XLA Ops:
  7.2 108.6 %copy-start = (bf16[2560,320]{0,1:T(8,128)(2,1)S(1)}, bf16[2560,320]{0,1:T(8,128)(2,1)}, u32[]{:S(2)}) copy-start(bf16[2560,320]{0,1:T(8,128)(2,1)} %param.25) | copy-start | bytes 4915204
  7.2 217.9 %all-gather.8.cloned.1.call-start = ((), (), s32[]{:S(2)}) async-start(), calls=%async_computation.3 | async-start | bytes 11141120 | tf_op jit(solution)/shard_map/all_gather | solution.py:127
  15.3 5.1 %copy-start.2 = (bf16[768,4,128]{2,0,1:T(8,128)(2,1)S(1)}, bf16[768,4,128]{2,0,1:T(8,128)(2,1)}, u32[]{:S(2)}) copy-start(bf16[768,4,128]{2,0,1:T(8,128)(2,1)} %copy.136) | copy-start | bytes 2359300
  16.1 4.3 %copy-start.3 = (bf16[128,4,128]{2,0,1:T(8,128)(2,1)S(1)}, bf16[128,4,128]{2,0,1:T(8,128)(2,1)}, u32[]{:S(2)}) copy-start(bf16[128,4,128]{2,0,1:T(8,128)(2,1)} %copy.137) | copy-start | bytes 393220
  31.1 1.2 copy-start.7
  32.2 210.2 %reduce-scatter.2.cloned.1.call-start = ((), (), s32[]{:S(2)}) async-start(), calls=%async_computation.4 | async-start | bytes 4718592 | tf_op jit(solution)/shard_map/reduce_scatter | solution.py:199
  34.5 2.3 copy-start.4
  34.5 2.3 copy-start.8
  105.7 1.1 copy-start.1
  108.7 5.3 %copy-start.6 = (bf16[2,4,512]{2,1,0:T(4,128)(2,1)S(1)}, bf16[2,4,512]{2,1,0:T(4,128)(2,1)}, u32[]{:S(2)}) copy-start(bf16[2,4,512]{2,1,0:T(4,128)(2,1)} %param.21) | copy-start | bytes 24580
  116.3 47.8 %copy-start.5 = (bf16[5120]{0:T(1024)(128)(2,1)S(1)}, bf16[5120]{0:T(1024)(128)(2,1)}, u32[]{:S(2)}) copy-start(bf16[5120]{0:T(1024)(128)(2,1)} %param.26) | copy-start | bytes 30724
  242.5 41.1 %all-to-all-start = ((f32[16,64,320]{2,1,0:T(8,128)}), f32[16,64,320]{2,1,0:T(8,128)S(1)}, u32[]{:S(2)}, u32[]{:S(2)}) async-start(f32[16,64,320]{2,1,0:T(8,128)} %reduce-scatter.2.cloned.1.call-done), calls=%async_computation.1 | async-start | bytes 3145728 | tf_op jit(solution)/shard_map/all_to_all | solution.py:200
Sparse Core Ops, SparseCore 0:
  32.4 159.1 all-gather.7
  235.3 7.1 reduce-scatter.1

commit v4 on v3

--- a/solution.py
+++ b/solution.py
@@ -187,20 +187,22 @@
     logits = jnp.dot(normed, head_weight, preferred_element_type=jnp.float32)
     local_max = jnp.max(logits, axis=-1)
     local_sum = jnp.sum(jnp.exp(logits - local_max[:, None]), axis=-1)
-    stats = lax.all_gather(jnp.stack([local_max, local_sum], -1), ("seq", "tp"), axis=0)
-    global_max = jnp.max(stats[..., 0], axis=0)
-    global_sum = jnp.sum(stats[..., 1] * jnp.exp(stats[..., 0] - global_max[None]), axis=0)
-    log_probs = logits - (global_max + jnp.log(global_sum))[:, None]
-    every_row, decode_out, log_probs = lax.optimization_barrier((every_row, decode_out, log_probs))
-
+    local_stats = jnp.stack([local_max, local_sum], -1)
+    every_row, local_stats = lax.optimization_barrier((every_row, local_stats))
     column_block = jnp.dot(every_row, out_weight, preferred_element_type=jnp.float32)
     prefill_block = column_block.reshape(n_seq, span_len, column_width)
 
     summed_rows = lax.psum_scatter(prefill_block, "tp", scatter_dimension=1, tiled=True)
+    summed_rows, local_stats = lax.optimization_barrier((summed_rows, local_stats))
     by_source = lax.all_to_all(summed_rows, "seq", split_axis=0, concat_axis=0, tiled=True)
     own_columns = lax.all_to_all(by_source, "tp", split_axis=0, concat_axis=1, tiled=True)
     projected = jnp.transpose(own_columns, (1, 0, 2)).reshape(span_len, feature_width)
     prefill_out = (prefill_hidden.astype(jnp.float32) + projected).astype(jnp.bfloat16)
+
+    stats = lax.all_gather(local_stats, ("seq", "tp"), axis=0)
+    global_max = jnp.max(stats[..., 0], axis=0)
+    global_sum = jnp.sum(stats[..., 1] * jnp.exp(stats[..., 0] - global_max[None]), axis=0)
+    log_probs = logits - (global_max + jnp.log(global_sum))[:, None]
 
     return (prefill_out, decode_out, log_probs)
 

time: 303 us -> 298 us (0.983)
  waiting for transfers between devices: 39.4 us -> 16.6 us
  blocking collectives: 155 us -> 174 us
    all_to_all x1, waiting for transfers between devices: 32.1 us -> 0.01 us  [local(): lax.all_to_all(summed_rows, 'seq', split_axis=0, concat_axis=0, tiled=True)]
    all_gather x1, blocking collectives: 39 us -> 57.7 us  [local(): stats = lax.all_gather(local_stats, ('seq', 'tp'), axis=0)]
    all_gather x1, waiting for transfers between devices: 0.01 us -> 6.36 us  [local(): lax.all_gather(prefill_attention, 'seq', axis=0)]
    unnamed x26 -> x28, local copies, waits for them, and re-layouts: 9.01 us -> 9.78 us
  transfers between devices with their start and end apart: 3 -> 3, of which waited for: 2 -> 2; matrix products, arithmetic and copies ran while one was open for 14% -> 15% of each run, Pallas kernels for 0% -> 0%
where the time goes in v4:
time: 298 us
  blocking collectives  174 us (58%)
  matrix products  42.6 us (14%)
  local copies, waits for them, and re-layouts  32.2 us (11%)
  waiting for transfers between devices  16.6 us (6%)
  between operations  14.6 us (5%)
  other arithmetic  10.4 us (3%)
  starting transfers between devices  6.99 us (2%)
    all_gather x1, blocking collectives, local(): small_gathered = lax.all_gather(small_rows, 'seq', axis=0)  64 us
    all_gather x1, blocking collectives, local(): stats = lax.all_gather(local_stats, ('seq', 'tp'), axis=0)  57.7 us
    all_gather x1, blocking collectives, local(): head_all = lax.all_gather(head_part, ('seq', 'tp'), axis=0)  47.5 us
    dot_general x1, matrix products, local(): logits = jnp.dot(normed, head_weight, preferred_element_type=jnp.float32)  19.8 us
    reduce_scatter x1, waiting for transfers between devices, local(): lax.psum_scatter(prefill_block, 'tp', scatter_dimension=1, tiled=True)  10.2 us
    reshape x1, matrix products, local(): prefill_block = column_block.reshape(n_seq, span_len, column_width)  10.1 us
    unnamed x28, local copies, waits for them, and re-layouts  9.78 us
    sub x1, matrix products, local(): weights = jnp.where(live_mask, jnp.exp(masked - row_max), 0.0)  7.22 us
  transfers between devices with their start and end apart: 3, of which 2 were waited for; matrix products, arithmetic and copies ran while one was open for 15% of the time, Pallas kernels for 0%

profile of v4, /device:TPU:0, one launch (start us, length us, event | category | flops | bytes accessed | tf_op | source)
XLA Modules:
  0.0 297.5 jit_solution(882775728363555834)
XLA Ops:
  7.2 1.4 dynamic_slice.14
  8.6 0.6 iota_compare_fusion.1
  9.3 2.4 fusion.61
  11.6 1.4 copy.165
  13.0 1.2 copy.136
  14.2 1.0 fusion.65
  15.3 0.8 copy.137
  16.1 2.2 copy.138
  18.3 1.2 copy.132
  19.5 0.8 fusion.26
  20.4 7.2 %fusion.68 = (f32[4,5,128]{2,1,0:T(8,128)S(1)}, bf16[4,5,128,896]{2,3,1,0:T(8,128)(2,1)}) fusion(pred[128,896]{0,1:T(8,128)(4,1)S(1)} %fusion.26, bf16[128,4,5,128]{0,3,2,1:T(8,128)(2,1)} %bitcast.116, bf16[128,4,128]{2,0,1:T(8,128)(2,1)S(1)} %copy-done.4, bf16[768,4,128]{2,0,1:T(8,128)(2,1)S(1)} %copy-done.3), kind=kOutput, calls=%fused_computation.103 | convolution fusion | flops 602801024 | bytes 6285312 | tf_op jit(solution)/shard_map/sub | solution.py:91
  27.6 3.5 %fusion.13 = bf16[128,4,5,128]{0,3,2,1:T(8,128)(2,1)S(1)} fusion(bf16[4,5,128,896]{2,3,1,0:T(8,128)(2,1)} %get-tuple-element.54, bf16[128,4,128]{0,2,1:T(8,128)(2,1)S(1)} %bitcast.119, bf16[768,4,128]{0,2,1:T(8,128)(2,1)} %bitcast.115, f32[128,4,5]{0,2,1:T(8,128)S(1)} %bitcast.128), kind=kOutput, calls=%fused_computation.12 | convolution fusion | flops 589692928 | bytes 6170624 | tf_op jit(solution)/shard_map/kgrs,skh->rkgh/dot_general | solution.py:94
  31.1 1.1 copy.141
  32.3 1.9 gather_fusion
  34.5 0.9 fusion.64
  35.4 1.3 copy.142
  36.9 0.3 fusion.67
  37.3 0.3 copy.144
  37.6 1.0 subtract_convert_fusion
  39.2 0.5 slice_reduce_fusion
  39.7 0.8 slice.76
  40.5 64.0 %all-gather.3 = bf16[16,11,2560]{2,1,0:T(8,128)(2,1)S(1)} all-gather(bf16[1,11,2560]{2,1,0:T(8,128)(2,1)S(1)} %maximum_bitcast_fusion.9), channel_id=2, replica_groups=mesh['seq'=16,'tp'=2] {'seq'}, dimensions={0}, use_global_device_ids=true | all-gather | bytes 957440 | tf_op jit(solution)/shard_map/all_gather | solution.py:126
  104.5 0.4 slice_convert_fusion
  104.9 0.9 copy.169
  105.7 1.1 copy-done.1
  107.4 1.3 mul.107
  108.7 2.3 mul.108
  111.0 1.9 fusion.24
  113.0 0.9 fusion.49
  114.9 0.8 dynamic-slice_convert_fusion.1
  115.7 0.6 fusion.36
  116.3 47.5 %all-gather.4 = f32[32,20,320]{2,1,0:T(8,128)S(1)} all-gather(f32[1,20,320]{2,1,0:T(8,128)S(1)} %fusion.36), channel_id=3, replica_groups=mesh['seq'=16,'tp'=2] {'seq','tp'}, dimensions={0}, use_global_device_ids=true | all-gather | bytes 844800 | tf_op jit(solution)/shard_map/all_gather | solution.py:172
  164.1 0.2 multiply_reduce_fusion
  164.3 19.8 %fusion.69 = (f32[20]{0:T(128)S(1)}, f32[20,4752]{1,0:T(8,128)S(1)}) fusion(bf16[5120,4752]{0,1:T(8,128)(2,1)} %param.27, f32[20,5120]{1,0:T(8,128)S(1)} %reshape.181, f32[5120]{0:T(1024)S(1)} %convert_element_type.132, f32[20]{0:T(128)S(1)} %add_rsqrt_fusion), kind=kOutput, calls=%fused_computation.104 | convolution fusion | flops 973611840 | bytes 49470880 | tf_op jit(solution)/shard_map/dot_general | solution.py:187
  184.1 0.8 copy-done.2
  184.9 0.3 exponential_reduce_fusion
  185.2 6.4 %all-gather.8.cloned.1.call-done = bf16[16,128,2560]{2,1,0:T(8,128)(2,1)} async-done(((bf16[1,128,2560]{2,1,0:T(8,128)(2,1)}), bf16[16,128,2560]{2,1,0:T(8,128)(2,1)}) %all-gather.8.cloned.1.call-update) | async-done | bytes 10485776 | tf_op jit(solution)/shard_map/all_gather | solution.py:127
  191.5 10.1 %fusion.71 = f32[2048,320]{1,0:T(8,128)} fusion(bf16[2048,2560]{1,0:T(8,128)(2,1)} %bitcast.127, bf16[2560,320]{0,1:T(8,128)(2,1)S(1)} %copy-done), kind=kOutput, calls=%fused_computation.106 | convolution fusion | flops 3355443200 | bytes 14745600 | tf_op jit(solution)/shard_map/reshape | solution.py:193
  201.6 10.2 %reduce-scatter.2.cloned.1.call-done = f32[16,64,320]{2,1,0:T(8,128)} async-done(((f32[16,128,320]{2,1,0:T(8,128)}), f32[16,64,320]{2,1,0:T(8,128)}) %reduce-scatter.2.cloned.1.call-update) | async-done | bytes 1310736 | tf_op jit(solution)/shard_map/reduce_scatter | solution.py:195
  211.9 6.9 %all-to-all-start = ((f32[16,64,320]{2,1,0:T(8,128)}), f32[16,64,320]{2,1,0:T(8,128)S(1)}, u32[]{:S(2)}, u32[]{:S(2)}) async-start(f32[16,64,320]{2,1,0:T(8,128)} %reduce-scatter.2.cloned.1.call-done), calls=%async_computation.1 | async-start | bytes 3145728 | tf_op jit(solution)/shard_map/all_to_all | solution.py:197
  218.8 2.2 copy.131
  221.1 0.6 constant_dynamic-slice_fusion
  221.7 57.7 %all-gather.5 = f32[32,20,2]{1,2,0:T(2,128)S(1)} all-gather(f32[1,20,2]{1,2,0:T(2,128)S(1)} %bitcast.125), channel_id=4, replica_groups=mesh['seq'=16,'tp'=2] {'seq','tp'}, dimensions={0}, use_global_device_ids=true | all-gather | bytes 5280 | tf_op jit(solution)/shard_map/all_gather | solution.py:202
  279.4 1.9 broadcast_subtract_fusion
  281.3 5.0 %all_to_all.23 = f32[16,64,320]{2,1,0:T(8,128)S(1)} all-to-all(f32[16,64,320]{2,1,0:T(8,128)S(1)} %all-to-all-done), channel_id=1, replica_groups=mesh['seq'=16,'tp'=2] {'tp'}, dimensions={0} | all-to-all | bytes 2621440 | tf_op jit(solution)/shard_map/all_to_all | solution.py:198
  286.5 1.5 copy.152
  288.0 1.6 fusion.16
  289.6 1.1 copy.154
  (81 shorter events, 3.6 us)
Async XLA Ops:
  7.2 108.6 %copy-start = (bf16[2560,320]{0,1:T(8,128)(2,1)S(1)}, bf16[2560,320]{0,1:T(8,128)(2,1)}, u32[]{:S(2)}) copy-start(bf16[2560,320]{0,1:T(8,128)(2,1)} %param.25) | copy-start | bytes 4915204
  7.2 184.4 %all-gather.8.cloned.1.call-start = ((), (), s32[]{:S(2)}) async-start(), calls=%async_computation.3 | async-start | bytes 11141120 | tf_op jit(solution)/shard_map/all_gather | solution.py:127
  15.3 5.1 %copy-start.3 = (bf16[768,4,128]{2,0,1:T(8,128)(2,1)S(1)}, bf16[768,4,128]{2,0,1:T(8,128)(2,1)}, u32[]{:S(2)}) copy-start(bf16[768,4,128]{2,0,1:T(8,128)(2,1)} %copy.136) | copy-start | bytes 2359300
  16.1 4.3 %copy-start.4 = (bf16[128,4,128]{2,0,1:T(8,128)(2,1)S(1)}, bf16[128,4,128]{2,0,1:T(8,128)(2,1)}, u32[]{:S(2)}) copy-start(bf16[128,4,128]{2,0,1:T(8,128)(2,1)} %copy.137) | copy-start | bytes 393220
  31.1 1.2 copy-start.8
  32.2 179.6 %reduce-scatter.2.cloned.1.call-start = ((), (), s32[]{:S(2)}) async-start(), calls=%async_computation.4 | async-start | bytes 4718592 | tf_op jit(solution)/shard_map/reduce_scatter | solution.py:195
  34.5 2.3 copy-start.5
  34.5 2.3 copy-start.9
  105.7 1.1 copy-start.1
  108.7 5.3 %copy-start.7 = (bf16[2,4,512]{2,1,0:T(4,128)(2,1)S(1)}, bf16[2,4,512]{2,1,0:T(4,128)(2,1)}, u32[]{:S(2)}) copy-start(bf16[2,4,512]{2,1,0:T(4,128)(2,1)} %param.21) | copy-start | bytes 24580
  116.3 47.8 %copy-start.6 = (bf16[5120]{0:T(1024)(128)(2,1)S(1)}, bf16[5120]{0:T(1024)(128)(2,1)}, u32[]{:S(2)}) copy-start(bf16[5120]{0:T(1024)(128)(2,1)} %param.26) | copy-start | bytes 30724
  184.1 0.8 copy-start.2
  211.9 69.5 %all-to-all-start = ((f32[16,64,320]{2,1,0:T(8,128)}), f32[16,64,320]{2,1,0:T(8,128)S(1)}, u32[]{:S(2)}, u32[]{:S(2)}) async-start(f32[16,64,320]{2,1,0:T(8,128)} %reduce-scatter.2.cloned.1.call-done), calls=%async_computation.1 | async-start | bytes 3145728 | tf_op jit(solution)/shard_map/all_to_all | solution.py:197
Sparse Core Ops, SparseCore 0:
  32.4 159.1 all-gather.7
  201.8 10.0 reduce-scatter.1

commit v5 on v3

--- a/solution.py
+++ b/solution.py
@@ -13,6 +13,24 @@
 neg_large = -1e30
 exact = lax.Precision.HIGHEST
 norm_eps = 1e-06
+
+
+def doubling_gather(value, axis):
+    count = lax.axis_size(axis)
+    if count & (count - 1):
+        return lax.all_gather(value, axis, axis=0)
+    index = lax.axis_index(axis)
+    block = value[None]
+    distance = 1
+    while distance < count:
+        pairs = [(i, i ^ distance) for i in range(count)]
+        other = lax.ppermute(block, axis, pairs)
+        low = (index & distance) == 0
+        block = jnp.where(
+            low, jnp.concatenate([block, other], 0), jnp.concatenate([other, block], 0)
+        )
+        distance *= 2
+    return block
 
 
 def local(
@@ -123,7 +141,7 @@
         ],
         0,
     )
-    small_gathered = lax.all_gather(small_rows, "seq", axis=0)
+    small_gathered = doubling_gather(small_rows, "seq")
     every_row = lax.all_gather(prefill_attention, "seq", axis=0).reshape(n_seq * span_len, feature_width)
     last_attention = small_gathered[:, 0]
     last_hidden = small_gathered[:, 1].astype(jnp.float32)
@@ -169,7 +187,7 @@
     head_attention = jnp.concatenate([decode_attention, last_attention], 0)
     head_part = jnp.dot(head_attention, out_weight, preferred_element_type=jnp.float32)
     head_part = jnp.where(owner_tp == tp_index, head_part + head_hidden_cols, head_part)
-    head_all = lax.all_gather(head_part, ("seq", "tp"), axis=0)
+    head_all = doubling_gather(doubling_gather(head_part, "tp"), "seq")
     head_rows_count = decode_count + n_seq
     head_all = head_all.reshape(n_seq, n_tp, head_rows_count, column_width)
     head_sum = jnp.sum(head_all, axis=1)
@@ -187,7 +205,10 @@
     logits = jnp.dot(normed, head_weight, preferred_element_type=jnp.float32)
     local_max = jnp.max(logits, axis=-1)
     local_sum = jnp.sum(jnp.exp(logits - local_max[:, None]), axis=-1)
-    stats = lax.all_gather(jnp.stack([local_max, local_sum], -1), ("seq", "tp"), axis=0)
+    local_stats = jnp.stack([local_max, local_sum], -1)
+    stats = doubling_gather(doubling_gather(local_stats, "tp"), "seq").reshape(
+        (n_seq * n_tp,) + local_stats.shape
+    )
     global_max = jnp.max(stats[..., 0], axis=0)
     global_sum = jnp.sum(stats[..., 1] * jnp.exp(stats[..., 0] - global_max[None]), axis=0)
     log_probs = logits - (global_max + jnp.log(global_sum))[:, None]
@@ -201,6 +222,7 @@
     own_columns = lax.all_to_all(by_source, "tp", split_axis=0, concat_axis=1, tiled=True)
     projected = jnp.transpose(own_columns, (1, 0, 2)).reshape(span_len, feature_width)
     prefill_out = (prefill_hidden.astype(jnp.float32) + projected).astype(jnp.bfloat16)
+
 
     return (prefill_out, decode_out, log_probs)
 

time: 303 us -> 330 us (1.089)
  waiting for transfers between devices: 39.4 us -> 198 us
  blocking collectives: 155 us -> 4.99 us
  starting transfers between devices: 6.98 us -> 22.8 us
    ppermute x0 -> x14, waiting for transfers between devices: none -> 156 us  [doubling_gather(): other = lax.ppermute(block, axis, pairs)]
    all_gather x3 -> x0, blocking collectives: 150 us -> none  [the longest x1 64 us: local(): small_gathered = lax.all_gather(small_rows, 'seq', axis=0)]
    ppermute x0 -> x14, starting transfers between devices: none -> 15.9 us  [doubling_gather(): other = lax.ppermute(block, axis, pairs)]
  transfers between devices with their start and end apart: 3 -> 17, of which waited for: 2 -> 16; matrix products, arithmetic and copies ran while one was open for 14% -> 14% of each run, Pallas kernels for 0% -> 0%
where the time goes in v5:
time: 330 us; the launch traced here: 327 us
  waiting for transfers between devices  198 us (60%)
  matrix products  42.6 us (13%)
  local copies, waits for them, and re-layouts  32.6 us (10%)
  starting transfers between devices  22.8 us (7%)
  between operations  14.6 us (4%)
  other arithmetic  11.6 us (4%)
  blocking collectives  4.99 us (2%)
    ppermute x14, waiting for transfers between devices, doubling_gather(): other = lax.ppermute(block, axis, pairs)  156 us
    all_to_all x1, waiting for transfers between devices, local(): lax.all_to_all(summed_rows, 'seq', split_axis=0, concat_axis=0, tiled=True)  32.1 us
    dot_general x1, matrix products, local(): logits = jnp.dot(normed, head_weight, preferred_element_type=jnp.float32)  19.8 us
    ppermute x14, starting transfers between devices, doubling_gather(): other = lax.ppermute(block, axis, pairs)  15.9 us
    reshape x1, matrix products, local(): prefill_block = column_block.reshape(n_seq, span_len, column_width)  10.1 us
    unnamed x26, local copies, waits for them, and re-layouts  9.89 us
    reduce_scatter x1, waiting for transfers between devices, local(): lax.psum_scatter(prefill_block, 'tp', scatter_dimension=1, tiled=True)  9.46 us
    sub x1, matrix products, local(): weights = jnp.where(live_mask, jnp.exp(masked - row_max), 0.0)  7.26 us
  transfers between devices with their start and end apart: 17, of which 16 were waited for; matrix products, arithmetic and copies ran while one was open for 14% of the time, Pallas kernels for 0%

profile of v5, /device:TPU:0, one launch (start us, length us, event | category | flops | bytes accessed | tf_op | source)
XLA Modules:
  0.0 326.9 jit_solution(11844118300685597473)
XLA Ops:
  7.2 1.4 dynamic_slice.14
  9.2 2.4 fusion.61
  11.6 1.4 copy.181
  13.0 1.2 copy.146
  15.4 2.2 copy.148
  17.7 1.2 copy.142
  19.8 7.3 %fusion.68 = (f32[4,5,128]{2,1,0:T(8,128)S(1)}, bf16[4,5,128,896]{2,3,1,0:T(8,128)(2,1)}) fusion(pred[128,896]{0,1:T(8,128)(4,1)S(1)} %fusion.27, bf16[128,4,5,128]{0,3,2,1:T(8,128)(2,1)} %bitcast.120, bf16[128,4,128]{2,0,1:T(8,128)(2,1)S(1)} %copy.147, bf16[768,4,128]{2,0,1:T(8,128)(2,1)S(1)} %copy-done.3), kind=kOutput, calls=%fused_computation.117 | convolution fusion | flops 602801024 | bytes 6285312 | tf_op jit(solution)/shard_map/sub | solution.py:109
  27.0 3.5 %fusion.13 = bf16[128,4,5,128]{0,3,2,1:T(8,128)(2,1)S(1)} fusion(bf16[4,5,128,896]{2,3,1,0:T(8,128)(2,1)} %get-tuple-element.53, bf16[128,4,128]{0,2,1:T(8,128)(2,1)S(1)} %bitcast.127, bf16[768,4,128]{0,2,1:T(8,128)(2,1)} %bitcast.119, f32[128,4,5]{0,2,1:T(8,128)S(1)} %bitcast.137), kind=kOutput, calls=%fused_computation.12 | convolution fusion | flops 589692928 | bytes 6170624 | tf_op jit(solution)/shard_map/kgrs,skh->rkgh/dot_general | solution.py:112
  30.6 1.1 copy.151
  31.8 1.9 gather_fusion
  34.8 1.3 copy.152
  40.1 3.0 collective-permute-start
  43.2 3.6 %collective-permute-done = bf16[1,11,2560]{2,1,0:T(8,128)(2,1)S(1)} collective-permute-done((bf16[1,11,2560]{2,1,0:T(8,128)(2,1)S(1)}, bf16[1,11,2560]{2,1,0:T(8,128)(2,1)S(1)}, u32[]{:S(2)}, u32[]{:S(2)}) %collective-permute-start) | collective-permute-done | bytes 56352 | tf_op jit(solution)/shard_map/ppermute | solution.py:27
  46.8 1.6 collective-permute-start.1
  48.4 5.9 %collective-permute-done.1 = bf16[2,11,2560]{2,1,0:T(8,128)(2,1)S(1)} collective-permute-done((bf16[2,11,2560]{2,1,0:T(8,128)(2,1)S(1)}, bf16[2,11,2560]{2,1,0:T(8,128)(2,1)S(1)}, u32[]{:S(2)}, u32[]{:S(2)}) %collective-permute-start.1) | collective-permute-done | bytes 112672 | tf_op jit(solution)/shard_map/ppermute | solution.py:27
  54.4 1.6 collective-permute-start.2
  56.0 12.5 %collective-permute-done.2 = bf16[4,11,2560]{2,1,0:T(8,128)(2,1)S(1)} collective-permute-done((bf16[4,11,2560]{2,1,0:T(8,128)(2,1)S(1)}, bf16[4,11,2560]{2,1,0:T(8,128)(2,1)S(1)}, u32[]{:S(2)}, u32[]{:S(2)}) %collective-permute-start.2) | collective-permute-done | bytes 225312 | tf_op jit(solution)/shard_map/ppermute | solution.py:27
  69.8 1.8 collective-permute-start.3
  72.5 41.1 %collective-permute-done.3 = bf16[8,11,2560]{2,0,1:T(8,128)(2,1)S(1)} collective-permute-done((bf16[8,11,2560]{2,0,1:T(8,128)(2,1)S(1)}, bf16[8,11,2560]{2,0,1:T(8,128)(2,1)S(1)}, u32[]{:S(2)}, u32[]{:S(2)}) %collective-permute-start.3) | collective-permute-done | bytes 450592 | tf_op jit(solution)/shard_map/ppermute | solution.py:27
  113.8 1.7 maximum_select_fusion
  116.7 1.1 copy-done.2
  118.3 1.3 mul.107
  119.6 2.3 mul.108
  121.9 1.9 fusion.25
  126.3 1.2 collective-permute-done.4
  128.5 5.6 %collective-permute-done.5 = f32[1,2,20,320]{3,2,1,0:T(8,128)S(1)} collective-permute-done((f32[1,2,20,320]{3,2,1,0:T(8,128)S(1)}, f32[1,2,20,320]{3,2,1,0:T(8,128)S(1)}, u32[]{:S(2)}, u32[]{:S(2)}) %collective-permute-start.5) | collective-permute-done | bytes 51232 | tf_op jit(solution)/shard_map/ppermute | solution.py:27
  135.0 8.6 %collective-permute-done.6 = f32[2,2,20,320]{3,2,1,0:T(8,128)S(1)} collective-permute-done((f32[2,2,20,320]{3,2,1,0:T(8,128)S(1)}, f32[2,2,20,320]{3,2,1,0:T(8,128)S(1)}, u32[]{:S(2)}, u32[]{:S(2)}) %collective-permute-start.6) | collective-permute-done | bytes 102432 | tf_op jit(solution)/shard_map/ppermute | solution.py:27
  143.6 1.8 collective-permute-start.7
  145.4 23.7 %collective-permute-done.7 = f32[4,2,20,320]{3,2,1,0:T(8,128)S(1)} collective-permute-done((f32[4,2,20,320]{3,2,1,0:T(8,128)S(1)}, f32[4,2,20,320]{3,2,1,0:T(8,128)S(1)}, u32[]{:S(2)}, u32[]{:S(2)}) %collective-permute-start.7) | collective-permute-done | bytes 204832 | tf_op jit(solution)/shard_map/ppermute | solution.py:27
  169.4 1.3 collective-permute-start.8
  170.7 40.6 %collective-permute-done.8 = f32[8,2,20,320]{3,0,2,1:T(8,128)S(1)} collective-permute-done((f32[8,2,20,320]{3,0,2,1:T(8,128)S(1)}, f32[8,2,20,320]{3,0,2,1:T(8,128)S(1)}, u32[]{:S(2)}, u32[]{:S(2)}) %collective-permute-start.8) | collective-permute-done | bytes 409632 | tf_op jit(solution)/shard_map/ppermute | solution.py:27
  212.0 19.8 %fusion.69 = (f32[20]{0:T(128)S(1)}, f32[20,4752]{1,0:T(8,128)S(1)}) fusion(bf16[5120,4752]{0,1:T(8,128)(2,1)} %param.27, f32[20,5120]{1,0:T(8,128)S(1)} %reshape.296, f32[5120]{0:T(1024)S(1)} %convert_element_type.132, f32[20]{0:T(128)S(1)} %add_rsqrt_fusion), kind=kOutput, calls=%fused_computation.118 | convolution fusion | flops 973611840 | bytes 49470880 | tf_op jit(solution)/shard_map/dot_general | solution.py:205
  232.1 1.1 collective-permute-done.9
  233.3 1.4 collective-permute-start.10
  234.7 2.1 collective-permute-done.10
  236.9 1.1 collective-permute-start.11
  238.0 2.5 collective-permute-done.11
  240.7 3.5 %collective-permute-done.12 = f32[4,2,20,2]{2,3,1,0:T(2,128)S(1)} collective-permute-done((f32[4,2,20,2]{2,3,1,0:T(2,128)S(1)}, f32[4,2,20,2]{2,3,1,0:T(2,128)S(1)}, u32[]{:S(2)}, u32[]{:S(2)}) %collective-permute-start.12) | collective-permute-done | bytes 1312 | tf_op jit(solution)/shard_map/ppermute | solution.py:27
  244.9 4.0 %collective-permute-done.13 = f32[8,2,20,2]{2,3,1,0:T(2,128)S(1)} collective-permute-done((f32[8,2,20,2]{2,3,1,0:T(2,128)S(1)}, f32[8,2,20,2]{2,3,1,0:T(2,128)S(1)}, u32[]{:S(2)}, u32[]{:S(2)}) %collective-permute-start.13) | collective-permute-done | bytes 2592 | tf_op jit(solution)/shard_map/ppermute | solution.py:27
  249.9 10.1 %fusion.71 = f32[2048,320]{1,0:T(8,128)} fusion(bf16[2048,2560]{1,0:T(8,128)(2,1)} %bitcast.136, bf16[2560,320]{0,1:T(8,128)(2,1)S(1)} %copy-done), kind=kOutput, calls=%fused_computation.120 | convolution fusion | flops 3355443200 | bytes 14745600 | tf_op jit(solution)/shard_map/reshape | solution.py:218
  260.0 9.5 %reduce-scatter.2.cloned.1.call-done = f32[16,64,320]{2,1,0:T(8,128)} async-done(((f32[16,128,320]{2,1,0:T(8,128)}), f32[16,64,320]{2,1,0:T(8,128)}) %reduce-scatter.2.cloned.1.call-update) | async-done | bytes 1310736 | tf_op jit(solution)/shard_map/reduce_scatter | solution.py:220
  269.5 6.9 %all-to-all-start = ((f32[16,64,320]{2,1,0:T(8,128)}), f32[16,64,320]{2,1,0:T(8,128)S(1)}, u32[]{:S(2)}, u32[]{:S(2)}) async-start(f32[16,64,320]{2,1,0:T(8,128)} %reduce-scatter.2.cloned.1.call-done), calls=%async_computation.1 | async-start | bytes 3145728 | tf_op jit(solution)/shard_map/all_to_all | solution.py:221
  276.4 2.2 copy.141
  278.6 32.1 %all-to-all-done = f32[16,64,320]{2,1,0:T(8,128)S(1)} async-done(((f32[16,64,320]{2,1,0:T(8,128)}), f32[16,64,320]{2,1,0:T(8,128)S(1)}, u32[]{:S(2)}, u32[]{:S(2)}) %all-to-all-start) | async-done | bytes 1310752 | tf_op jit(solution)/shard_map/all_to_all | solution.py:221
  310.6 5.0 %all_to_all.23 = f32[16,64,320]{2,1,0:T(8,128)S(1)} all-to-all(f32[16,64,320]{2,1,0:T(8,128)S(1)} %all-to-all-done), channel_id=1, replica_groups=mesh['seq'=16,'tp'=2] {'tp'}, dimensions={0} | all-to-all | bytes 2621440 | tf_op jit(solution)/shard_map/all_to_all | solution.py:222
  315.8 1.5 copy.168
  317.3 1.6 fusion.16
  318.9 1.1 copy.169
  (122 shorter events, 19.7 us)
Async XLA Ops:
  7.2 118.5 %copy-start = (bf16[2560,320]{0,1:T(8,128)(2,1)S(1)}, bf16[2560,320]{0,1:T(8,128)(2,1)}, u32[]{:S(2)}) copy-start(bf16[2560,320]{0,1:T(8,128)(2,1)} %param.25) | copy-start | bytes 4915204
  7.2 242.8 %all-gather.2.cloned.1.call-start = ((), (), s32[]{:S(2)}) async-start(), calls=%async_computation.3 | async-start | bytes 11141120 | tf_op jit(solution)/shard_map/all_gather | solution.py:145
  15.4 4.3 %copy-start.3 = (bf16[768,4,128]{2,0,1:T(8,128)(2,1)S(1)}, bf16[768,4,128]{2,0,1:T(8,128)(2,1)}, u32[]{:S(2)}) copy-start(bf16[768,4,128]{2,0,1:T(8,128)(2,1)} %copy.146) | copy-start | bytes 2359300
  30.6 1.2 copy-start.7
  31.7 237.8 %reduce-scatter.2.cloned.1.call-start = ((), (), s32[]{:S(2)}) async-start(), calls=%async_computation.4 | async-start | bytes 4718592 | tf_op jit(solution)/shard_map/reduce_scatter | solution.py:220
  33.9 2.3 copy-start.4
  33.9 2.3 copy-start.8
  40.1 6.6 %collective-permute-start = (bf16[1,11,2560]{2,1,0:T(8,128)(2,1)S(1)}, bf16[1,11,2560]{2,1,0:T(8,128)(2,1)S(1)}, u32[]{:S(2)}, u32[]{:S(2)}) collective-permute-start(bf16[1,11,2560]{2,1,0:T(8,128)(2,1)S(1)} %maximum_bitcast_fusion.9), channel_id=1, source_target_pairs={{0,2},{2,0},{4,6},{6,4},{8,10},{10,8},{12,14},{14,12},{16,18},{18,... | collective-permute-start | bytes 168968 | tf_op jit(solution)/shard_map/ppermute | solution.py:27
  43.2 28.4 %copy-start.6 = (bf16[2,4,512]{2,1,0:T(4,128)(2,1)S(1)}, bf16[2,4,512]{2,1,0:T(4,128)(2,1)}, u32[]{:S(2)}) copy-start(bf16[2,4,512]{2,1,0:T(4,128)(2,1)} %param.21) | copy-start | bytes 24580
  46.8 7.5 %collective-permute-start.1 = (bf16[2,11,2560]{2,1,0:T(8,128)(2,1)S(1)}, bf16[2,11,2560]{2,1,0:T(8,128)(2,1)S(1)}, u32[]{:S(2)}, u32[]{:S(2)}) collective-permute-start(bf16[2,11,2560]{2,1,0:T(8,128)(2,1)S(1)} %maximum_select_fusion.6), channel_id=1, source_target_pairs={{0,4},{2,6},{4,0},{6,2},{8,12},{10,14},{12,8},{14,10},{16,20},{18,... | collective-permute-start | bytes 337928 | tf_op jit(solution)/shard_map/ppermute | solution.py:27
  54.4 14.1 %collective-permute-start.2 = (bf16[4,11,2560]{2,1,0:T(8,128)(2,1)S(1)}, bf16[4,11,2560]{2,1,0:T(8,128)(2,1)S(1)}, u32[]{:S(2)}, u32[]{:S(2)}) collective-permute-start(bf16[4,11,2560]{2,1,0:T(8,128)(2,1)S(1)} %maximum_select_fusion.4), channel_id=1, source_target_pairs={{0,8},{2,10},{4,12},{6,14},{8,0},{10,2},{12,4},{14,6},{16,24},{18,... | collective-permute-start | bytes 675848 | tf_op jit(solution)/shard_map/ppermute | solution.py:27
  68.6 0.9 copy-start.1
  69.8 43.8 %collective-permute-start.3 = (bf16[8,11,2560]{2,0,1:T(8,128)(2,1)S(1)}, bf16[8,11,2560]{2,0,1:T(8,128)(2,1)S(1)}, u32[]{:S(2)}, u32[]{:S(2)}) collective-permute-start(bf16[8,11,2560]{2,0,1:T(8,128)(2,1)S(1)} %copy.156), channel_id=1, source_target_pairs={{0,16},{2,18},{4,20},{6,22},{8,24},{10,26},{12,28},{14,30},{16,0},... | collective-permute-start | bytes 1351688 | tf_op jit(solution)/shard_map/ppermute | solution.py:27
  116.7 1.1 copy-start.2
  126.2 1.3 collective-permute-start.4
  127.5 43.2 %copy-start.5 = (bf16[5120]{0:T(1024)(128)(2,1)S(1)}, bf16[5120]{0:T(1024)(128)(2,1)}, u32[]{:S(2)}) copy-start(bf16[5120]{0:T(1024)(128)(2,1)} %param.26) | copy-start | bytes 30724
  127.5 6.6 %collective-permute-start.5 = (f32[1,2,20,320]{3,2,1,0:T(8,128)S(1)}, f32[1,2,20,320]{3,2,1,0:T(8,128)S(1)}, u32[]{:S(2)}, u32[]{:S(2)}) collective-permute-start(f32[1,2,20,320]{3,2,1,0:T(8,128)S(1)} %maximum_select_fusion.8), channel_id=1, source_target_pairs={{0,2},{2,0},{4,6},{6,4},{8,10},{10,8},{12,14},{14,12},{16,18},{18,... | collective-permute-start | bytes 153608 | tf_op jit(solution)/shard_map/ppermute | solution.py:27
  134.1 9.5 %collective-permute-start.6 = (f32[2,2,20,320]{3,2,1,0:T(8,128)S(1)}, f32[2,2,20,320]{3,2,1,0:T(8,128)S(1)}, u32[]{:S(2)}, u32[]{:S(2)}) collective-permute-start(f32[2,2,20,320]{3,2,1,0:T(8,128)S(1)} %maximum_select_fusion.7), channel_id=1, source_target_pairs={{0,4},{2,6},{4,0},{6,2},{8,12},{10,14},{12,8},{14,10},{16,20},{18,... | collective-permute-start | bytes 307208 | tf_op jit(solution)/shard_map/ppermute | solution.py:27
  143.6 25.5 %collective-permute-start.7 = (f32[4,2,20,320]{3,2,1,0:T(8,128)S(1)}, f32[4,2,20,320]{3,2,1,0:T(8,128)S(1)}, u32[]{:S(2)}, u32[]{:S(2)}) collective-permute-start(f32[4,2,20,320]{3,2,1,0:T(8,128)S(1)} %maximum_select_fusion.5), channel_id=1, source_target_pairs={{0,8},{2,10},{4,12},{6,14},{8,0},{10,2},{12,4},{14,6},{16,24},{18,... | collective-permute-start | bytes 614408 | tf_op jit(solution)/shard_map/ppermute | solution.py:27
  169.4 41.9 %collective-permute-start.8 = (f32[8,2,20,320]{3,0,2,1:T(8,128)S(1)}, f32[8,2,20,320]{3,0,2,1:T(8,128)S(1)}, u32[]{:S(2)}, u32[]{:S(2)}) collective-permute-start(f32[8,2,20,320]{3,0,2,1:T(8,128)S(1)} %copy.161), channel_id=1, source_target_pairs={{0,16},{2,18},{4,20},{6,22},{8,24},{10,26},{12,28},{14,30},{16,0},... | collective-permute-start | bytes 1228808 | tf_op jit(solution)/shard_map/ppermute | solution.py:27
  232.1 1.2 collective-permute-start.9
  233.3 3.6 %collective-permute-start.10 = (f32[1,2,20,2]{2,3,1,0:T(2,128)S(1)}, f32[1,2,20,2]{2,3,1,0:T(2,128)S(1)}, u32[]{:S(2)}, u32[]{:S(2)}) collective-permute-start(f32[1,2,20,2]{2,3,1,0:T(2,128)S(1)} %maximum_select_fusion.13), channel_id=1, source_target_pairs={{0,2},{2,0},{4,6},{6,4},{8,10},{10,8},{12,14},{14,12},{16,18},{18,... | collective-permute-start | bytes 968 | tf_op jit(solution)/shard_map/ppermute | solution.py:27
  236.9 3.6 %collective-permute-start.11 = (f32[2,2,20,2]{2,3,1,0:T(2,128)S(1)}, f32[2,2,20,2]{2,3,1,0:T(2,128)S(1)}, u32[]{:S(2)}, u32[]{:S(2)}) collective-permute-start(f32[2,2,20,2]{2,3,1,0:T(2,128)S(1)} %maximum_select_fusion.12), channel_id=1, source_target_pairs={{0,4},{2,6},{4,0},{6,2},{8,12},{10,14},{12,8},{14,10},{16,20},{18,... | collective-permute-start | bytes 1928 | tf_op jit(solution)/shard_map/ppermute | solution.py:27
  240.5 3.7 %collective-permute-start.12 = (f32[4,2,20,2]{2,3,1,0:T(2,128)S(1)}, f32[4,2,20,2]{2,3,1,0:T(2,128)S(1)}, u32[]{:S(2)}, u32[]{:S(2)}) collective-permute-start(f32[4,2,20,2]{2,3,1,0:T(2,128)S(1)} %maximum_select_fusion.11), channel_id=1, source_target_pairs={{0,8},{2,10},{4,12},{6,14},{8,0},{10,2},{12,4},{14,6},{16,24},{18,... | collective-permute-start | bytes 3848 | tf_op jit(solution)/shard_map/ppermute | solution.py:27
  244.2 4.7 %collective-permute-start.13 = (f32[8,2,20,2]{2,3,1,0:T(2,128)S(1)}, f32[8,2,20,2]{2,3,1,0:T(2,128)S(1)}, u32[]{:S(2)}, u32[]{:S(2)}) collective-permute-start(f32[8,2,20,2]{2,3,1,0:T(2,128)S(1)} %maximum_select_fusion.10), channel_id=1, source_target_pairs={{0,16},{2,18},{4,20},{6,22},{8,24},{10,26},{12,28},{14,30},{16,0},... | collective-permute-start | bytes 7688 | tf_op jit(solution)/shard_map/ppermute | solution.py:27
  269.5 41.1 %all-to-all-start = ((f32[16,64,320]{2,1,0:T(8,128)}), f32[16,64,320]{2,1,0:T(8,128)S(1)}, u32[]{:S(2)}, u32[]{:S(2)}) async-start(f32[16,64,320]{2,1,0:T(8,128)} %reduce-scatter.2.cloned.1.call-done), calls=%async_computation.1 | async-start | bytes 3145728 | tf_op jit(solution)/shard_map/all_to_all | solution.py:221
Sparse Core Ops, SparseCore 0:
  31.8 178.6 all-gather.1
  260.2 9.2 reduce-scatter.1

commit v6 on v5

--- a/solution.py
+++ b/solution.py
@@ -141,7 +141,7 @@
         ],
         0,
     )
-    small_gathered = doubling_gather(small_rows, "seq")
+    small_gathered = lax.all_gather(small_rows, "seq", axis=0)
     every_row = lax.all_gather(prefill_attention, "seq", axis=0).reshape(n_seq * span_len, feature_width)
     last_attention = small_gathered[:, 0]
     last_hidden = small_gathered[:, 1].astype(jnp.float32)
@@ -187,7 +187,7 @@
     head_attention = jnp.concatenate([decode_attention, last_attention], 0)
     head_part = jnp.dot(head_attention, out_weight, preferred_element_type=jnp.float32)
     head_part = jnp.where(owner_tp == tp_index, head_part + head_hidden_cols, head_part)
-    head_all = doubling_gather(doubling_gather(head_part, "tp"), "seq")
+    head_all = lax.all_gather(head_part, ("seq", "tp"), axis=0)
     head_rows_count = decode_count + n_seq
     head_all = head_all.reshape(n_seq, n_tp, head_rows_count, column_width)
     head_sum = jnp.sum(head_all, axis=1)

time: 330 us -> 283 us (0.86)
  waiting for transfers between devices: 198 us -> 54.8 us
  blocking collectives: 4.99 us -> 117 us
  starting transfers between devices: 22.8 us -> 9.6 us
    ppermute x14 -> x5, waiting for transfers between devices: 156 us -> 13.5 us  [doubling_gather(): other = lax.ppermute(block, axis, pairs)]
    all_gather x0 -> x2, blocking collectives: none -> 112 us  [the longest x1 64.7 us: local(): small_gathered = lax.all_gather(small_rows, 'seq', axis=0)]
    ppermute x14 -> x5, starting transfers between devices: 15.9 us -> 2.63 us  [doubling_gather(): other = lax.ppermute(block, axis, pairs)]
  transfers between devices with their start and end apart: 17 -> 8, of which waited for: 16 -> 7; matrix products, arithmetic and copies ran while one was open for 14% -> 15% of each run, Pallas kernels for 0% -> 0%
where the time goes in v6:
time: 283 us; the launch traced here: 280 us
  blocking collectives  117 us (41%)
  waiting for transfers between devices  54.8 us (19%)
  matrix products  42.6 us (15%)
  local copies, waits for them, and re-layouts  31.5 us (11%)
  between operations  14.6 us (5%)
  starting transfers between devices  9.6 us (3%)
  other arithmetic  9.46 us (3%)
    all_gather x1, blocking collectives, local(): small_gathered = lax.all_gather(small_rows, 'seq', axis=0)  64.7 us
    all_gather x1, blocking collectives, local(): head_all = lax.all_gather(head_part, ('seq', 'tp'), axis=0)  47.7 us
    all_to_all x1, waiting for transfers between devices, local(): lax.all_to_all(summed_rows, 'seq', split_axis=0, concat_axis=0, tiled=True)  32.1 us
    dot_general x1, matrix products, local(): logits = jnp.dot(normed, head_weight, preferred_element_type=jnp.float32)  19.8 us
    ppermute x5, waiting for transfers between devices, doubling_gather(): other = lax.ppermute(block, axis, pairs)  13.5 us
    reshape x1, matrix products, local(): prefill_block = column_block.reshape(n_seq, span_len, column_width)  10.1 us
    reduce_scatter x1, waiting for transfers between devices, local(): lax.psum_scatter(prefill_block, 'tp', scatter_dimension=1, tiled=True)  9.18 us
    unnamed x26, local copies, waits for them, and re-layouts  9.01 us
  transfers between devices with their start and end apart: 8, of which 7 were waited for; matrix products, arithmetic and copies ran while one was open for 15% of the time, Pallas kernels for 0%

profile of v6, /device:TPU:0, one launch (start us, length us, event | category | flops | bytes accessed | tf_op | source)
XLA Modules:
  0.0 280.0 jit_solution(16204195157827423159)
XLA Ops:
  7.2 1.4 dynamic_slice.14
  8.6 0.6 iota_compare_fusion.1
  9.3 2.4 fusion.63
  11.6 1.4 copy.165
  13.0 1.2 copy.136
  14.2 1.0 fusion.67
  15.3 0.8 copy.137
  16.1 2.2 copy.138
  18.3 1.2 copy.132
  19.5 0.8 fusion.26
  20.4 7.2 %fusion.70 = (f32[4,5,128]{2,1,0:T(8,128)S(1)}, bf16[4,5,128,896]{2,3,1,0:T(8,128)(2,1)}) fusion(pred[128,896]{0,1:T(8,128)(4,1)S(1)} %fusion.26, bf16[128,4,5,128]{0,3,2,1:T(8,128)(2,1)} %bitcast.121, bf16[128,4,128]{2,0,1:T(8,128)(2,1)S(1)} %copy-done.3, bf16[768,4,128]{2,0,1:T(8,128)(2,1)S(1)} %copy-done.2), kind=kOutput, calls=%fused_computation.109 | convolution fusion | flops 602801024 | bytes 6285312 | tf_op jit(solution)/shard_map/sub | solution.py:109
  27.6 3.5 %fusion.13 = bf16[128,4,5,128]{0,3,2,1:T(8,128)(2,1)S(1)} fusion(bf16[4,5,128,896]{2,3,1,0:T(8,128)(2,1)} %get-tuple-element.53, bf16[128,4,128]{0,2,1:T(8,128)(2,1)S(1)} %bitcast.126, bf16[768,4,128]{0,2,1:T(8,128)(2,1)} %bitcast.120, f32[128,4,5]{0,2,1:T(8,128)S(1)} %bitcast.135), kind=kOutput, calls=%fused_computation.12 | convolution fusion | flops 589692928 | bytes 6170624 | tf_op jit(solution)/shard_map/kgrs,skh->rkgh/dot_general | solution.py:112
  31.1 1.1 copy.141
  32.3 1.9 gather_fusion
  34.5 0.9 fusion.66
  35.4 1.3 copy.142
  37.6 1.0 subtract_convert_fusion
  39.2 0.5 slice_reduce_fusion
  39.7 0.8 slice.76
  40.5 64.7 %all-gather.2 = bf16[16,11,2560]{2,1,0:T(8,128)(2,1)S(1)} all-gather(bf16[1,11,2560]{2,1,0:T(8,128)(2,1)S(1)} %maximum_bitcast_fusion.9), channel_id=2, replica_groups=mesh['seq'=16,'tp'=2] {'seq'}, dimensions={0}, use_global_device_ids=true | all-gather | bytes 957440 | tf_op jit(solution)/shard_map/all_gather | solution.py:144
  105.7 0.9 copy.169
  106.5 1.1 copy-done.1
  108.2 1.3 mul.107
  109.5 2.3 mul.108
  111.8 1.9 fusion.24
  113.8 0.9 fusion.49
  115.7 0.8 dynamic-slice_convert_fusion.1
  116.5 0.5 fusion.36
  117.1 47.7 %all-gather.3 = f32[32,20,320]{2,1,0:T(8,128)S(1)} all-gather(f32[1,20,320]{2,1,0:T(8,128)S(1)} %fusion.36), channel_id=3, replica_groups=mesh['seq'=16,'tp'=2] {'seq','tp'}, dimensions={0}, use_global_device_ids=true | all-gather | bytes 844800 | tf_op jit(solution)/shard_map/all_gather | solution.py:190
  165.4 19.8 %fusion.71 = (f32[20]{0:T(128)S(1)}, f32[20,4752]{1,0:T(8,128)S(1)}) fusion(bf16[5120,4752]{0,1:T(8,128)(2,1)} %param.27, f32[20,5120]{1,0:T(8,128)S(1)} %reshape.243, f32[5120]{0:T(1024)S(1)} %convert_element_type.132, f32[20]{0:T(128)S(1)} %add_rsqrt_fusion), kind=kOutput, calls=%fused_computation.110 | convolution fusion | flops 973611840 | bytes 49470880 | tf_op jit(solution)/shard_map/dot_general | solution.py:205
  185.4 0.4 collective-permute-start
  185.9 0.8 collective-permute-done
  186.7 2.1 collective-permute-start.1
  188.7 1.6 collective-permute-done.1
  190.3 3.6 %collective-permute-done.2 = f32[2,2,20,2]{2,3,1,0:T(2,128)S(1)} collective-permute-done((f32[2,2,20,2]{2,3,1,0:T(2,128)S(1)}, f32[2,2,20,2]{2,3,1,0:T(2,128)S(1)}, u32[]{:S(2)}, u32[]{:S(2)}) %collective-permute-start.2) | collective-permute-done | bytes 672 | tf_op jit(solution)/shard_map/ppermute | solution.py:27
  194.1 3.5 %collective-permute-done.3 = f32[4,2,20,2]{2,3,1,0:T(2,128)S(1)} collective-permute-done((f32[4,2,20,2]{2,3,1,0:T(2,128)S(1)}, f32[4,2,20,2]{2,3,1,0:T(2,128)S(1)}, u32[]{:S(2)}, u32[]{:S(2)}) %collective-permute-start.3) | collective-permute-done | bytes 1312 | tf_op jit(solution)/shard_map/ppermute | solution.py:27
  197.7 0.6 constant_dynamic-slice_fusion
  198.4 4.0 %collective-permute-done.4 = f32[8,2,20,2]{2,3,1,0:T(2,128)S(1)} collective-permute-done((f32[8,2,20,2]{2,3,1,0:T(2,128)S(1)}, f32[8,2,20,2]{2,3,1,0:T(2,128)S(1)}, u32[]{:S(2)}, u32[]{:S(2)}) %collective-permute-start.4) | collective-permute-done | bytes 2592 | tf_op jit(solution)/shard_map/ppermute | solution.py:27
  202.5 0.9 broadcast_subtract_fusion
  203.4 10.1 %fusion.73 = f32[2048,320]{1,0:T(8,128)} fusion(bf16[2048,2560]{1,0:T(8,128)(2,1)} %bitcast.134, bf16[2560,320]{0,1:T(8,128)(2,1)S(1)} %copy-done), kind=kOutput, calls=%fused_computation.112 | convolution fusion | flops 3355443200 | bytes 14745600 | tf_op jit(solution)/shard_map/reshape | solution.py:218
  213.5 9.2 %reduce-scatter.2.cloned.1.call-done = f32[16,64,320]{2,1,0:T(8,128)} async-done(((f32[16,128,320]{2,1,0:T(8,128)}), f32[16,64,320]{2,1,0:T(8,128)}) %reduce-scatter.2.cloned.1.call-update) | async-done | bytes 1310736 | tf_op jit(solution)/shard_map/reduce_scatter | solution.py:220
  222.7 6.9 %all-to-all-start = ((f32[16,64,320]{2,1,0:T(8,128)}), f32[16,64,320]{2,1,0:T(8,128)S(1)}, u32[]{:S(2)}, u32[]{:S(2)}) async-start(f32[16,64,320]{2,1,0:T(8,128)} %reduce-scatter.2.cloned.1.call-done), calls=%async_computation.1 | async-start | bytes 3145728 | tf_op jit(solution)/shard_map/all_to_all | solution.py:221
  229.6 2.2 copy.131
  231.7 32.1 %all-to-all-done = f32[16,64,320]{2,1,0:T(8,128)S(1)} async-done(((f32[16,64,320]{2,1,0:T(8,128)}), f32[16,64,320]{2,1,0:T(8,128)S(1)}, u32[]{:S(2)}, u32[]{:S(2)}) %all-to-all-start) | async-done | bytes 1310752 | tf_op jit(solution)/shard_map/all_to_all | solution.py:221
  263.8 5.0 %all_to_all.23 = f32[16,64,320]{2,1,0:T(8,128)S(1)} all-to-all(f32[16,64,320]{2,1,0:T(8,128)S(1)} %all-to-all-done), channel_id=1, replica_groups=mesh['seq'=16,'tp'=2] {'tp'}, dimensions={0} | all-to-all | bytes 2621440 | tf_op jit(solution)/shard_map/all_to_all | solution.py:222
  268.9 1.5 copy.153
  270.5 1.6 fusion.16
  272.1 1.1 copy.154
  (94 shorter events, 5.2 us)
Async XLA Ops:
  7.2 109.4 %copy-start = (bf16[2560,320]{0,1:T(8,128)(2,1)S(1)}, bf16[2560,320]{0,1:T(8,128)(2,1)}, u32[]{:S(2)}) copy-start(bf16[2560,320]{0,1:T(8,128)(2,1)} %param.25) | copy-start | bytes 4915204
  7.2 196.2 %all-gather.6.cloned.1.call-start = ((), (), s32[]{:S(2)}) async-start(), calls=%async_computation.3 | async-start | bytes 11141120 | tf_op jit(solution)/shard_map/all_gather | solution.py:145
  15.3 5.1 %copy-start.2 = (bf16[768,4,128]{2,0,1:T(8,128)(2,1)S(1)}, bf16[768,4,128]{2,0,1:T(8,128)(2,1)}, u32[]{:S(2)}) copy-start(bf16[768,4,128]{2,0,1:T(8,128)(2,1)} %copy.136) | copy-start | bytes 2359300
  16.1 4.3 %copy-start.3 = (bf16[128,4,128]{2,0,1:T(8,128)(2,1)S(1)}, bf16[128,4,128]{2,0,1:T(8,128)(2,1)}, u32[]{:S(2)}) copy-start(bf16[128,4,128]{2,0,1:T(8,128)(2,1)} %copy.137) | copy-start | bytes 393220
  31.1 1.2 copy-start.7
  32.2 190.4 %reduce-scatter.2.cloned.1.call-start = ((), (), s32[]{:S(2)}) async-start(), calls=%async_computation.4 | async-start | bytes 4718592 | tf_op jit(solution)/shard_map/reduce_scatter | solution.py:220
  34.5 2.3 copy-start.4
  34.5 2.3 copy-start.8
  106.5 1.1 copy-start.1
  109.5 5.3 %copy-start.6 = (bf16[2,4,512]{2,1,0:T(4,128)(2,1)S(1)}, bf16[2,4,512]{2,1,0:T(4,128)(2,1)}, u32[]{:S(2)}) copy-start(bf16[2,4,512]{2,1,0:T(4,128)(2,1)} %param.21) | copy-start | bytes 24580
  117.1 48.0 %copy-start.5 = (bf16[5120]{0:T(1024)(128)(2,1)S(1)}, bf16[5120]{0:T(1024)(128)(2,1)}, u32[]{:S(2)}) copy-start(bf16[5120]{0:T(1024)(128)(2,1)} %param.26) | copy-start | bytes 30724
  185.4 1.2 collective-permute-start
  186.7 3.6 %collective-permute-start.1 = (f32[1,2,20,2]{2,3,1,0:T(2,128)S(1)}, f32[1,2,20,2]{2,3,1,0:T(2,128)S(1)}, u32[]{:S(2)}, u32[]{:S(2)}) collective-permute-start(f32[1,2,20,2]{2,3,1,0:T(2,128)S(1)} %maximum_select_fusion.4), channel_id=1, source_target_pairs={{0,2},{2,0},{4,6},{6,4},{8,10},{10,8},{12,14},{14,12},{16,18},{18,... | collective-permute-start | bytes 968 | tf_op jit(solution)/shard_map/ppermute | solution.py:27
  190.3 3.6 %collective-permute-start.2 = (f32[2,2,20,2]{2,3,1,0:T(2,128)S(1)}, f32[2,2,20,2]{2,3,1,0:T(2,128)S(1)}, u32[]{:S(2)}, u32[]{:S(2)}) collective-permute-start(f32[2,2,20,2]{2,3,1,0:T(2,128)S(1)} %maximum_select_fusion.3), channel_id=1, source_target_pairs={{0,4},{2,6},{4,0},{6,2},{8,12},{10,14},{12,8},{14,10},{16,20},{18,... | collective-permute-start | bytes 1928 | tf_op jit(solution)/shard_map/ppermute | solution.py:27
  193.9 3.7 %collective-permute-start.3 = (f32[4,2,20,2]{2,3,1,0:T(2,128)S(1)}, f32[4,2,20,2]{2,3,1,0:T(2,128)S(1)}, u32[]{:S(2)}, u32[]{:S(2)}) collective-permute-start(f32[4,2,20,2]{2,3,1,0:T(2,128)S(1)} %maximum_select_fusion.2), channel_id=1, source_target_pairs={{0,8},{2,10},{4,12},{6,14},{8,0},{10,2},{12,4},{14,6},{16,24},{18,... | collective-permute-start | bytes 3848 | tf_op jit(solution)/shard_map/ppermute | solution.py:27
  197.7 4.7 %collective-permute-start.4 = (f32[8,2,20,2]{2,3,1,0:T(2,128)S(1)}, f32[8,2,20,2]{2,3,1,0:T(2,128)S(1)}, u32[]{:S(2)}, u32[]{:S(2)}) collective-permute-start(f32[8,2,20,2]{2,3,1,0:T(2,128)S(1)} %maximum_select_fusion.1), channel_id=1, source_target_pairs={{0,16},{2,18},{4,20},{6,22},{8,24},{10,26},{12,28},{14,30},{16,0},... | collective-permute-start | bytes 7688 | tf_op jit(solution)/shard_map/ppermute | solution.py:27
  222.7 41.1 %all-to-all-start = ((f32[16,64,320]{2,1,0:T(8,128)}), f32[16,64,320]{2,1,0:T(8,128)S(1)}, u32[]{:S(2)}, u32[]{:S(2)}) async-start(f32[16,64,320]{2,1,0:T(8,128)} %reduce-scatter.2.cloned.1.call-done), calls=%async_computation.1 | async-start | bytes 3145728 | tf_op jit(solution)/shard_map/all_to_all | solution.py:221
Sparse Core Ops, SparseCore 0:
  32.4 158.8 all-gather.5
  213.6 9.0 reduce-scatter.1

commit v7 on v6

--- a/solution.py
+++ b/solution.py
@@ -206,13 +206,13 @@
     local_max = jnp.max(logits, axis=-1)
     local_sum = jnp.sum(jnp.exp(logits - local_max[:, None]), axis=-1)
     local_stats = jnp.stack([local_max, local_sum], -1)
+    every_row, local_stats = lax.optimization_barrier((every_row, local_stats))
     stats = doubling_gather(doubling_gather(local_stats, "tp"), "seq").reshape(
         (n_seq * n_tp,) + local_stats.shape
     )
     global_max = jnp.max(stats[..., 0], axis=0)
     global_sum = jnp.sum(stats[..., 1] * jnp.exp(stats[..., 0] - global_max[None]), axis=0)
     log_probs = logits - (global_max + jnp.log(global_sum))[:, None]
-    every_row, decode_out, log_probs = lax.optimization_barrier((every_row, decode_out, log_probs))
 
     column_block = jnp.dot(every_row, out_weight, preferred_element_type=jnp.float32)
     prefill_block = column_block.reshape(n_seq, span_len, column_width)

time: 283 us -> 275 us (0.972)
  waiting for transfers between devices: 54.8 us -> 42.6 us
  starting transfers between devices: 9.6 us -> 14.4 us
    all_to_all x1, waiting for transfers between devices: 32.1 us -> 0.01 us  [local(): lax.all_to_all(summed_rows, 'seq', split_axis=0, concat_axis=0, tiled=True)]
    ppermute x5, waiting for transfers between devices: 13.5 us -> 29.5 us  [doubling_gather(): other = lax.ppermute(block, axis, pairs)]
    all_gather x1, waiting for transfers between devices: 0.01 us -> 5.04 us  [local(): lax.all_gather(prefill_attention, 'seq', axis=0)]
    ppermute x5, starting transfers between devices: 2.63 us -> 7.38 us  [doubling_gather(): other = lax.ppermute(block, axis, pairs)]
    unnamed x26 -> x28, local copies, waits for them, and re-layouts: 9.01 us -> 9.78 us
  transfers between devices with their start and end apart: 8 -> 8, of which waited for: 7 -> 6; matrix products, arithmetic and copies ran while one was open for 15% -> 16% of each run, Pallas kernels for 0% -> 0%
where the time goes in v7:
time: 275 us; the launch traced here: 274 us
  blocking collectives  117 us (43%)
  matrix products  42.6 us (15%)
  waiting for transfers between devices  42.6 us (15%)
  local copies, waits for them, and re-layouts  32.3 us (12%)
  between operations  14.6 us (5%)
  starting transfers between devices  14.4 us (5%)
  other arithmetic  10.5 us (4%)
    all_gather x1, blocking collectives, local(): small_gathered = lax.all_gather(small_rows, 'seq', axis=0)  64.7 us
    all_gather x1, blocking collectives, local(): head_all = lax.all_gather(head_part, ('seq', 'tp'), axis=0)  47.7 us
    ppermute x5, waiting for transfers between devices, doubling_gather(): other = lax.ppermute(block, axis, pairs)  29.5 us
    dot_general x1, matrix products, local(): logits = jnp.dot(normed, head_weight, preferred_element_type=jnp.float32)  19.8 us
    reshape x1, matrix products, local(): prefill_block = column_block.reshape(n_seq, span_len, column_width)  10.1 us
    unnamed x28, local copies, waits for them, and re-layouts  9.78 us
    reduce_scatter x1, waiting for transfers between devices, local(): lax.psum_scatter(prefill_block, 'tp', scatter_dimension=1, tiled=True)  8.08 us
    ppermute x5, starting transfers between devices, doubling_gather(): other = lax.ppermute(block, axis, pairs)  7.38 us
  transfers between devices with their start and end apart: 8, of which 6 were waited for; matrix products, arithmetic and copies ran while one was open for 16% of the time, Pallas kernels for 0%

profile of v7, /device:TPU:0, one launch (start us, length us, event | category | flops | bytes accessed | tf_op | source)
XLA Modules:
  0.0 274.4 jit_solution(11792758364974358723)
XLA Ops:
  7.2 1.4 dynamic_slice.14
  8.6 0.6 iota_compare_fusion.1
  9.3 2.4 fusion.61
  11.6 1.4 copy.165
  13.0 1.2 copy.136
  14.2 1.0 fusion.65
  15.3 0.8 copy.137
  16.1 2.2 copy.138
  18.3 1.2 copy.132
  19.5 0.8 fusion.26
  20.4 7.2 %fusion.68 = (f32[4,5,128]{2,1,0:T(8,128)S(1)}, bf16[4,5,128,896]{2,3,1,0:T(8,128)(2,1)}) fusion(pred[128,896]{0,1:T(8,128)(4,1)S(1)} %fusion.26, bf16[128,4,5,128]{0,3,2,1:T(8,128)(2,1)} %bitcast.119, bf16[128,4,128]{2,0,1:T(8,128)(2,1)S(1)} %copy-done.4, bf16[768,4,128]{2,0,1:T(8,128)(2,1)S(1)} %copy-done.3), kind=kOutput, calls=%fused_computation.107 | convolution fusion | flops 602801024 | bytes 6285312 | tf_op jit(solution)/shard_map/sub | solution.py:109
  27.6 3.5 %fusion.13 = bf16[128,4,5,128]{0,3,2,1:T(8,128)(2,1)S(1)} fusion(bf16[4,5,128,896]{2,3,1,0:T(8,128)(2,1)} %get-tuple-element.49, bf16[128,4,128]{0,2,1:T(8,128)(2,1)S(1)} %bitcast.124, bf16[768,4,128]{0,2,1:T(8,128)(2,1)} %bitcast.118, f32[128,4,5]{0,2,1:T(8,128)S(1)} %bitcast.135), kind=kOutput, calls=%fused_computation.12 | convolution fusion | flops 589692928 | bytes 6170624 | tf_op jit(solution)/shard_map/kgrs,skh->rkgh/dot_general | solution.py:112
  31.1 1.1 copy.141
  32.3 1.9 gather_fusion
  34.5 0.9 fusion.64
  35.4 1.3 copy.142
  37.6 1.0 subtract_convert_fusion
  39.7 0.8 slice.76
  40.5 64.7 %all-gather.2 = bf16[16,11,2560]{2,1,0:T(8,128)(2,1)S(1)} all-gather(bf16[1,11,2560]{2,1,0:T(8,128)(2,1)S(1)} %maximum_bitcast_fusion.9), channel_id=2, replica_groups=mesh['seq'=16,'tp'=2] {'seq'}, dimensions={0}, use_global_device_ids=true | all-gather | bytes 957440 | tf_op jit(solution)/shard_map/all_gather | solution.py:144
  105.7 0.9 copy.169
  106.5 1.1 copy-done.1
  108.2 1.3 mul.107
  109.5 2.3 mul.108
  111.8 1.9 fusion.24
  113.8 0.9 fusion.49
  115.7 0.8 dynamic-slice_convert_fusion.1
  116.5 0.5 fusion.36
  117.1 47.7 %all-gather.3 = f32[32,20,320]{2,1,0:T(8,128)S(1)} all-gather(f32[1,20,320]{2,1,0:T(8,128)S(1)} %fusion.36), channel_id=3, replica_groups=mesh['seq'=16,'tp'=2] {'seq','tp'}, dimensions={0}, use_global_device_ids=true | all-gather | bytes 844800 | tf_op jit(solution)/shard_map/all_gather | solution.py:190
  165.4 19.8 %fusion.69 = (f32[20]{0:T(128)S(1)}, f32[20,4752]{1,0:T(8,128)S(1)}) fusion(bf16[5120,4752]{0,1:T(8,128)(2,1)} %param.27, f32[20,5120]{1,0:T(8,128)S(1)} %reshape.243, f32[5120]{0:T(1024)S(1)} %convert_element_type.132, f32[20]{0:T(128)S(1)} %add_rsqrt_fusion), kind=kOutput, calls=%fused_computation.108 | convolution fusion | flops 973611840 | bytes 49470880 | tf_op jit(solution)/shard_map/dot_general | solution.py:205
  185.2 0.8 copy-done.2
  186.2 5.0 %all-gather.6.cloned.1.call-done = bf16[16,128,2560]{2,1,0:T(8,128)(2,1)} async-done(((bf16[1,128,2560]{2,1,0:T(8,128)(2,1)}), bf16[16,128,2560]{2,1,0:T(8,128)(2,1)}) %all-gather.6.cloned.1.call-update) | async-done | bytes 10485776 | tf_op jit(solution)/shard_map/all_gather | solution.py:145
  191.2 10.1 %fusion.71 = f32[2048,320]{1,0:T(8,128)} fusion(bf16[2048,2560]{1,0:T(8,128)(2,1)} %bitcast.134, bf16[2560,320]{0,1:T(8,128)(2,1)S(1)} %copy-done), kind=kOutput, calls=%fused_computation.110 | convolution fusion | flops 3355443200 | bytes 14745600 | tf_op jit(solution)/shard_map/reshape | solution.py:218
  201.4 1.1 collective-permute-done
  202.6 0.7 collective-permute-start.1
  203.2 8.1 %reduce-scatter.2.cloned.1.call-done = f32[16,64,320]{2,1,0:T(8,128)} async-done(((f32[16,128,320]{2,1,0:T(8,128)}), f32[16,64,320]{2,1,0:T(8,128)}) %reduce-scatter.2.cloned.1.call-update) | async-done | bytes 1310736 | tf_op jit(solution)/shard_map/reduce_scatter | solution.py:220
  211.3 6.9 %all-to-all-start = ((f32[16,64,320]{2,1,0:T(8,128)}), f32[16,64,320]{2,1,0:T(8,128)S(1)}, u32[]{:S(2)}, u32[]{:S(2)}) async-start(f32[16,64,320]{2,1,0:T(8,128)} %reduce-scatter.2.cloned.1.call-done), calls=%async_computation.1 | async-start | bytes 3145728 | tf_op jit(solution)/shard_map/all_to_all | solution.py:221
  218.3 2.0 collective-permute-start.2
  220.3 7.3 %collective-permute-done.2 = f32[2,2,20,2]{2,3,1,0:T(2,128)S(1)} collective-permute-done((f32[2,2,20,2]{2,3,1,0:T(2,128)S(1)}, f32[2,2,20,2]{2,3,1,0:T(2,128)S(1)}, u32[]{:S(2)}, u32[]{:S(2)}) %collective-permute-start.2) | collective-permute-done | bytes 672 | tf_op jit(solution)/shard_map/ppermute | solution.py:27
  227.8 16.4 %collective-permute-done.3 = f32[4,2,20,2]{2,3,1,0:T(2,128)S(1)} collective-permute-done((f32[4,2,20,2]{2,3,1,0:T(2,128)S(1)}, f32[4,2,20,2]{2,3,1,0:T(2,128)S(1)}, u32[]{:S(2)}, u32[]{:S(2)}) %collective-permute-start.3) | collective-permute-done | bytes 1312 | tf_op jit(solution)/shard_map/ppermute | solution.py:27
  244.2 4.6 %collective-permute-start.4 = (f32[8,2,20,2]{2,3,1,0:T(2,128)S(1)}, f32[8,2,20,2]{2,3,1,0:T(2,128)S(1)}, u32[]{:S(2)}, u32[]{:S(2)}) collective-permute-start(f32[8,2,20,2]{2,3,1,0:T(2,128)S(1)} %maximum_select_fusion.1), channel_id=1, source_target_pairs={{0,16},{2,18},{4,20},{6,22},{8,24},{10,26},{12,28},{14,30},{16,0},... | collective-permute-start | bytes 7688 | tf_op jit(solution)/shard_map/ppermute | solution.py:27
  248.9 0.6 constant_dynamic-slice_fusion
  249.5 2.2 copy.131
  251.6 4.6 %collective-permute-done.4 = f32[8,2,20,2]{2,3,1,0:T(2,128)S(1)} collective-permute-done((f32[8,2,20,2]{2,3,1,0:T(2,128)S(1)}, f32[8,2,20,2]{2,3,1,0:T(2,128)S(1)}, u32[]{:S(2)}, u32[]{:S(2)}) %collective-permute-start.4) | collective-permute-done | bytes 2592 | tf_op jit(solution)/shard_map/ppermute | solution.py:27
  256.3 1.9 broadcast_subtract_fusion
  258.2 5.0 %all_to_all.23 = f32[16,64,320]{2,1,0:T(8,128)S(1)} all-to-all(f32[16,64,320]{2,1,0:T(8,128)S(1)} %all-to-all-done), channel_id=1, replica_groups=mesh['seq'=16,'tp'=2] {'tp'}, dimensions={0} | all-to-all | bytes 2621440 | tf_op jit(solution)/shard_map/all_to_all | solution.py:222
  263.4 1.5 copy.152
  264.9 1.6 fusion.16
  266.5 1.1 copy.154
  (96 shorter events, 5.7 us)
Async XLA Ops:
  7.2 109.4 %copy-start = (bf16[2560,320]{0,1:T(8,128)(2,1)S(1)}, bf16[2560,320]{0,1:T(8,128)(2,1)}, u32[]{:S(2)}) copy-start(bf16[2560,320]{0,1:T(8,128)(2,1)} %param.25) | copy-start | bytes 4915204
  7.2 184.1 %all-gather.6.cloned.1.call-start = ((), (), s32[]{:S(2)}) async-start(), calls=%async_computation.3 | async-start | bytes 11141120 | tf_op jit(solution)/shard_map/all_gather | solution.py:145
  15.3 5.1 %copy-start.3 = (bf16[768,4,128]{2,0,1:T(8,128)(2,1)S(1)}, bf16[768,4,128]{2,0,1:T(8,128)(2,1)}, u32[]{:S(2)}) copy-start(bf16[768,4,128]{2,0,1:T(8,128)(2,1)} %copy.136) | copy-start | bytes 2359300
  16.1 4.3 %copy-start.4 = (bf16[128,4,128]{2,0,1:T(8,128)(2,1)S(1)}, bf16[128,4,128]{2,0,1:T(8,128)(2,1)}, u32[]{:S(2)}) copy-start(bf16[128,4,128]{2,0,1:T(8,128)(2,1)} %copy.137) | copy-start | bytes 393220
  31.1 1.2 copy-start.8
  32.2 179.1 %reduce-scatter.2.cloned.1.call-start = ((), (), s32[]{:S(2)}) async-start(), calls=%async_computation.4 | async-start | bytes 4718592 | tf_op jit(solution)/shard_map/reduce_scatter | solution.py:220
  34.5 2.3 copy-start.5
  34.5 2.3 copy-start.9
  106.5 1.1 copy-start.1
  109.5 5.3 %copy-start.7 = (bf16[2,4,512]{2,1,0:T(4,128)(2,1)S(1)}, bf16[2,4,512]{2,1,0:T(4,128)(2,1)}, u32[]{:S(2)}) copy-start(bf16[2,4,512]{2,1,0:T(4,128)(2,1)} %param.21) | copy-start | bytes 24580
  117.1 48.0 %copy-start.6 = (bf16[5120]{0:T(1024)(128)(2,1)S(1)}, bf16[5120]{0:T(1024)(128)(2,1)}, u32[]{:S(2)}) copy-start(bf16[5120]{0:T(1024)(128)(2,1)} %param.26) | copy-start | bytes 30724
  185.2 0.8 copy-start.2
  201.4 1.2 collective-permute-start
  202.6 15.7 %collective-permute-start.1 = (f32[1,2,20,2]{2,3,1,0:T(2,128)S(1)}, f32[1,2,20,2]{2,3,1,0:T(2,128)S(1)}, u32[]{:S(2)}, u32[]{:S(2)}) collective-permute-start(f32[1,2,20,2]{2,3,1,0:T(2,128)S(1)} %maximum_select_fusion.4), channel_id=1, source_target_pairs={{0,2},{2,0},{4,6},{6,4},{8,10},{10,8},{12,14},{14,12},{16,18},{18,... | collective-permute-start | bytes 968 | tf_op jit(solution)/shard_map/ppermute | solution.py:27
  211.3 46.9 %all-to-all-start = ((f32[16,64,320]{2,1,0:T(8,128)}), f32[16,64,320]{2,1,0:T(8,128)S(1)}, u32[]{:S(2)}, u32[]{:S(2)}) async-start(f32[16,64,320]{2,1,0:T(8,128)} %reduce-scatter.2.cloned.1.call-done), calls=%async_computation.1 | async-start | bytes 3145728 | tf_op jit(solution)/shard_map/all_to_all | solution.py:221
  218.3 9.3 %collective-permute-start.2 = (f32[2,2,20,2]{2,3,1,0:T(2,128)S(1)}, f32[2,2,20,2]{2,3,1,0:T(2,128)S(1)}, u32[]{:S(2)}, u32[]{:S(2)}) collective-permute-start(f32[2,2,20,2]{2,3,1,0:T(2,128)S(1)} %maximum_select_fusion.3), channel_id=1, source_target_pairs={{0,4},{2,6},{4,0},{6,2},{8,12},{10,14},{12,8},{14,10},{16,20},{18,... | collective-permute-start | bytes 1928 | tf_op jit(solution)/shard_map/ppermute | solution.py:27
  227.6 16.6 %collective-permute-start.3 = (f32[4,2,20,2]{2,3,1,0:T(2,128)S(1)}, f32[4,2,20,2]{2,3,1,0:T(2,128)S(1)}, u32[]{:S(2)}, u32[]{:S(2)}) collective-permute-start(f32[4,2,20,2]{2,3,1,0:T(2,128)S(1)} %maximum_select_fusion.2), channel_id=1, source_target_pairs={{0,8},{2,10},{4,12},{6,14},{8,0},{10,2},{12,4},{14,6},{16,24},{18,... | collective-permute-start | bytes 3848 | tf_op jit(solution)/shard_map/ppermute | solution.py:27
  244.2 12.0 %collective-permute-start.4 = (f32[8,2,20,2]{2,3,1,0:T(2,128)S(1)}, f32[8,2,20,2]{2,3,1,0:T(2,128)S(1)}, u32[]{:S(2)}, u32[]{:S(2)}) collective-permute-start(f32[8,2,20,2]{2,3,1,0:T(2,128)S(1)} %maximum_select_fusion.1), channel_id=1, source_target_pairs={{0,16},{2,18},{4,20},{6,22},{8,24},{10,26},{12,28},{14,30},{16,0},... | collective-permute-start | bytes 7688 | tf_op jit(solution)/shard_map/ppermute | solution.py:27
Sparse Core Ops, SparseCore 0:
  32.4 158.8 all-gather.5
  201.5 9.7 reduce-scatter.1

commit v8 on v5

--- a/solution.py
+++ b/solution.py
@@ -21,16 +21,21 @@
         return lax.all_gather(value, axis, axis=0)
     index = lax.axis_index(axis)
     block = value[None]
-    distance = 1
-    while distance < count:
+    steps = 0
+    distance = count // 2
+    while distance >= 1:
         pairs = [(i, i ^ distance) for i in range(count)]
         other = lax.ppermute(block, axis, pairs)
         low = (index & distance) == 0
         block = jnp.where(
             low, jnp.concatenate([block, other], 0), jnp.concatenate([other, block], 0)
         )
-        distance *= 2
-    return block
+        steps += 1
+        distance //= 2
+    rest = value.shape
+    block = block.reshape((2,) * steps + rest)
+    order = tuple(range(steps - 1, -1, -1)) + tuple(range(steps, steps + len(rest)))
+    return jnp.transpose(block, order).reshape((count,) + rest)
 
 
 def local(
@@ -206,13 +211,13 @@
     local_max = jnp.max(logits, axis=-1)
     local_sum = jnp.sum(jnp.exp(logits - local_max[:, None]), axis=-1)
     local_stats = jnp.stack([local_max, local_sum], -1)
+    every_row, local_stats = lax.optimization_barrier((every_row, local_stats))
     stats = doubling_gather(doubling_gather(local_stats, "tp"), "seq").reshape(
         (n_seq * n_tp,) + local_stats.shape
     )
     global_max = jnp.max(stats[..., 0], axis=0)
     global_sum = jnp.sum(stats[..., 1] * jnp.exp(stats[..., 0] - global_max[None]), axis=0)
     log_probs = logits - (global_max + jnp.log(global_sum))[:, None]
-    every_row, decode_out, log_probs = lax.optimization_barrier((every_row, decode_out, log_probs))
 
     column_block = jnp.dot(every_row, out_weight, preferred_element_type=jnp.float32)
     prefill_block = column_block.reshape(n_seq, span_len, column_width)

time: 330 us -> 288 us (0.87)
  waiting for transfers between devices: 198 us -> 152 us
  starting transfers between devices: 22.8 us -> 28.8 us
    all_to_all x1, waiting for transfers between devices: 32.1 us -> 0.01 us  [local(): lax.all_to_all(summed_rows, 'seq', split_axis=0, concat_axis=0, tiled=True)]
    ppermute x14, waiting for transfers between devices: 156 us -> 142 us  [doubling_gather(): other = lax.ppermute(block, axis, pairs)]
    ppermute x14, starting transfers between devices: 15.9 us -> 21.8 us  [doubling_gather(): other = lax.ppermute(block, axis, pairs)]
    unnamed x26 -> x23, local copies, waits for them, and re-layouts: 9.89 us -> 8.72 us
  transfers between devices with their start and end apart: 17 -> 17, of which waited for: 16 -> 14; matrix products, arithmetic and copies ran while one was open for 14% -> 16% of each run, Pallas kernels for 0% -> 0%
where the time goes in v8:
time: 288 us; the launch traced here: 287 us
  waiting for transfers between devices  152 us (53%)
  matrix products  42.6 us (15%)
  local copies, waits for them, and re-layouts  34 us (12%)
  starting transfers between devices  28.8 us (10%)
  between operations  14.7 us (5%)
  other arithmetic  9.9 us (3%)
  blocking collectives  4.99 us (2%)
    ppermute x14, waiting for transfers between devices, doubling_gather(): other = lax.ppermute(block, axis, pairs)  142 us
    ppermute x14, starting transfers between devices, doubling_gather(): other = lax.ppermute(block, axis, pairs)  21.8 us
    dot_general x1, matrix products, local(): logits = jnp.dot(normed, head_weight, preferred_element_type=jnp.float32)  19.8 us
    reshape x1, matrix products, local(): prefill_block = column_block.reshape(n_seq, span_len, column_width)  10.1 us
    reduce_scatter x1, waiting for transfers between devices, local(): lax.psum_scatter(prefill_block, 'tp', scatter_dimension=1, tiled=True)  9.32 us
    unnamed x23, local copies, waits for them, and re-layouts  8.72 us
    sub x1, matrix products, local(): weights = jnp.where(live_mask, jnp.exp(masked - row_max), 0.0)  7.24 us
    all_to_all x1, starting transfers between devices, local(): lax.all_to_all(summed_rows, 'seq', split_axis=0, concat_axis=0, tiled=True)  6.89 us
  transfers between devices with their start and end apart: 17, of which 14 were waited for; matrix products, arithmetic and copies ran while one was open for 16% of the time, Pallas kernels for 0%

profile of v8, /device:TPU:0, one launch (start us, length us, event | category | flops | bytes accessed | tf_op | source)
XLA Modules:
  0.0 286.8 jit_solution(13312766408111721123)
XLA Ops:
  7.2 1.4 dynamic_slice.14
  9.3 2.4 fusion.61
  11.6 1.4 copy.179
  13.0 1.2 copy.137
  14.2 1.0 fusion.65
  15.4 2.2 copy.139
  17.7 1.2 copy.133
  19.8 7.2 %fusion.67 = (f32[4,5,128]{2,1,0:T(8,128)S(1)}, bf16[4,5,128,896]{2,3,1,0:T(8,128)(2,1)}) fusion(pred[128,896]{0,1:T(8,128)(4,1)S(1)} %fusion.27, bf16[128,4,5,128]{0,3,2,1:T(8,128)(2,1)} %bitcast.140, bf16[128,4,128]{2,0,1:T(8,128)(2,1)S(1)} %copy.138, bf16[768,4,128]{2,0,1:T(8,128)(2,1)S(1)} %copy-done.3), kind=kOutput, calls=%fused_computation.119 | convolution fusion | flops 602801024 | bytes 6285312 | tf_op jit(solution)/shard_map/sub | solution.py:114
  27.0 3.5 %fusion.13 = bf16[128,4,5,128]{0,3,2,1:T(8,128)(2,1)S(1)} fusion(bf16[4,5,128,896]{2,3,1,0:T(8,128)(2,1)} %get-tuple-element.44, bf16[128,4,128]{0,2,1:T(8,128)(2,1)S(1)} %bitcast.146, bf16[768,4,128]{0,2,1:T(8,128)(2,1)} %bitcast.139, f32[128,4,5]{0,2,1:T(8,128)S(1)} %bitcast.156), kind=kOutput, calls=%fused_computation.13 | convolution fusion | flops 589692928 | bytes 6170624 | tf_op jit(solution)/shard_map/kgrs,skh->rkgh/dot_general | solution.py:117
  30.5 1.1 copy.142
  31.7 1.9 gather_fusion
  34.8 1.3 copy.143
  37.0 1.0 subtract_convert_fusion
  40.1 4.1 %collective-permute-start = (bf16[1,11,2560]{2,1,0:T(8,128)(2,1)S(1)}, bf16[1,11,2560]{2,1,0:T(8,128)(2,1)S(1)}, u32[]{:S(2)}, u32[]{:S(2)}) collective-permute-start(bf16[1,11,2560]{2,1,0:T(8,128)(2,1)S(1)} %maximum_bitcast_fusion.9), channel_id=1, source_target_pairs={{0,16},{2,18},{4,20},{6,22},{8,24},{10,26},{12,28},{14,30},{16,0},... | collective-permute-start | bytes 168968 | tf_op jit(solution)/shard_map/ppermute | solution.py:28
  44.3 6.6 %collective-permute-done = bf16[1,11,2560]{2,1,0:T(8,128)(2,1)S(1)} collective-permute-done((bf16[1,11,2560]{2,1,0:T(8,128)(2,1)S(1)}, bf16[1,11,2560]{2,1,0:T(8,128)(2,1)S(1)}, u32[]{:S(2)}, u32[]{:S(2)}) %collective-permute-start) | collective-permute-done | bytes 56352 | tf_op jit(solution)/shard_map/ppermute | solution.py:28
  50.9 3.5 %collective-permute-start.1 = (bf16[2,11,2560]{2,1,0:T(8,128)(2,1)S(1)}, bf16[2,11,2560]{2,1,0:T(8,128)(2,1)S(1)}, u32[]{:S(2)}, u32[]{:S(2)}) collective-permute-start(bf16[2,11,2560]{2,1,0:T(8,128)(2,1)S(1)} %maximum_select_fusion.6), channel_id=1, source_target_pairs={{0,8},{2,10},{4,12},{6,14},{8,0},{10,2},{12,4},{14,6},{16,24},{18,... | collective-permute-start | bytes 337928 | tf_op jit(solution)/shard_map/ppermute | solution.py:28
  54.3 10.5 %collective-permute-done.1 = bf16[2,11,2560]{2,1,0:T(8,128)(2,1)S(1)} collective-permute-done((bf16[2,11,2560]{2,1,0:T(8,128)(2,1)S(1)}, bf16[2,11,2560]{2,1,0:T(8,128)(2,1)S(1)}, u32[]{:S(2)}, u32[]{:S(2)}) %collective-permute-start.1) | collective-permute-done | bytes 112672 | tf_op jit(solution)/shard_map/ppermute | solution.py:28
  64.9 1.8 collective-permute-start.2
  66.7 9.5 %collective-permute-done.2 = bf16[4,11,2560]{2,1,0:T(8,128)(2,1)S(1)} collective-permute-done((bf16[4,11,2560]{2,1,0:T(8,128)(2,1)S(1)}, bf16[4,11,2560]{2,1,0:T(8,128)(2,1)S(1)}, u32[]{:S(2)}, u32[]{:S(2)}) %collective-permute-start.2) | collective-permute-done | bytes 225312 | tf_op jit(solution)/shard_map/ppermute | solution.py:28
  76.7 1.7 collective-permute-start.3
  79.4 19.0 %collective-permute-done.3 = bf16[8,11,2560]{2,0,1:T(8,128)(2,1)S(1)} collective-permute-done((bf16[8,11,2560]{2,0,1:T(8,128)(2,1)S(1)}, bf16[8,11,2560]{2,0,1:T(8,128)(2,1)S(1)}, u32[]{:S(2)}, u32[]{:S(2)}) %collective-permute-start.3) | collective-permute-done | bytes 450592 | tf_op jit(solution)/shard_map/ppermute | solution.py:28
  98.9 1.0 copy.185
  101.9 1.3 mul.107
  103.3 2.3 mul.108
  105.6 1.5 fusion.25
  109.4 1.2 collective-permute-done.4
  110.6 1.4 collective-permute-start.5
  112.0 6.7 %collective-permute-done.5 = f32[1,2,20,320]{3,2,1,0:T(8,128)S(1)} collective-permute-done((f32[1,2,20,320]{3,2,1,0:T(8,128)S(1)}, f32[1,2,20,320]{3,2,1,0:T(8,128)S(1)}, u32[]{:S(2)}, u32[]{:S(2)}) %collective-permute-start.5) | collective-permute-done | bytes 51232 | tf_op jit(solution)/shard_map/ppermute | solution.py:28
  118.8 14.4 %collective-permute-done.6 = f32[2,2,20,320]{3,2,1,0:T(8,128)S(1)} collective-permute-done((f32[2,2,20,320]{3,2,1,0:T(8,128)S(1)}, f32[2,2,20,320]{3,2,1,0:T(8,128)S(1)}, u32[]{:S(2)}, u32[]{:S(2)}) %collective-permute-start.6) | collective-permute-done | bytes 102432 | tf_op jit(solution)/shard_map/ppermute | solution.py:28
  133.2 2.6 collective-permute-start.7
  135.8 12.7 %collective-permute-done.7 = f32[4,2,20,320]{3,2,1,0:T(8,128)S(1)} collective-permute-done((f32[4,2,20,320]{3,2,1,0:T(8,128)S(1)}, f32[4,2,20,320]{3,2,1,0:T(8,128)S(1)}, u32[]{:S(2)}, u32[]{:S(2)}) %collective-permute-start.7) | collective-permute-done | bytes 204832 | tf_op jit(solution)/shard_map/ppermute | solution.py:28
  148.8 20.9 %collective-permute-done.8 = f32[8,2,20,320]{3,0,2,1:T(8,128)S(1)} collective-permute-done((f32[8,2,20,320]{3,0,2,1:T(8,128)S(1)}, f32[8,2,20,320]{3,0,2,1:T(8,128)S(1)}, u32[]{:S(2)}, u32[]{:S(2)}) %collective-permute-start.8) | collective-permute-done | bytes 409632 | tf_op jit(solution)/shard_map/ppermute | solution.py:28
  171.0 19.8 %fusion.68 = (f32[20]{0:T(128)S(1)}, f32[20,4752]{1,0:T(8,128)S(1)}) fusion(bf16[5120,4752]{0,1:T(8,128)(2,1)} %param.27, f32[20,5120]{1,0:T(8,128)S(1)} %reshape.316, f32[5120]{0:T(1024)S(1)} %convert_element_type.143, f32[20]{0:T(128)S(1)} %add_rsqrt_fusion), kind=kOutput, calls=%fused_computation.120 | convolution fusion | flops 973611840 | bytes 49470880 | tf_op jit(solution)/shard_map/dot_general | solution.py:210
  192.5 10.1 %fusion.70 = f32[2048,320]{1,0:T(8,128)} fusion(bf16[2048,2560]{1,0:T(8,128)(2,1)} %bitcast.155, bf16[2560,320]{0,1:T(8,128)(2,1)S(1)} %copy-done), kind=kOutput, calls=%fused_computation.122 | convolution fusion | flops 3355443200 | bytes 14745600 | tf_op jit(solution)/shard_map/reshape | solution.py:223
  202.7 9.3 %reduce-scatter.2.cloned.1.call-done = f32[16,64,320]{2,1,0:T(8,128)} async-done(((f32[16,128,320]{2,1,0:T(8,128)}), f32[16,64,320]{2,1,0:T(8,128)}) %reduce-scatter.2.cloned.1.call-update) | async-done | bytes 1310736 | tf_op jit(solution)/shard_map/reduce_scatter | solution.py:225
  212.0 6.9 %all-to-all-start = ((f32[16,64,320]{2,1,0:T(8,128)}), f32[16,64,320]{2,1,0:T(8,128)S(1)}, u32[]{:S(2)}, u32[]{:S(2)}) async-start(f32[16,64,320]{2,1,0:T(8,128)} %reduce-scatter.2.cloned.1.call-done), calls=%async_computation.1 | async-start | bytes 3145728 | tf_op jit(solution)/shard_map/all_to_all | solution.py:226
  218.9 2.9 %collective-permute-start.10 = (f32[1,2,20,2]{2,3,1,0:T(2,128)S(1)}, f32[1,2,20,2]{2,3,1,0:T(2,128)S(1)}, u32[]{:S(2)}, u32[]{:S(2)}) collective-permute-start(f32[1,2,20,2]{2,3,1,0:T(2,128)S(1)} %maximum_select_fusion.13), channel_id=1, source_target_pairs={{0,16},{2,18},{4,20},{6,22},{8,24},{10,26},{12,28},{14,30},{16,0},... | collective-permute-start | bytes 968 | tf_op jit(solution)/shard_map/ppermute | solution.py:28
  221.8 34.5 %collective-permute-done.10 = f32[1,2,20,2]{2,3,1,0:T(2,128)S(1)} collective-permute-done((f32[1,2,20,2]{2,3,1,0:T(2,128)S(1)}, f32[1,2,20,2]{2,3,1,0:T(2,128)S(1)}, u32[]{:S(2)}, u32[]{:S(2)}) %collective-permute-start.10) | collective-permute-done | bytes 352 | tf_op jit(solution)/shard_map/ppermute | solution.py:28
  256.3 3.6 %collective-permute-done.11 = f32[2,2,20,2]{2,3,1,0:T(2,128)S(1)} collective-permute-done((f32[2,2,20,2]{2,3,1,0:T(2,128)S(1)}, f32[2,2,20,2]{2,3,1,0:T(2,128)S(1)}, u32[]{:S(2)}, u32[]{:S(2)}) %collective-permute-start.11) | collective-permute-done | bytes 672 | tf_op jit(solution)/shard_map/ppermute | solution.py:28
  259.9 2.6 collective-permute-start.12
  262.5 2.2 copy.132
  264.8 1.0 collective-permute-start.13
  266.4 2.2 collective-permute-done.13
  268.7 1.9 broadcast_subtract_fusion
  270.6 5.0 %all_to_all.23 = f32[16,64,320]{2,1,0:T(8,128)S(1)} all-to-all(f32[16,64,320]{2,1,0:T(8,128)S(1)} %all-to-all-done), channel_id=1, replica_groups=mesh['seq'=16,'tp'=2] {'tp'}, dimensions={0} | all-to-all | bytes 2621440 | tf_op jit(solution)/shard_map/all_to_all | solution.py:227
  275.8 1.5 copy.162
  277.3 1.6 fusion.16
  278.9 1.1 copy.166
  (126 shorter events, 16.7 us)
Async XLA Ops:
  7.2 101.6 %copy-start = (bf16[2560,320]{0,1:T(8,128)(2,1)S(1)}, bf16[2560,320]{0,1:T(8,128)(2,1)}, u32[]{:S(2)}) copy-start(bf16[2560,320]{0,1:T(8,128)(2,1)} %param.25) | copy-start | bytes 4915204
  7.2 185.3 %all-gather.2.cloned.1.call-start = ((), (), s32[]{:S(2)}) async-start(), calls=%async_computation.3 | async-start | bytes 11141120 | tf_op jit(solution)/shard_map/all_gather | solution.py:150
  15.4 4.3 %copy-start.3 = (bf16[768,4,128]{2,0,1:T(8,128)(2,1)S(1)}, bf16[768,4,128]{2,0,1:T(8,128)(2,1)}, u32[]{:S(2)}) copy-start(bf16[768,4,128]{2,0,1:T(8,128)(2,1)} %copy.137) | copy-start | bytes 2359300
  30.5 1.2 copy-start.7
  31.7 180.4 %reduce-scatter.2.cloned.1.call-start = ((), (), s32[]{:S(2)}) async-start(), calls=%async_computation.4 | async-start | bytes 4718592 | tf_op jit(solution)/shard_map/reduce_scatter | solution.py:225
  33.9 2.3 copy-start.4
  33.9 2.3 copy-start.8
  40.1 10.7 %collective-permute-start = (bf16[1,11,2560]{2,1,0:T(8,128)(2,1)S(1)}, bf16[1,11,2560]{2,1,0:T(8,128)(2,1)S(1)}, u32[]{:S(2)}, u32[]{:S(2)}) collective-permute-start(bf16[1,11,2560]{2,1,0:T(8,128)(2,1)S(1)} %maximum_bitcast_fusion.9), channel_id=1, source_target_pairs={{0,16},{2,18},{4,20},{6,22},{8,24},{10,26},{12,28},{14,30},{16,0},... | collective-permute-start | bytes 168968 | tf_op jit(solution)/shard_map/ppermute | solution.py:28
  44.3 34.2 %copy-start.6 = (bf16[2,4,512]{2,1,0:T(4,128)(2,1)S(1)}, bf16[2,4,512]{2,1,0:T(4,128)(2,1)}, u32[]{:S(2)}) copy-start(bf16[2,4,512]{2,1,0:T(4,128)(2,1)} %param.21) | copy-start | bytes 24580
  50.9 14.0 %collective-permute-start.1 = (bf16[2,11,2560]{2,1,0:T(8,128)(2,1)S(1)}, bf16[2,11,2560]{2,1,0:T(8,128)(2,1)S(1)}, u32[]{:S(2)}, u32[]{:S(2)}) collective-permute-start(bf16[2,11,2560]{2,1,0:T(8,128)(2,1)S(1)} %maximum_select_fusion.6), channel_id=1, source_target_pairs={{0,8},{2,10},{4,12},{6,14},{8,0},{10,2},{12,4},{14,6},{16,24},{18,... | collective-permute-start | bytes 337928 | tf_op jit(solution)/shard_map/ppermute | solution.py:28
  64.9 11.3 %collective-permute-start.2 = (bf16[4,11,2560]{2,1,0:T(8,128)(2,1)S(1)}, bf16[4,11,2560]{2,1,0:T(8,128)(2,1)S(1)}, u32[]{:S(2)}, u32[]{:S(2)}) collective-permute-start(bf16[4,11,2560]{2,1,0:T(8,128)(2,1)S(1)} %maximum_select_fusion.4), channel_id=1, source_target_pairs={{0,4},{2,6},{4,0},{6,2},{8,12},{10,14},{12,8},{14,10},{16,20},{18,... | collective-permute-start | bytes 675848 | tf_op jit(solution)/shard_map/ppermute | solution.py:28
  76.7 21.7 %collective-permute-start.3 = (bf16[8,11,2560]{2,0,1:T(8,128)(2,1)S(1)}, bf16[8,11,2560]{2,0,1:T(8,128)(2,1)S(1)}, u32[]{:S(2)}, u32[]{:S(2)}) collective-permute-start(bf16[8,11,2560]{2,0,1:T(8,128)(2,1)S(1)} %copy.147), channel_id=1, source_target_pairs={{0,2},{2,0},{4,6},{6,4},{8,10},{10,8},{12,14},{14,12},{16,18},{18,... | collective-permute-start | bytes 1351688 | tf_op jit(solution)/shard_map/ppermute | solution.py:28
  100.3 0.9 copy-start.2
  109.3 1.3 collective-permute-start.4
  110.6 38.2 %copy-start.5 = (bf16[5120]{0:T(1024)(128)(2,1)S(1)}, bf16[5120]{0:T(1024)(128)(2,1)}, u32[]{:S(2)}) copy-start(bf16[5120]{0:T(1024)(128)(2,1)} %param.26) | copy-start | bytes 30724
  110.6 8.1 %collective-permute-start.5 = (f32[1,2,20,320]{3,2,1,0:T(8,128)S(1)}, f32[1,2,20,320]{3,2,1,0:T(8,128)S(1)}, u32[]{:S(2)}, u32[]{:S(2)}) collective-permute-start(f32[1,2,20,320]{3,2,1,0:T(8,128)S(1)} %maximum_select_fusion.8), channel_id=1, source_target_pairs={{0,16},{2,18},{4,20},{6,22},{8,24},{10,26},{12,28},{14,30},{16,0},... | collective-permute-start | bytes 153608 | tf_op jit(solution)/shard_map/ppermute | solution.py:28
  118.7 14.4 %collective-permute-start.6 = (f32[2,2,20,320]{3,2,1,0:T(8,128)S(1)}, f32[2,2,20,320]{3,2,1,0:T(8,128)S(1)}, u32[]{:S(2)}, u32[]{:S(2)}) collective-permute-start(f32[2,2,20,320]{3,2,1,0:T(8,128)S(1)} %maximum_select_fusion.7), channel_id=1, source_target_pairs={{0,8},{2,10},{4,12},{6,14},{8,0},{10,2},{12,4},{14,6},{16,24},{18,... | collective-permute-start | bytes 307208 | tf_op jit(solution)/shard_map/ppermute | solution.py:28
  133.2 15.3 %collective-permute-start.7 = (f32[4,2,20,320]{3,2,1,0:T(8,128)S(1)}, f32[4,2,20,320]{3,2,1,0:T(8,128)S(1)}, u32[]{:S(2)}, u32[]{:S(2)}) collective-permute-start(f32[4,2,20,320]{3,2,1,0:T(8,128)S(1)} %maximum_select_fusion.5), channel_id=1, source_target_pairs={{0,4},{2,6},{4,0},{6,2},{8,12},{10,14},{12,8},{14,10},{16,20},{18,... | collective-permute-start | bytes 614408 | tf_op jit(solution)/shard_map/ppermute | solution.py:28
  148.7 21.0 %collective-permute-start.8 = (f32[8,2,20,320]{3,0,2,1:T(8,128)S(1)}, f32[8,2,20,320]{3,0,2,1:T(8,128)S(1)}, u32[]{:S(2)}, u32[]{:S(2)}) collective-permute-start(f32[8,2,20,320]{3,0,2,1:T(8,128)S(1)} %copy.155), channel_id=1, source_target_pairs={{0,2},{2,0},{4,6},{6,4},{8,10},{10,8},{12,14},{14,12},{16,18},{18,... | collective-permute-start | bytes 1228808 | tf_op jit(solution)/shard_map/ppermute | solution.py:28
  190.7 0.8 copy-start.1
  202.6 16.3 %collective-permute-start.9 = (f32[1,20,2]{1,2,0:T(2,128)S(1)}, f32[1,20,2]{1,2,0:T(2,128)S(1)}, u32[]{:S(2)}, u32[]{:S(2)}) collective-permute-start(f32[1,20,2]{1,2,0:T(2,128)S(1)} %bitcast.151), channel_id=1, source_target_pairs={{0,1},{1,0},{2,3},{3,2},{4,5},{5,4},{6,7},{7,6},{8,9},{9,8},{10,11... | collective-permute-start | bytes 488 | tf_op jit(solution)/shard_map/ppermute | solution.py:28
  212.0 58.6 %all-to-all-start = ((f32[16,64,320]{2,1,0:T(8,128)}), f32[16,64,320]{2,1,0:T(8,128)S(1)}, u32[]{:S(2)}, u32[]{:S(2)}) async-start(f32[16,64,320]{2,1,0:T(8,128)} %reduce-scatter.2.cloned.1.call-done), calls=%async_computation.1 | async-start | bytes 3145728 | tf_op jit(solution)/shard_map/all_to_all | solution.py:226
  218.9 37.3 %collective-permute-start.10 = (f32[1,2,20,2]{2,3,1,0:T(2,128)S(1)}, f32[1,2,20,2]{2,3,1,0:T(2,128)S(1)}, u32[]{:S(2)}, u32[]{:S(2)}) collective-permute-start(f32[1,2,20,2]{2,3,1,0:T(2,128)S(1)} %maximum_select_fusion.13), channel_id=1, source_target_pairs={{0,16},{2,18},{4,20},{6,22},{8,24},{10,26},{12,28},{14,30},{16,0},... | collective-permute-start | bytes 968 | tf_op jit(solution)/shard_map/ppermute | solution.py:28
  256.3 3.6 %collective-permute-start.11 = (f32[2,2,20,2]{2,3,1,0:T(2,128)S(1)}, f32[2,2,20,2]{2,3,1,0:T(2,128)S(1)}, u32[]{:S(2)}, u32[]{:S(2)}) collective-permute-start(f32[2,2,20,2]{2,3,1,0:T(2,128)S(1)} %maximum_select_fusion.12), channel_id=1, source_target_pairs={{0,8},{2,10},{4,12},{6,14},{8,0},{10,2},{12,4},{14,6},{16,24},{18,... | collective-permute-start | bytes 1928 | tf_op jit(solution)/shard_map/ppermute | solution.py:28
  259.9 4.9 %collective-permute-start.12 = (f32[4,2,20,2]{2,3,1,0:T(2,128)S(1)}, f32[4,2,20,2]{2,3,1,0:T(2,128)S(1)}, u32[]{:S(2)}, u32[]{:S(2)}) collective-permute-start(f32[4,2,20,2]{2,3,1,0:T(2,128)S(1)} %maximum_select_fusion.11), channel_id=1, source_target_pairs={{0,4},{2,6},{4,0},{6,2},{8,12},{10,14},{12,8},{14,10},{16,20},{18,... | collective-permute-start | bytes 3848 | tf_op jit(solution)/shard_map/ppermute | solution.py:28
  264.8 3.8 %collective-permute-start.13 = (f32[8,2,20,2]{2,3,1,0:T(2,128)S(1)}, f32[8,2,20,2]{2,3,1,0:T(2,128)S(1)}, u32[]{:S(2)}, u32[]{:S(2)}) collective-permute-start(f32[8,2,20,2]{2,3,1,0:T(2,128)S(1)} %maximum_select_fusion.10), channel_id=1, source_target_pairs={{0,2},{2,0},{4,6},{6,4},{8,10},{10,8},{12,14},{14,12},{16,18},{18,... | collective-permute-start | bytes 7688 | tf_op jit(solution)/shard_map/ppermute | solution.py:28
Sparse Core Ops, SparseCore 0:
  31.8 160.6 all-gather.1
  202.7 9.2 reduce-scatter.1

commit v9 on v7

--- a/solution.py
+++ b/solution.py
@@ -15,22 +15,33 @@
 norm_eps = 1e-06
 
 
-def doubling_gather(value, axis):
+def doubling_gather(value, axis, high_first=False):
     count = lax.axis_size(axis)
     if count & (count - 1):
         return lax.all_gather(value, axis, axis=0)
     index = lax.axis_index(axis)
     block = value[None]
+    distances = []
     distance = 1
     while distance < count:
+        distances.append(distance)
+        distance *= 2
+    if high_first:
+        distances = distances[::-1]
+    for distance in distances:
         pairs = [(i, i ^ distance) for i in range(count)]
         other = lax.ppermute(block, axis, pairs)
         low = (index & distance) == 0
         block = jnp.where(
             low, jnp.concatenate([block, other], 0), jnp.concatenate([other, block], 0)
         )
-        distance *= 2
-    return block
+    if not high_first:
+        return block
+    steps = len(distances)
+    rest = value.shape
+    block = block.reshape((2,) * steps + rest)
+    order = tuple(range(steps - 1, -1, -1)) + tuple(range(steps, steps + len(rest)))
+    return jnp.transpose(block, order).reshape((count,) + rest)
 
 
 def local(
@@ -141,7 +152,7 @@
         ],
         0,
     )
-    small_gathered = lax.all_gather(small_rows, "seq", axis=0)
+    small_gathered = doubling_gather(small_rows, "seq", high_first=True)
     every_row = lax.all_gather(prefill_attention, "seq", axis=0).reshape(n_seq * span_len, feature_width)
     last_attention = small_gathered[:, 0]
     last_hidden = small_gathered[:, 1].astype(jnp.float32)

time: 275 us -> 275 us (level)
  blocking collectives: 117 us -> 59.2 us
  waiting for transfers between devices: 42.6 us -> 89 us
  starting transfers between devices: 14.4 us -> 25.9 us
    all_gather x1 -> x0, blocking collectives: 64.7 us -> none  [local(): small_gathered = lax.all_gather(small_rows, 'seq', axis=0)]
    ppermute x5 -> x9, waiting for transfers between devices: 29.5 us -> 75 us  [doubling_gather(): other = lax.ppermute(block, axis, pairs)]
    ppermute x5 -> x9, starting transfers between devices: 7.38 us -> 18.7 us  [doubling_gather(): other = lax.ppermute(block, axis, pairs)]
    all_gather x1, blocking collectives: 47.7 us -> 54.2 us  [local(): head_all = lax.all_gather(head_part, ('seq', 'tp'), axis=0)]
    unnamed x28 -> x23, local copies, waits for them, and re-layouts: 9.78 us -> 8.73 us
  transfers between devices with their start and end apart: 8 -> 12, of which waited for: 6 -> 10; matrix products, arithmetic and copies ran while one was open for 16% -> 16% of each run, Pallas kernels for 0% -> 0%
where the time goes in v9:
time: 275 us; the launch traced here: 274 us
  waiting for transfers between devices  89 us (32%)
  blocking collectives  59.2 us (22%)
  matrix products  42.6 us (15%)
  local copies, waits for them, and re-layouts  33.1 us (12%)
  starting transfers between devices  25.9 us (9%)
  between operations  14.6 us (5%)
  other arithmetic  9.71 us (4%)
    ppermute x9, waiting for transfers between devices, doubling_gather(): other = lax.ppermute(block, axis, pairs)  75 us
    all_gather x1, blocking collectives, local(): head_all = lax.all_gather(head_part, ('seq', 'tp'), axis=0)  54.2 us
    dot_general x1, matrix products, local(): logits = jnp.dot(normed, head_weight, preferred_element_type=jnp.float32)  19.8 us
    ppermute x9, starting transfers between devices, doubling_gather(): other = lax.ppermute(block, axis, pairs)  18.7 us
    reshape x1, matrix products, local(): prefill_block = column_block.reshape(n_seq, span_len, column_width)  10.1 us
    unnamed x23, local copies, waits for them, and re-layouts  8.73 us
    reduce_scatter x1, waiting for transfers between devices, local(): lax.psum_scatter(prefill_block, 'tp', scatter_dimension=1, tiled=True)  8.45 us
    sub x1, matrix products, local(): weights = jnp.where(live_mask, jnp.exp(masked - row_max), 0.0)  7.24 us
  transfers between devices with their start and end apart: 12, of which 10 were waited for; matrix products, arithmetic and copies ran while one was open for 16% of the time, Pallas kernels for 0%

profile of v9, /device:TPU:0, one launch (start us, length us, event | category | flops | bytes accessed | tf_op | source)
XLA Modules:
  0.0 274.1 jit_solution(988673916258465116)
XLA Ops:
  7.2 1.4 dynamic_slice.14
  9.3 2.4 fusion.61
  11.6 1.4 copy.187
  13.0 1.2 copy.152
  14.2 1.0 fusion.65
  15.4 2.2 copy.154
  17.7 1.2 copy.148
  18.9 0.8 fusion.26
  19.8 7.2 %fusion.68 = (f32[4,5,128]{2,1,0:T(8,128)S(1)}, bf16[4,5,128,896]{2,3,1,0:T(8,128)(2,1)}) fusion(pred[128,896]{0,1:T(8,128)(4,1)S(1)} %fusion.26, bf16[128,4,5,128]{0,3,2,1:T(8,128)(2,1)} %bitcast.126, bf16[128,4,128]{2,0,1:T(8,128)(2,1)S(1)} %copy.153, bf16[768,4,128]{2,0,1:T(8,128)(2,1)S(1)} %copy-done.3), kind=kOutput, calls=%fused_computation.111 | convolution fusion | flops 602801024 | bytes 6285312 | tf_op jit(solution)/shard_map/sub | solution.py:120
  27.0 3.5 %fusion.13 = bf16[128,4,5,128]{0,3,2,1:T(8,128)(2,1)S(1)} fusion(bf16[4,5,128,896]{2,3,1,0:T(8,128)(2,1)} %get-tuple-element.49, bf16[128,4,128]{0,2,1:T(8,128)(2,1)S(1)} %bitcast.130, bf16[768,4,128]{0,2,1:T(8,128)(2,1)} %bitcast.125, f32[128,4,5]{0,2,1:T(8,128)S(1)} %bitcast.140), kind=kOutput, calls=%fused_computation.13 | convolution fusion | flops 589692928 | bytes 6170624 | tf_op jit(solution)/shard_map/kgrs,skh->rkgh/dot_general | solution.py:123
  30.5 1.1 copy.157
  31.9 1.9 gather_fusion
  34.1 0.9 fusion.63
  35.0 1.3 copy.158
  37.2 1.0 subtract_convert_fusion
  39.3 0.8 slice.76
  40.1 4.1 %collective-permute-start = (bf16[1,11,2560]{2,1,0:T(8,128)(2,1)S(1)}, bf16[1,11,2560]{2,1,0:T(8,128)(2,1)S(1)}, u32[]{:S(2)}, u32[]{:S(2)}) collective-permute-start(bf16[1,11,2560]{2,1,0:T(8,128)(2,1)S(1)} %maximum_bitcast_fusion.9), channel_id=1, source_target_pairs={{0,16},{2,18},{4,20},{6,22},{8,24},{10,26},{12,28},{14,30},{16,0},... | collective-permute-start | bytes 168968 | tf_op jit(solution)/shard_map/ppermute | solution.py:33
  44.3 6.6 %collective-permute-done = bf16[1,11,2560]{2,1,0:T(8,128)(2,1)S(1)} collective-permute-done((bf16[1,11,2560]{2,1,0:T(8,128)(2,1)S(1)}, bf16[1,11,2560]{2,1,0:T(8,128)(2,1)S(1)}, u32[]{:S(2)}, u32[]{:S(2)}) %collective-permute-start) | collective-permute-done | bytes 56352 | tf_op jit(solution)/shard_map/ppermute | solution.py:33
  50.9 3.5 %collective-permute-start.1 = (bf16[2,11,2560]{2,1,0:T(8,128)(2,1)S(1)}, bf16[2,11,2560]{2,1,0:T(8,128)(2,1)S(1)}, u32[]{:S(2)}, u32[]{:S(2)}) collective-permute-start(bf16[2,11,2560]{2,1,0:T(8,128)(2,1)S(1)} %maximum_select_fusion.3), channel_id=1, source_target_pairs={{0,8},{2,10},{4,12},{6,14},{8,0},{10,2},{12,4},{14,6},{16,24},{18,... | collective-permute-start | bytes 337928 | tf_op jit(solution)/shard_map/ppermute | solution.py:33
  54.4 10.5 %collective-permute-done.1 = bf16[2,11,2560]{2,1,0:T(8,128)(2,1)S(1)} collective-permute-done((bf16[2,11,2560]{2,1,0:T(8,128)(2,1)S(1)}, bf16[2,11,2560]{2,1,0:T(8,128)(2,1)S(1)}, u32[]{:S(2)}, u32[]{:S(2)}) %collective-permute-start.1) | collective-permute-done | bytes 112672 | tf_op jit(solution)/shard_map/ppermute | solution.py:33
  64.9 1.8 collective-permute-start.2
  66.7 9.5 %collective-permute-done.2 = bf16[4,11,2560]{2,1,0:T(8,128)(2,1)S(1)} collective-permute-done((bf16[4,11,2560]{2,1,0:T(8,128)(2,1)S(1)}, bf16[4,11,2560]{2,1,0:T(8,128)(2,1)S(1)}, u32[]{:S(2)}, u32[]{:S(2)}) %collective-permute-start.2) | collective-permute-done | bytes 225312 | tf_op jit(solution)/shard_map/ppermute | solution.py:33
  76.7 1.8 collective-permute-start.3
  79.5 18.9 %collective-permute-done.3 = bf16[8,11,2560]{2,0,1:T(8,128)(2,1)S(1)} collective-permute-done((bf16[8,11,2560]{2,0,1:T(8,128)(2,1)S(1)}, bf16[8,11,2560]{2,0,1:T(8,128)(2,1)S(1)}, u32[]{:S(2)}, u32[]{:S(2)}) %collective-permute-start.3) | collective-permute-done | bytes 450592 | tf_op jit(solution)/shard_map/ppermute | solution.py:33
  98.9 1.0 copy.197
  100.3 0.9 copy-done.2
  101.9 1.3 mul.107
  103.3 2.3 mul.108
  105.6 1.5 fusion.24
  107.7 0.9 fusion.64
  109.3 54.2 %all-gather.1 = f32[32,20,320]{2,1,0:T(8,128)S(1)} all-gather(f32[1,20,320]{2,1,0:T(8,128)S(1)} %fusion.36), channel_id=2, replica_groups=mesh['seq'=16,'tp'=2] {'seq','tp'}, dimensions={0}, use_global_device_ids=true | all-gather | bytes 844800 | tf_op jit(solution)/shard_map/all_gather | solution.py:201
  164.1 19.8 %fusion.69 = (f32[20]{0:T(128)S(1)}, f32[20,4752]{1,0:T(8,128)S(1)}) fusion(bf16[5120,4752]{0,1:T(8,128)(2,1)} %param.27, f32[20,5120]{1,0:T(8,128)S(1)} %reshape.252, f32[5120]{0:T(1024)S(1)} %convert_element_type.132, f32[20]{0:T(128)S(1)} %add_rsqrt_fusion), kind=kOutput, calls=%fused_computation.112 | convolution fusion | flops 973611840 | bytes 49470880 | tf_op jit(solution)/shard_map/dot_general | solution.py:216
  184.9 5.5 %all-gather.4.cloned.1.call-done = bf16[16,128,2560]{2,1,0:T(8,128)(2,1)} async-done(((bf16[1,128,2560]{2,1,0:T(8,128)(2,1)}), bf16[16,128,2560]{2,1,0:T(8,128)(2,1)}) %all-gather.4.cloned.1.call-update) | async-done | bytes 10485776 | tf_op jit(solution)/shard_map/all_gather | solution.py:156
  190.4 10.1 %fusion.71 = f32[2048,320]{1,0:T(8,128)} fusion(bf16[2048,2560]{1,0:T(8,128)(2,1)} %bitcast.139, bf16[2560,320]{0,1:T(8,128)(2,1)S(1)} %copy-done), kind=kOutput, calls=%fused_computation.114 | convolution fusion | flops 3355443200 | bytes 14745600 | tf_op jit(solution)/shard_map/reshape | solution.py:229
  200.6 1.1 collective-permute-done.4
  202.5 8.5 %reduce-scatter.2.cloned.1.call-done = f32[16,64,320]{2,1,0:T(8,128)} async-done(((f32[16,128,320]{2,1,0:T(8,128)}), f32[16,64,320]{2,1,0:T(8,128)}) %reduce-scatter.2.cloned.1.call-update) | async-done | bytes 1310736 | tf_op jit(solution)/shard_map/reduce_scatter | solution.py:231
  211.0 6.9 %all-to-all-start = ((f32[16,64,320]{2,1,0:T(8,128)}), f32[16,64,320]{2,1,0:T(8,128)S(1)}, u32[]{:S(2)}, u32[]{:S(2)}) async-start(f32[16,64,320]{2,1,0:T(8,128)} %reduce-scatter.2.cloned.1.call-done), calls=%async_computation.1 | async-start | bytes 3145728 | tf_op jit(solution)/shard_map/all_to_all | solution.py:232
  218.0 2.0 collective-permute-start.6
  219.9 7.3 %collective-permute-done.6 = f32[2,2,20,2]{2,3,1,0:T(2,128)S(1)} collective-permute-done((f32[2,2,20,2]{2,3,1,0:T(2,128)S(1)}, f32[2,2,20,2]{2,3,1,0:T(2,128)S(1)}, u32[]{:S(2)}, u32[]{:S(2)}) %collective-permute-start.6) | collective-permute-done | bytes 672 | tf_op jit(solution)/shard_map/ppermute | solution.py:33
  227.4 2.2 copy.147
  229.6 14.3 %collective-permute-done.7 = f32[4,2,20,2]{2,3,1,0:T(2,128)S(1)} collective-permute-done((f32[4,2,20,2]{2,3,1,0:T(2,128)S(1)}, f32[4,2,20,2]{2,3,1,0:T(2,128)S(1)}, u32[]{:S(2)}, u32[]{:S(2)}) %collective-permute-start.7) | collective-permute-done | bytes 1312 | tf_op jit(solution)/shard_map/ppermute | solution.py:33
  243.9 4.6 %collective-permute-start.8 = (f32[8,2,20,2]{2,3,1,0:T(2,128)S(1)}, f32[8,2,20,2]{2,3,1,0:T(2,128)S(1)}, u32[]{:S(2)}, u32[]{:S(2)}) collective-permute-start(f32[8,2,20,2]{2,3,1,0:T(2,128)S(1)} %maximum_select_fusion.5), channel_id=1, source_target_pairs={{0,16},{2,18},{4,20},{6,22},{8,24},{10,26},{12,28},{14,30},{16,0},... | collective-permute-start | bytes 7688 | tf_op jit(solution)/shard_map/ppermute | solution.py:33
  249.2 6.7 %collective-permute-done.8 = f32[8,2,20,2]{2,3,1,0:T(2,128)S(1)} collective-permute-done((f32[8,2,20,2]{2,3,1,0:T(2,128)S(1)}, f32[8,2,20,2]{2,3,1,0:T(2,128)S(1)}, u32[]{:S(2)}, u32[]{:S(2)}) %collective-permute-start.8) | collective-permute-done | bytes 2592 | tf_op jit(solution)/shard_map/ppermute | solution.py:33
  256.0 1.9 broadcast_subtract_fusion
  257.9 5.0 %all_to_all.23 = f32[16,64,320]{2,1,0:T(8,128)S(1)} all-to-all(f32[16,64,320]{2,1,0:T(8,128)S(1)} %all-to-all-done), channel_id=1, replica_groups=mesh['seq'=16,'tp'=2] {'tp'}, dimensions={0} | all-to-all | bytes 2621440 | tf_op jit(solution)/shard_map/all_to_all | solution.py:233
  263.1 1.5 copy.173
  264.6 1.6 fusion.16
  266.2 1.1 copy.175
  (107 shorter events, 11.3 us)
Async XLA Ops:
  7.2 101.6 %copy-start = (bf16[2560,320]{0,1:T(8,128)(2,1)S(1)}, bf16[2560,320]{0,1:T(8,128)(2,1)}, u32[]{:S(2)}) copy-start(bf16[2560,320]{0,1:T(8,128)(2,1)} %param.25) | copy-start | bytes 4915204
  7.2 183.2 %all-gather.4.cloned.1.call-start = ((), (), s32[]{:S(2)}) async-start(), calls=%async_computation.3 | async-start | bytes 11141120 | tf_op jit(solution)/shard_map/all_gather | solution.py:156
  15.4 4.3 %copy-start.3 = (bf16[768,4,128]{2,0,1:T(8,128)(2,1)S(1)}, bf16[768,4,128]{2,0,1:T(8,128)(2,1)}, u32[]{:S(2)}) copy-start(bf16[768,4,128]{2,0,1:T(8,128)(2,1)} %copy.152) | copy-start | bytes 2359300
  30.5 1.4 copy-start.7
  31.7 179.3 %reduce-scatter.2.cloned.1.call-start = ((), (), s32[]{:S(2)}) async-start(), calls=%async_computation.4 | async-start | bytes 4718592 | tf_op jit(solution)/shard_map/reduce_scatter | solution.py:231
  34.0 2.3 copy-start.4
  34.1 2.3 copy-start.8
  40.1 10.7 %collective-permute-start = (bf16[1,11,2560]{2,1,0:T(8,128)(2,1)S(1)}, bf16[1,11,2560]{2,1,0:T(8,128)(2,1)S(1)}, u32[]{:S(2)}, u32[]{:S(2)}) collective-permute-start(bf16[1,11,2560]{2,1,0:T(8,128)(2,1)S(1)} %maximum_bitcast_fusion.9), channel_id=1, source_target_pairs={{0,16},{2,18},{4,20},{6,22},{8,24},{10,26},{12,28},{14,30},{16,0},... | collective-permute-start | bytes 168968 | tf_op jit(solution)/shard_map/ppermute | solution.py:33
  44.3 34.3 %copy-start.6 = (bf16[2,4,512]{2,1,0:T(4,128)(2,1)S(1)}, bf16[2,4,512]{2,1,0:T(4,128)(2,1)}, u32[]{:S(2)}) copy-start(bf16[2,4,512]{2,1,0:T(4,128)(2,1)} %param.21) | copy-start | bytes 24580
  50.9 27.7 %copy-start.5 = (bf16[5120]{0:T(1024)(128)(2,1)S(1)}, bf16[5120]{0:T(1024)(128)(2,1)}, u32[]{:S(2)}) copy-start(bf16[5120]{0:T(1024)(128)(2,1)} %param.26) | copy-start | bytes 30724
  50.9 14.0 %collective-permute-start.1 = (bf16[2,11,2560]{2,1,0:T(8,128)(2,1)S(1)}, bf16[2,11,2560]{2,1,0:T(8,128)(2,1)S(1)}, u32[]{:S(2)}, u32[]{:S(2)}) collective-permute-start(bf16[2,11,2560]{2,1,0:T(8,128)(2,1)S(1)} %maximum_select_fusion.3), channel_id=1, source_target_pairs={{0,8},{2,10},{4,12},{6,14},{8,0},{10,2},{12,4},{14,6},{16,24},{18,... | collective-permute-start | bytes 337928 | tf_op jit(solution)/shard_map/ppermute | solution.py:33
  64.9 11.3 %collective-permute-start.2 = (bf16[4,11,2560]{2,1,0:T(8,128)(2,1)S(1)}, bf16[4,11,2560]{2,1,0:T(8,128)(2,1)S(1)}, u32[]{:S(2)}, u32[]{:S(2)}) collective-permute-start(bf16[4,11,2560]{2,1,0:T(8,128)(2,1)S(1)} %maximum_select_fusion.2), channel_id=1, source_target_pairs={{0,4},{2,6},{4,0},{6,2},{8,12},{10,14},{12,8},{14,10},{16,20},{18,... | collective-permute-start | bytes 675848 | tf_op jit(solution)/shard_map/ppermute | solution.py:33
  76.7 21.8 %collective-permute-start.3 = (bf16[8,11,2560]{2,0,1:T(8,128)(2,1)S(1)}, bf16[8,11,2560]{2,0,1:T(8,128)(2,1)S(1)}, u32[]{:S(2)}, u32[]{:S(2)}) collective-permute-start(bf16[8,11,2560]{2,0,1:T(8,128)(2,1)S(1)} %copy.162), channel_id=1, source_target_pairs={{0,2},{2,0},{4,6},{6,4},{8,10},{10,8},{12,14},{14,12},{16,18},{18,... | collective-permute-start | bytes 1351688 | tf_op jit(solution)/shard_map/ppermute | solution.py:33
  100.3 0.9 copy-start.2
  183.9 0.8 copy-start.1
  200.5 1.2 collective-permute-start.4
  201.8 16.2 %collective-permute-start.5 = (f32[1,2,20,2]{2,3,1,0:T(2,128)S(1)}, f32[1,2,20,2]{2,3,1,0:T(2,128)S(1)}, u32[]{:S(2)}, u32[]{:S(2)}) collective-permute-start(f32[1,2,20,2]{2,3,1,0:T(2,128)S(1)} %maximum_select_fusion.8), channel_id=1, source_target_pairs={{0,2},{2,0},{4,6},{6,4},{8,10},{10,8},{12,14},{14,12},{16,18},{18,... | collective-permute-start | bytes 968 | tf_op jit(solution)/shard_map/ppermute | solution.py:33
  211.0 46.9 %all-to-all-start = ((f32[16,64,320]{2,1,0:T(8,128)}), f32[16,64,320]{2,1,0:T(8,128)S(1)}, u32[]{:S(2)}, u32[]{:S(2)}) async-start(f32[16,64,320]{2,1,0:T(8,128)} %reduce-scatter.2.cloned.1.call-done), calls=%async_computation.1 | async-start | bytes 3145728 | tf_op jit(solution)/shard_map/all_to_all | solution.py:232
  218.0 9.3 %collective-permute-start.6 = (f32[2,2,20,2]{2,3,1,0:T(2,128)S(1)}, f32[2,2,20,2]{2,3,1,0:T(2,128)S(1)}, u32[]{:S(2)}, u32[]{:S(2)}) collective-permute-start(f32[2,2,20,2]{2,3,1,0:T(2,128)S(1)} %maximum_select_fusion.7), channel_id=1, source_target_pairs={{0,4},{2,6},{4,0},{6,2},{8,12},{10,14},{12,8},{14,10},{16,20},{18,... | collective-permute-start | bytes 1928 | tf_op jit(solution)/shard_map/ppermute | solution.py:33
  227.3 16.6 %collective-permute-start.7 = (f32[4,2,20,2]{2,3,1,0:T(2,128)S(1)}, f32[4,2,20,2]{2,3,1,0:T(2,128)S(1)}, u32[]{:S(2)}, u32[]{:S(2)}) collective-permute-start(f32[4,2,20,2]{2,3,1,0:T(2,128)S(1)} %maximum_select_fusion.6), channel_id=1, source_target_pairs={{0,8},{2,10},{4,12},{6,14},{8,0},{10,2},{12,4},{14,6},{16,24},{18,... | collective-permute-start | bytes 3848 | tf_op jit(solution)/shard_map/ppermute | solution.py:33
  243.9 12.0 %collective-permute-start.8 = (f32[8,2,20,2]{2,3,1,0:T(2,128)S(1)}, f32[8,2,20,2]{2,3,1,0:T(2,128)S(1)}, u32[]{:S(2)}, u32[]{:S(2)}) collective-permute-start(f32[8,2,20,2]{2,3,1,0:T(2,128)S(1)} %maximum_select_fusion.5), channel_id=1, source_target_pairs={{0,16},{2,18},{4,20},{6,22},{8,24},{10,26},{12,28},{14,30},{16,0},... | collective-permute-start | bytes 7688 | tf_op jit(solution)/shard_map/ppermute | solution.py:33
Sparse Core Ops, SparseCore 0:
  31.8 158.6 all-gather.3
  200.7 10.2 reduce-scatter.1

commit v10 on v9

--- a/solution.py
+++ b/solution.py
@@ -153,7 +153,11 @@
         0,
     )
     small_gathered = doubling_gather(small_rows, "seq", high_first=True)
-    every_row = lax.all_gather(prefill_attention, "seq", axis=0).reshape(n_seq * span_len, feature_width)
+    chunk_rows = span_len // 2
+    every_chunk = [
+        lax.all_gather(prefill_attention[c * chunk_rows : (c + 1) * chunk_rows], "seq", axis=0)
+        for c in range(2)
+    ]
     last_attention = small_gathered[:, 0]
     last_hidden = small_gathered[:, 1].astype(jnp.float32)
     every_flat = small_gathered[:, 2:].reshape(n_seq, -1).astype(jnp.float32)
@@ -217,7 +221,7 @@
     local_max = jnp.max(logits, axis=-1)
     local_sum = jnp.sum(jnp.exp(logits - local_max[:, None]), axis=-1)
     local_stats = jnp.stack([local_max, local_sum], -1)
-    every_row, local_stats = lax.optimization_barrier((every_row, local_stats))
+    every_chunk[1], local_stats = lax.optimization_barrier((every_chunk[1], local_stats))
     stats = doubling_gather(doubling_gather(local_stats, "tp"), "seq").reshape(
         (n_seq * n_tp,) + local_stats.shape
     )
@@ -225,12 +229,23 @@
     global_sum = jnp.sum(stats[..., 1] * jnp.exp(stats[..., 0] - global_max[None]), axis=0)
     log_probs = logits - (global_max + jnp.log(global_sum))[:, None]
 
-    column_block = jnp.dot(every_row, out_weight, preferred_element_type=jnp.float32)
-    prefill_block = column_block.reshape(n_seq, span_len, column_width)
-
-    summed_rows = lax.psum_scatter(prefill_block, "tp", scatter_dimension=1, tiled=True)
-    by_source = lax.all_to_all(summed_rows, "seq", split_axis=0, concat_axis=0, tiled=True)
-    own_columns = lax.all_to_all(by_source, "tp", split_axis=0, concat_axis=1, tiled=True)
+    pieces = []
+    for rows in every_chunk:
+        block = jnp.dot(
+            rows.reshape(n_seq * chunk_rows, feature_width),
+            out_weight,
+            preferred_element_type=jnp.float32,
+        ).reshape(n_seq, chunk_rows, column_width)
+        if n_tp == 2:
+            half = chunk_rows // 2
+            mine = lax.dynamic_slice_in_dim(block, tp_index * half, half, axis=1)
+            theirs = lax.dynamic_slice_in_dim(block, (1 - tp_index) * half, half, axis=1)
+            summed = mine + lax.ppermute(theirs, "tp", [(0, 1), (1, 0)])
+        else:
+            summed = lax.psum_scatter(block, "tp", scatter_dimension=1, tiled=True)
+        by_source = lax.all_to_all(summed, "seq", split_axis=0, concat_axis=0, tiled=True)
+        pieces.append(lax.all_to_all(by_source, "tp", split_axis=0, concat_axis=1, tiled=True))
+    own_columns = jnp.concatenate(pieces, 1)
     projected = jnp.transpose(own_columns, (1, 0, 2)).reshape(span_len, feature_width)
     prefill_out = (prefill_hidden.astype(jnp.float32) + projected).astype(jnp.bfloat16)
 

time: 275 us -> 297 us (1.080)
  waiting for transfers between devices: 89 us -> 102 us
  local copies, waits for them, and re-layouts: 33.1 us -> 40.4 us
  other arithmetic: 9.71 us -> 13.9 us
    all_gather x1 -> x2, waiting for transfers between devices: 5.51 us -> 38.6 us  [local(): lax.all_gather(prefill_attention[c * chunk_rows:(c + 1) * chunk_rows], 's...]
    ppermute x9, waiting for transfers between devices: 75 us -> 45.9 us  [doubling_gather(): other = lax.ppermute(block, axis, pairs)]
    all_to_all x1 -> x2, waiting for transfers between devices: 0.01 us -> 17 us  [local(): lax.all_to_all(summed, 'seq', split_axis=0, concat_axis=0, tiled=True)]
    dot_general x0 -> x2, matrix products: none -> 11.5 us  [local(): jnp.dot(rows.reshape(n_seq * chunk_rows, feature_width), out_weight, pref...]
    reshape x1 -> x0, matrix products: 10.1 us -> none  [local(): prefill_block = column_block.reshape(n_seq, span_len, column_width)]
    reduce_scatter x1 -> x0, waiting for transfers between devices: 8.45 us -> none  [local(): lax.psum_scatter(prefill_block, 'tp', scatter_dimension=1, tiled=True)]
    all_gather x1, blocking collectives: 54.2 us -> 47.6 us  [local(): head_all = lax.all_gather(head_part, ('seq', 'tp'), axis=0)]
    ppermute x9, starting transfers between devices: 18.7 us -> 13.8 us  [doubling_gather(): other = lax.ppermute(block, axis, pairs)]
  transfers between devices with their start and end apart: 12 -> 15, of which waited for: 10 -> 8; matrix products, arithmetic and copies ran while one was open for 16% -> 22% of each run, Pallas kernels for 0% -> 0%
where the time goes in v10:
time: 297 us; the launch traced here: 296 us
  waiting for transfers between devices  102 us (34%)
  blocking collectives  57.2 us (19%)
  matrix products  44.7 us (15%)
  local copies, waits for them, and re-layouts  40.4 us (14%)
  starting transfers between devices  23.1 us (8%)
  between operations  14.7 us (5%)
  other arithmetic  13.9 us (5%)
    all_gather x1, blocking collectives, local(): head_all = lax.all_gather(head_part, ('seq', 'tp'), axis=0)  47.6 us
    ppermute x9, waiting for transfers between devices, doubling_gather(): other = lax.ppermute(block, axis, pairs)  45.9 us
    all_gather x2, waiting for transfers between devices, local(): lax.all_gather(prefill_attention[c * chunk_rows:(c + 1) * chunk_rows], 's...  38.6 us
    dot_general x1, matrix products, local(): logits = jnp.dot(normed, head_weight, preferred_element_type=jnp.float32)  19.8 us
    all_to_all x2, waiting for transfers between devices, local(): lax.all_to_all(summed, 'seq', split_axis=0, concat_axis=0, tiled=True)  17 us
    ppermute x9, starting transfers between devices, doubling_gather(): other = lax.ppermute(block, axis, pairs)  13.8 us
    dot_general x2, matrix products, local(): jnp.dot(rows.reshape(n_seq * chunk_rows, feature_width), out_weight, pref...  11.5 us
    all_to_all x2, blocking collectives, local(): lax.all_to_all(by_source, 'tp', split_axis=0, concat_axis=1, tiled=True)  9.6 us
  transfers between devices with their start and end apart: 15, of which 8 were waited for; matrix products, arithmetic and copies ran while one was open for 22% of the time, Pallas kernels for 0%

profile of v10, /device:TPU:0, one launch (start us, length us, event | category | flops | bytes accessed | tf_op | source)
XLA Modules:
  0.0 295.7 jit_solution(8700003377086773813)
XLA Ops:
  7.2 1.4 dynamic_slice.26
  9.3 2.4 fusion.65
  11.6 1.4 copy.179
  13.0 1.2 copy.142
  15.4 2.2 copy.144
  17.9 1.2 copy.138
  19.3 1.4 fusion.30
  20.7 7.5 %fusion.73 = (f32[4,5,128]{2,1,0:T(8,128)S(1)}, bf16[4,5,128,896]{2,3,1,0:T(8,128)(2,1)}) fusion(pred[128,896]{0,1:T(8,128)(4,1)} %fusion.30, bf16[128,4,5,128]{0,3,2,1:T(8,128)(2,1)} %bitcast.133, bf16[128,4,128]{2,0,1:T(8,128)(2,1)S(1)} %copy.143, bf16[768,4,128]{2,0,1:T(8,128)(2,1)S(1)} %copy-done.5), kind=kOutput, calls=%fused_computation.120 | convolution fusion | flops 602801024 | bytes 6285312 | tf_op jit(solution)/shard_map/sub | solution.py:120
  28.2 3.9 %fusion.17 = bf16[128,4,5,128]{3,0,2,1:T(8,128)(2,1)S(1)} fusion(bf16[4,5,128,896]{2,3,1,0:T(8,128)(2,1)} %get-tuple-element.48, bf16[128,4,128]{2,0,1:T(8,128)(2,1)S(1)} %copy.139, bf16[768,4,128]{2,0,1:T(8,128)(2,1)S(1)} %copy-done.6, f32[128,4,5]{0,2,1:T(8,128)S(1)} %bitcast.147), kind=kOutput, calls=%fused_computation.18 | convolution fusion | flops 589692928 | bytes 6170624 | tf_op jit(solution)/shard_map/kgrs,skh->rkgh/dot_general | solution.py:123
  32.5 1.1 all_gather.20
  33.9 1.9 gather_fusion
  41.2 4.1 %collective-permute-start.1 = (bf16[1,11,2560]{2,1,0:T(8,128)(2,1)S(1)}, bf16[1,11,2560]{2,1,0:T(8,128)(2,1)S(1)}, u32[]{:S(2)}, u32[]{:S(2)}) collective-permute-start(bf16[1,11,2560]{2,1,0:T(8,128)(2,1)S(1)} %maximum_bitcast_fusion.10), channel_id=1, source_target_pairs={{0,16},{2,18},{4,20},{6,22},{8,24},{10,26},{12,28},{14,30},{16,0},... | collective-permute-start | bytes 168968 | tf_op jit(solution)/shard_map/ppermute | solution.py:33
  45.3 5.7 %collective-permute-done.1 = bf16[1,11,2560]{2,1,0:T(8,128)(2,1)S(1)} collective-permute-done((bf16[1,11,2560]{2,1,0:T(8,128)(2,1)S(1)}, bf16[1,11,2560]{2,1,0:T(8,128)(2,1)S(1)}, u32[]{:S(2)}, u32[]{:S(2)}) %collective-permute-start.1) | collective-permute-done | bytes 56352 | tf_op jit(solution)/shard_map/ppermute | solution.py:33
  51.1 2.8 collective-permute-start.2
  54.0 6.6 %collective-permute-done.2 = bf16[2,11,2560]{2,1,0:T(8,128)(2,1)S(1)} collective-permute-done((bf16[2,11,2560]{2,1,0:T(8,128)(2,1)S(1)}, bf16[2,11,2560]{2,1,0:T(8,128)(2,1)S(1)}, u32[]{:S(2)}, u32[]{:S(2)}) %collective-permute-start.2) | collective-permute-done | bytes 112672 | tf_op jit(solution)/shard_map/ppermute | solution.py:33
  60.6 1.4 collective-permute-start.3
  62.3 1.1 all_gather.18
  63.4 10.1 %collective-permute-done.3 = bf16[4,11,2560]{2,1,0:T(8,128)(2,1)} collective-permute-done((bf16[4,11,2560]{2,1,0:T(8,128)(2,1)S(1)}, bf16[4,11,2560]{2,1,0:T(8,128)(2,1)}, u32[]{:S(2)}, u32[]{:S(2)}) %collective-permute-start.3) | collective-permute-done | bytes 225312 | tf_op jit(solution)/shard_map/ppermute | solution.py:33
  73.6 1.3 maximum_select_fusion.1
  74.9 1.0 copy.154
  76.4 1.1 copy.135
  78.5 8.2 %collective-permute-done.4 = bf16[8,11,2560]{2,0,1:T(8,128)(2,1)} collective-permute-done((bf16[8,11,2560]{2,0,1:T(8,128)(2,1)}, bf16[8,11,2560]{2,0,1:T(8,128)(2,1)}, u32[]{:S(2)}, u32[]{:S(2)}) %collective-permute-start.4) | collective-permute-done | bytes 450592 | tf_op jit(solution)/shard_map/ppermute | solution.py:33
  86.7 1.2 copy.155
  91.3 1.3 mul.117
  92.6 2.3 mul.118
  94.9 1.5 fusion.28
  98.6 47.6 %all-gather.1 = f32[32,20,320]{2,1,0:T(8,128)S(1)} all-gather(f32[1,20,320]{2,1,0:T(8,128)S(1)} %fusion.40), channel_id=2, replica_groups=mesh['seq'=16,'tp'=2] {'seq','tp'}, dimensions={0}, use_global_device_ids=true | all-gather | bytes 844800 | tf_op jit(solution)/shard_map/all_gather | solution.py:205
  146.9 19.8 %fusion.74 = (f32[20]{0:T(128)S(1)}, f32[20,4752]{1,0:T(8,128)S(1)}) fusion(bf16[5120,4752]{0,1:T(8,128)(2,1)} %param.27, f32[20,5120]{1,0:T(8,128)S(1)} %reshape.256, f32[5120]{0:T(1024)S(1)} %convert_element_type.132, f32[20]{0:T(128)S(1)} %add_rsqrt_fusion), kind=kOutput, calls=%fused_computation.121 | convolution fusion | flops 973611840 | bytes 49470880 | tf_op jit(solution)/shard_map/dot_general | solution.py:220
  167.5 4.8 %fusion.7 = f32[16,64,320]{2,1,0:T(8,128)S(1)} fusion(bf16[16,64,2560]{2,1,0:T(8,128)(2,1)} %all-gather.7.cloned.1.call-done, bf16[2560,320]{0,1:T(8,128)(2,1)S(1)} %copy-done), kind=kOutput, calls=%fused_computation.10 | convolution fusion | flops 1677721600 | bytes 8192000 | tf_op jit(solution)/shard_map/dot_general | solution.py:234
  172.5 1.1 copy-done.3
  173.5 1.0 constant_dynamic-slice_fusion.1
  174.7 1.4 collective-permute-done.7
  176.0 38.6 %all-gather.5.cloned.1.call-done = bf16[16,64,2560]{2,1,0:T(8,128)(2,1)} async-done(((bf16[1,64,2560]{2,1,0:T(8,128)(2,1)}), bf16[16,64,2560]{2,1,0:T(8,128)(2,1)}) %all-gather.5.cloned.1.call-update) | async-done | bytes 5242896 | tf_op jit(solution)/shard_map/all_gather | solution.py:158
  214.6 6.7 %fusion.9 = f32[16,64,320]{2,1,0:T(8,128)} fusion(bf16[16,64,2560]{2,1,0:T(8,128)(2,1)} %all-gather.5.cloned.1.call-done, bf16[2560,320]{0,1:T(8,128)(2,1)S(1)} %copy-done), kind=kOutput, calls=%fused_computation.12 | convolution fusion | flops 1677721600 | bytes 8192000 | tf_op jit(solution)/shard_map/dot_general | solution.py:234
  221.3 1.6 collective-permute-start.9
  223.9 4.3 %all-to-all-start.2 = ((f32[16,32,320]{2,1,0:T(8,128)}), f32[16,32,320]{2,1,0:T(8,128)S(1)}, u32[]{:S(2)}, u32[]{:S(2)}) async-start(f32[16,32,320]{2,1,0:T(8,128)} %dynamic-slice_add_fusion), calls=%async_computation.2 | async-start | bytes 1572864 | tf_op jit(solution)/shard_map/all_to_all | solution.py:246
  228.2 2.1 constant_dynamic-slice_fusion.2
  230.3 2.9 collective-permute-start.10
  233.8 13.8 %collective-permute-done.10 = f32[8,2,20,2]{2,3,1,0:T(2,128)S(1)} collective-permute-done((f32[8,2,20,2]{2,3,1,0:T(2,128)S(1)}, f32[8,2,20,2]{2,3,1,0:T(2,128)S(1)}, u32[]{:S(2)}, u32[]{:S(2)}) %collective-permute-start.10) | collective-permute-done | bytes 2592 | tf_op jit(solution)/shard_map/ppermute | solution.py:33
  247.8 2.4 dynamic-slice_add_fusion.1
  250.1 5.1 %all_to_all.46 = f32[16,32,320]{2,1,0:T(8,128)} all-to-all(f32[16,32,320]{2,1,0:T(8,128)S(1)} %all-to-all-done.2), channel_id=1, replica_groups=mesh['seq'=16,'tp'=2] {'tp'}, dimensions={0} | all-to-all | bytes 1310720 | tf_op jit(solution)/shard_map/all_to_all | solution.py:247
  255.3 4.6 %all-to-all-start = ((f32[16,32,320]{2,1,0:T(8,128)}), f32[16,32,320]{2,1,0:T(8,128)S(1)}, u32[]{:S(2)}, u32[]{:S(2)}) async-start(f32[16,32,320]{2,1,0:T(8,128)} %dynamic-slice_add_fusion.1), calls=%async_computation | async-start | bytes 1572864 | tf_op jit(solution)/shard_map/all_to_all | solution.py:246
  260.8 2.1 copy.163
  262.9 17.0 %all-to-all-done = f32[16,32,320]{2,1,0:T(8,128)S(1)} async-done(((f32[16,32,320]{2,1,0:T(8,128)}), f32[16,32,320]{2,1,0:T(8,128)S(1)}, u32[]{:S(2)}, u32[]{:S(2)}) %all-to-all-start) | async-done | bytes 655392 | tf_op jit(solution)/shard_map/all_to_all | solution.py:246
  279.9 4.5 %all_to_all.47 = f32[16,32,320]{2,1,0:T(8,128)S(1)} all-to-all(f32[16,32,320]{2,1,0:T(8,128)S(1)} %all-to-all-done), channel_id=1, replica_groups=mesh['seq'=16,'tp'=2] {'tp'}, dimensions={0} | all-to-all | bytes 1310720 | tf_op jit(solution)/shard_map/all_to_all | solution.py:247
  284.6 1.6 copy.164
  286.1 1.6 fusion.20
  287.7 1.1 copy.166
  (138 shorter events, 20.0 us)
Async XLA Ops:
  7.2 90.9 %copy-start = (bf16[2560,320]{0,1:T(8,128)(2,1)S(1)}, bf16[2560,320]{0,1:T(8,128)(2,1)}, u32[]{:S(2)}) copy-start(bf16[2560,320]{0,1:T(8,128)(2,1)} %param.25) | copy-start | bytes 4915204
  7.2 159.9 %all-gather.7.cloned.1.call-start = ((), (), s32[]{:S(2)}) async-start(), calls=%async_computation.5 | async-start | bytes 5570560 | tf_op jit(solution)/shard_map/all_gather | solution.py:158
  17.9 2.9 copy-start.5
  20.7 7.5 %copy-start.6 = (bf16[768,4,128]{2,0,1:T(8,128)(2,1)S(1)}, bf16[768,4,128]{2,0,1:T(8,128)(2,1)}, u32[]{:S(2)}) copy-start(bf16[768,4,128]{2,0,1:T(8,128)(2,1)} %copy.138) | copy-start | bytes 2359300
  32.2 1.5 copy-start.8
  32.2 1.7 copy-start.13
  33.6 181.0 %all-gather.5.cloned.1.call-start = ((), (), s32[]{:S(2)}) async-start(), calls=%async_computation.4 | async-start | bytes 5570560 | tf_op jit(solution)/shard_map/all_gather | solution.py:158
  36.0 1.2 copy-start.14
  37.1 8.2 %copy-start.9 = (bf16[4,4,5,128]{3,2,1,0:T(8,128)(2,1)}, bf16[4,4,5,128]{3,2,1,0:T(8,128)(2,1)S(1)}, u32[]{:S(2)}) copy-start(bf16[4,4,5,128]{3,2,1,0:T(8,128)(2,1)S(1)} %reshape.246) | copy-start | bytes 61444
  41.2 9.9 %collective-permute-start.1 = (bf16[1,11,2560]{2,1,0:T(8,128)(2,1)S(1)}, bf16[1,11,2560]{2,1,0:T(8,128)(2,1)S(1)}, u32[]{:S(2)}, u32[]{:S(2)}) collective-permute-start(bf16[1,11,2560]{2,1,0:T(8,128)(2,1)S(1)} %maximum_bitcast_fusion.10), channel_id=1, source_target_pairs={{0,16},{2,18},{4,20},{6,22},{8,24},{10,26},{12,28},{14,30},{16,0},... | collective-permute-start | bytes 168968 | tf_op jit(solution)/shard_map/ppermute | solution.py:33
  51.1 9.4 %collective-permute-start.2 = (bf16[2,11,2560]{2,1,0:T(8,128)(2,1)S(1)}, bf16[2,11,2560]{2,1,0:T(8,128)(2,1)S(1)}, u32[]{:S(2)}, u32[]{:S(2)}) collective-permute-start(bf16[2,11,2560]{2,1,0:T(8,128)(2,1)S(1)} %maximum_select_fusion.3), channel_id=1, source_target_pairs={{0,8},{2,10},{4,12},{6,14},{8,0},{10,2},{12,4},{14,6},{16,24},{18,... | collective-permute-start | bytes 337928 | tf_op jit(solution)/shard_map/ppermute | solution.py:33
  60.6 12.9 %collective-permute-start.3 = (bf16[4,11,2560]{2,1,0:T(8,128)(2,1)S(1)}, bf16[4,11,2560]{2,1,0:T(8,128)(2,1)}, u32[]{:S(2)}, u32[]{:S(2)}) collective-permute-start(bf16[4,11,2560]{2,1,0:T(8,128)(2,1)S(1)} %maximum_select_fusion.2), channel_id=1, source_target_pairs={{0,4},{2,6},{4,0},{6,2},{8,12},{10,14},{12,8},{14,10},{16,20},{18,... | collective-permute-start | bytes 675848 | tf_op jit(solution)/shard_map/ppermute | solution.py:33
  62.3 14.2 %copy-start.12 = (bf16[2,4,512]{2,1,0:T(4,128)(2,1)S(1)}, bf16[2,4,512]{2,1,0:T(4,128)(2,1)}, u32[]{:S(2)}) copy-start(bf16[2,4,512]{2,1,0:T(4,128)(2,1)} %param.21) | copy-start | bytes 24580
  62.3 14.2 %copy-start.7 = (bf16[128,2560]{1,0:T(8,128)(2,1)S(1)}, bf16[128,2560]{1,0:T(8,128)(2,1)}, u32[]{:S(2)}) copy-start(bf16[128,2560]{1,0:T(8,128)(2,1)} %param.14) | copy-start | bytes 1966084
  63.4 14.1 %copy-start.11 = (bf16[5120]{0:T(1024)(128)(2,1)S(1)}, bf16[5120]{0:T(1024)(128)(2,1)}, u32[]{:S(2)}) copy-start(bf16[5120]{0:T(1024)(128)(2,1)} %param.26) | copy-start | bytes 30724
  63.4 14.9 %copy-start.10 = (bf16[4,4,5,128]{3,2,1,0:T(8,128)(2,1)S(1)}, bf16[4,4,5,128]{3,2,1,0:T(8,128)(2,1)}, u32[]{:S(2)}) copy-start(bf16[4,4,5,128]{3,2,1,0:T(8,128)(2,1)} %copy-done.9) | copy-start | bytes 61444
  75.9 10.8 %collective-permute-start.4 = (bf16[8,11,2560]{2,0,1:T(8,128)(2,1)}, bf16[8,11,2560]{2,0,1:T(8,128)(2,1)}, u32[]{:S(2)}, u32[]{:S(2)}) collective-permute-start(bf16[8,11,2560]{2,0,1:T(8,128)(2,1)} %copy.154), channel_id=1, source_target_pairs={{0,2},{2,0},{4,6},{6,4},{8,10},{10,8},{12,14},{14,12},{16,18},{18,... | collective-permute-start | bytes 1351688 | tf_op jit(solution)/shard_map/ppermute | solution.py:33
  89.6 0.9 copy-start.1
  167.1 5.3 %collective-permute-start.6 = (f32[1,20,2]{1,2,0:T(2,128)S(1)}, f32[1,20,2]{1,2,0:T(2,128)S(1)}, u32[]{:S(2)}, u32[]{:S(2)}) collective-permute-start(f32[1,20,2]{1,2,0:T(2,128)S(1)} %bitcast.143), channel_id=1, source_target_pairs={{0,1},{1,0},{2,3},{3,2},{4,5},{5,4},{6,7},{7,6},{8,9},{9,8},{10,11... | collective-permute-start | bytes 488 | tf_op jit(solution)/shard_map/ppermute | solution.py:33
  172.3 1.2 copy-start.3
  172.4 3.7 %collective-permute-start.7 = (f32[1,2,20,2]{2,3,1,0:T(2,128)S(1)}, f32[1,2,20,2]{2,3,1,0:T(2,128)S(1)}, u32[]{:S(2)}, u32[]{:S(2)}) collective-permute-start(f32[1,2,20,2]{2,3,1,0:T(2,128)S(1)} %maximum_select_fusion.8), channel_id=1, source_target_pairs={{0,2},{2,0},{4,6},{6,4},{8,10},{10,8},{12,14},{14,12},{16,18},{18,... | collective-permute-start | bytes 968 | tf_op jit(solution)/shard_map/ppermute | solution.py:33
  174.5 48.3 %collective-permute-start.5 = (f32[16,32,320]{2,1,0:T(8,128)}, f32[16,32,320]{2,1,0:T(8,128)S(1)}, u32[]{:S(2)}, u32[]{:S(2)}) collective-permute-start(f32[16,32,320]{2,1,0:T(8,128)} %constant_dynamic-slice_fusion.1), channel_id=1, source_target_pairs={{0,1},{1,0},{2,3},{3,2},{4,5},{5,4},{6,7},{7,6},{8,9},{9,8},{10,11... | collective-permute-start | bytes 1966088 | tf_op jit(solution)/shard_map/ppermute | solution.py:243
  176.0 45.3 %collective-permute-start.8 = (f32[2,2,20,2]{2,3,1,0:T(2,128)S(1)}, f32[2,2,20,2]{2,3,1,0:T(2,128)S(1)}, u32[]{:S(2)}, u32[]{:S(2)}) collective-permute-start(f32[2,2,20,2]{2,3,1,0:T(2,128)S(1)} %maximum_select_fusion.7), channel_id=1, source_target_pairs={{0,4},{2,6},{4,0},{6,2},{8,12},{10,14},{12,8},{14,10},{16,20},{18,... | collective-permute-start | bytes 1928 | tf_op jit(solution)/shard_map/ppermute | solution.py:33
  214.6 8.3 %copy-start.4 = (f32[16,64,320]{2,1,0:T(8,128)S(1)}, f32[16,64,320]{2,1,0:T(8,128)}, u32[]{:S(2)}) copy-start(f32[16,64,320]{2,1,0:T(8,128)} %copy-done.3) | copy-start | bytes 3932164
  221.3 9.0 %collective-permute-start.9 = (f32[4,2,20,2]{2,3,1,0:T(2,128)S(1)}, f32[4,2,20,2]{2,3,1,0:T(2,128)S(1)}, u32[]{:S(2)}, u32[]{:S(2)}) collective-permute-start(f32[4,2,20,2]{2,3,1,0:T(2,128)S(1)} %maximum_select_fusion.6), channel_id=1, source_target_pairs={{0,8},{2,10},{4,12},{6,14},{8,0},{10,2},{12,4},{14,6},{16,24},{18,... | collective-permute-start | bytes 3848 | tf_op jit(solution)/shard_map/ppermute | solution.py:33
  223.9 26.3 %all-to-all-start.2 = ((f32[16,32,320]{2,1,0:T(8,128)}), f32[16,32,320]{2,1,0:T(8,128)S(1)}, u32[]{:S(2)}, u32[]{:S(2)}) async-start(f32[16,32,320]{2,1,0:T(8,128)} %dynamic-slice_add_fusion), calls=%async_computation.2 | async-start | bytes 1572864 | tf_op jit(solution)/shard_map/all_to_all | solution.py:246
  230.3 17.5 %collective-permute-start = (f32[16,32,320]{2,1,0:T(8,128)}, f32[16,32,320]{2,1,0:T(8,128)}, u32[]{:S(2)}, u32[]{:S(2)}) collective-permute-start(f32[16,32,320]{2,1,0:T(8,128)} %constant_dynamic-slice_fusion.2), channel_id=1, source_target_pairs={{0,1},{1,0},{2,3},{3,2},{4,5},{5,4},{6,7},{7,6},{8,9},{9,8},{10,11... | collective-permute-start | bytes 1966088 | tf_op jit(solution)/shard_map/ppermute | solution.py:243
  230.3 17.3 %collective-permute-start.10 = (f32[8,2,20,2]{2,3,1,0:T(2,128)S(1)}, f32[8,2,20,2]{2,3,1,0:T(2,128)S(1)}, u32[]{:S(2)}, u32[]{:S(2)}) collective-permute-start(f32[8,2,20,2]{2,3,1,0:T(2,128)S(1)} %maximum_select_fusion.5), channel_id=1, source_target_pairs={{0,16},{2,18},{4,20},{6,22},{8,24},{10,26},{12,28},{14,30},{16,0},... | collective-permute-start | bytes 7688 | tf_op jit(solution)/shard_map/ppermute | solution.py:33
  255.3 24.6 %all-to-all-start = ((f32[16,32,320]{2,1,0:T(8,128)}), f32[16,32,320]{2,1,0:T(8,128)S(1)}, u32[]{:S(2)}, u32[]{:S(2)}) async-start(f32[16,32,320]{2,1,0:T(8,128)} %dynamic-slice_add_fusion.1), calls=%async_computation | async-start | bytes 1572864 | tf_op jit(solution)/shard_map/all_to_all | solution.py:246
  279.9 4.5 %copy-start.2 = (f32[2,8,32,320]{3,2,0,1:T(8,128)S(1)}, f32[2,8,32,320]{3,2,0,1:T(8,128)}, u32[]{:S(2)}) copy-start(f32[2,8,32,320]{3,2,0,1:T(8,128)} %copy.163) | copy-start | bytes 1966084
Sparse Core Ops, SparseCore 0:
  33.7 94.5 all-gather.6
  131.1 83.4 all-gather.4

commit v11 on v9

--- a/solution.py
+++ b/solution.py
@@ -229,10 +229,14 @@
     prefill_block = column_block.reshape(n_seq, span_len, column_width)
 
     summed_rows = lax.psum_scatter(prefill_block, "tp", scatter_dimension=1, tiled=True)
-    by_source = lax.all_to_all(summed_rows, "seq", split_axis=0, concat_axis=0, tiled=True)
+    by_source = lax.all_to_all(
+        summed_rows.astype(jnp.bfloat16), "seq", split_axis=0, concat_axis=0, tiled=True
+    )
     own_columns = lax.all_to_all(by_source, "tp", split_axis=0, concat_axis=1, tiled=True)
     projected = jnp.transpose(own_columns, (1, 0, 2)).reshape(span_len, feature_width)
-    prefill_out = (prefill_hidden.astype(jnp.float32) + projected).astype(jnp.bfloat16)
+    prefill_out = (prefill_hidden.astype(jnp.float32) + projected.astype(jnp.float32)).astype(
+        jnp.bfloat16
+    )
 
 
     return (prefill_out, decode_out, log_probs)

time: 275 us -> 258 us (0.938)
  waiting for transfers between devices: 89 us -> 77.3 us
  starting transfers between devices: 25.9 us -> 21.2 us
    ppermute x9, waiting for transfers between devices: 75 us -> 55.7 us  [doubling_gather(): other = lax.ppermute(block, axis, pairs)]
    all_to_all x1, waiting for transfers between devices: 0.01 us -> 15.2 us  [local(): lax.all_to_all(summed_rows.astype(jnp.bfloat16), 'seq', split_axis=0, con...]
    reduce_scatter x1, waiting for transfers between devices: 8.45 us -> 0.02 us  [local(): lax.psum_scatter(prefill_block, 'tp', scatter_dimension=1, tiled=True)]
  transfers between devices with their start and end apart: 12 -> 12, of which waited for: 10 -> 11; matrix products, arithmetic and copies ran while one was open for 16% -> 17% of each run, Pallas kernels for 0% -> 0%
where the time goes in v11:
time: 258 us; the launch traced here: 257 us
  waiting for transfers between devices  77.3 us (30%)
  blocking collectives  58.4 us (23%)
  matrix products  42.6 us (17%)
  local copies, waits for them, and re-layouts  31.3 us (12%)
  starting transfers between devices  21.2 us (8%)
  between operations  14.6 us (6%)
  other arithmetic  11.3 us (4%)
    ppermute x9, waiting for transfers between devices, doubling_gather(): other = lax.ppermute(block, axis, pairs)  55.7 us
    all_gather x1, blocking collectives, local(): head_all = lax.all_gather(head_part, ('seq', 'tp'), axis=0)  54.1 us
    dot_general x1, matrix products, local(): logits = jnp.dot(normed, head_weight, preferred_element_type=jnp.float32)  19.8 us
    ppermute x9, starting transfers between devices, doubling_gather(): other = lax.ppermute(block, axis, pairs)  16.1 us
    all_to_all x1, waiting for transfers between devices, local(): lax.all_to_all(summed_rows.astype(jnp.bfloat16), 'seq', split_axis=0, con...  15.2 us
    reshape x1, matrix products, local(): prefill_block = column_block.reshape(n_seq, span_len, column_width)  10.1 us
    sub x1, matrix products, local(): weights = jnp.where(live_mask, jnp.exp(masked - row_max), 0.0)  7.24 us
    unnamed x23, local copies, waits for them, and re-layouts  6.87 us
  transfers between devices with their start and end apart: 12, of which 11 were waited for; matrix products, arithmetic and copies ran while one was open for 17% of the time, Pallas kernels for 0%

profile of v11, /device:TPU:0, one launch (start us, length us, event | category | flops | bytes accessed | tf_op | source)
XLA Modules:
  0.0 256.7 jit_solution(8625440753218822371)
XLA Ops:
  7.2 1.4 dynamic_slice.14
  9.2 2.4 fusion.61
  11.6 1.4 copy.187
  13.0 1.2 copy.152
  14.2 1.0 fusion.65
  15.4 2.2 copy.154
  17.7 1.2 copy.148
  19.7 7.2 %fusion.68 = (f32[4,5,128]{2,1,0:T(8,128)S(1)}, bf16[4,5,128,896]{2,3,1,0:T(8,128)(2,1)}) fusion(pred[128,896]{0,1:T(8,128)(4,1)S(1)} %fusion.26, bf16[128,4,5,128]{0,3,2,1:T(8,128)(2,1)} %bitcast.127, bf16[128,4,128]{2,0,1:T(8,128)(2,1)S(1)} %copy.153, bf16[768,4,128]{2,0,1:T(8,128)(2,1)S(1)} %copy-done.2), kind=kOutput, calls=%fused_computation.112 | convolution fusion | flops 602801024 | bytes 6285312 | tf_op jit(solution)/shard_map/sub | solution.py:120
  27.0 3.5 %fusion.13 = bf16[128,4,5,128]{0,3,2,1:T(8,128)(2,1)S(1)} fusion(bf16[4,5,128,896]{2,3,1,0:T(8,128)(2,1)} %get-tuple-element.49, bf16[128,4,128]{0,2,1:T(8,128)(2,1)S(1)} %bitcast.131, bf16[768,4,128]{0,2,1:T(8,128)(2,1)} %bitcast.126, f32[128,4,5]{0,2,1:T(8,128)S(1)} %bitcast.141), kind=kOutput, calls=%fused_computation.14 | convolution fusion | flops 589692928 | bytes 6170624 | tf_op jit(solution)/shard_map/kgrs,skh->rkgh/dot_general | solution.py:123
  30.5 1.1 copy.157
  31.9 1.9 gather_fusion
  34.1 0.9 fusion.63
  35.0 1.3 copy.158
  37.2 1.0 subtract_convert_fusion
  40.1 4.1 %collective-permute-start = (bf16[1,11,2560]{2,1,0:T(8,128)(2,1)S(1)}, bf16[1,11,2560]{2,1,0:T(8,128)(2,1)S(1)}, u32[]{:S(2)}, u32[]{:S(2)}) collective-permute-start(bf16[1,11,2560]{2,1,0:T(8,128)(2,1)S(1)} %maximum_bitcast_fusion.9), channel_id=1, source_target_pairs={{0,16},{2,18},{4,20},{6,22},{8,24},{10,26},{12,28},{14,30},{16,0},... | collective-permute-start | bytes 168968 | tf_op jit(solution)/shard_map/ppermute | solution.py:33
  44.3 6.6 %collective-permute-done = bf16[1,11,2560]{2,1,0:T(8,128)(2,1)S(1)} collective-permute-done((bf16[1,11,2560]{2,1,0:T(8,128)(2,1)S(1)}, bf16[1,11,2560]{2,1,0:T(8,128)(2,1)S(1)}, u32[]{:S(2)}, u32[]{:S(2)}) %collective-permute-start) | collective-permute-done | bytes 56352 | tf_op jit(solution)/shard_map/ppermute | solution.py:33
  50.9 3.5 %collective-permute-start.1 = (bf16[2,11,2560]{2,1,0:T(8,128)(2,1)S(1)}, bf16[2,11,2560]{2,1,0:T(8,128)(2,1)S(1)}, u32[]{:S(2)}, u32[]{:S(2)}) collective-permute-start(bf16[2,11,2560]{2,1,0:T(8,128)(2,1)S(1)} %maximum_select_fusion.3), channel_id=1, source_target_pairs={{0,8},{2,10},{4,12},{6,14},{8,0},{10,2},{12,4},{14,6},{16,24},{18,... | collective-permute-start | bytes 337928 | tf_op jit(solution)/shard_map/ppermute | solution.py:33
  54.3 10.5 %collective-permute-done.1 = bf16[2,11,2560]{2,1,0:T(8,128)(2,1)S(1)} collective-permute-done((bf16[2,11,2560]{2,1,0:T(8,128)(2,1)S(1)}, bf16[2,11,2560]{2,1,0:T(8,128)(2,1)S(1)}, u32[]{:S(2)}, u32[]{:S(2)}) %collective-permute-start.1) | collective-permute-done | bytes 112672 | tf_op jit(solution)/shard_map/ppermute | solution.py:33
  64.9 1.8 collective-permute-start.2
  66.7 9.6 %collective-permute-done.2 = bf16[4,11,2560]{2,1,0:T(8,128)(2,1)S(1)} collective-permute-done((bf16[4,11,2560]{2,1,0:T(8,128)(2,1)S(1)}, bf16[4,11,2560]{2,1,0:T(8,128)(2,1)S(1)}, u32[]{:S(2)}, u32[]{:S(2)}) %collective-permute-start.2) | collective-permute-done | bytes 225312 | tf_op jit(solution)/shard_map/ppermute | solution.py:33
  76.7 1.6 collective-permute-start.3
  79.3 19.2 %collective-permute-done.3 = bf16[8,11,2560]{2,0,1:T(8,128)(2,1)S(1)} collective-permute-done((bf16[8,11,2560]{2,0,1:T(8,128)(2,1)S(1)}, bf16[8,11,2560]{2,0,1:T(8,128)(2,1)S(1)}, u32[]{:S(2)}, u32[]{:S(2)}) %collective-permute-start.3) | collective-permute-done | bytes 450592 | tf_op jit(solution)/shard_map/ppermute | solution.py:33
  99.1 1.0 copy.197
  100.4 0.9 copy-done.1
  102.1 1.3 mul.107
  103.4 2.4 mul.108
  105.7 1.5 fusion.24
  107.8 0.9 fusion.64
  109.4 54.1 %all-gather.1 = f32[32,20,320]{2,1,0:T(8,128)S(1)} all-gather(f32[1,20,320]{2,1,0:T(8,128)S(1)} %fusion.36), channel_id=2, replica_groups=mesh['seq'=16,'tp'=2] {'seq','tp'}, dimensions={0}, use_global_device_ids=true | all-gather | bytes 844800 | tf_op jit(solution)/shard_map/all_gather | solution.py:201
  164.1 19.8 %fusion.69 = (f32[20]{0:T(128)S(1)}, f32[20,4752]{1,0:T(8,128)S(1)}) fusion(bf16[5120,4752]{0,1:T(8,128)(2,1)} %param.27, f32[20,5120]{1,0:T(8,128)S(1)} %reshape.253, f32[5120]{0:T(1024)S(1)} %convert_element_type.150, f32[20]{0:T(128)S(1)} %add_rsqrt_fusion), kind=kOutput, calls=%fused_computation.113 | convolution fusion | flops 973611840 | bytes 49470880 | tf_op jit(solution)/shard_map/dot_general | solution.py:216
  184.1 6.3 %all-gather.4.cloned.1.call-done = bf16[16,128,2560]{2,1,0:T(8,128)(2,1)} async-done(((bf16[1,128,2560]{2,1,0:T(8,128)(2,1)}), bf16[16,128,2560]{2,1,0:T(8,128)(2,1)}) %all-gather.4.cloned.1.call-update) | async-done | bytes 10485776 | tf_op jit(solution)/shard_map/all_gather | solution.py:156
  190.4 10.1 %fusion.71 = f32[2048,320]{1,0:T(8,128)} fusion(bf16[2048,2560]{1,0:T(8,128)(2,1)} %bitcast.140, bf16[2560,320]{0,1:T(8,128)(2,1)S(1)} %copy-done), kind=kOutput, calls=%fused_computation.115 | convolution fusion | flops 3355443200 | bytes 14745600 | tf_op jit(solution)/shard_map/reshape | solution.py:229
  200.6 1.1 collective-permute-done.4
  202.5 2.8 %collective-permute-done.5 = f32[1,2,20,2]{2,3,1,0:T(2,128)S(1)} collective-permute-done((f32[1,2,20,2]{2,3,1,0:T(2,128)S(1)}, f32[1,2,20,2]{2,3,1,0:T(2,128)S(1)}, u32[]{:S(2)}, u32[]{:S(2)}) %collective-permute-start.5) | collective-permute-done | bytes 352 | tf_op jit(solution)/shard_map/ppermute | solution.py:33
  206.2 2.8 %collective-permute-done.6 = f32[2,2,20,2]{2,3,1,0:T(2,128)S(1)} collective-permute-done((f32[2,2,20,2]{2,3,1,0:T(2,128)S(1)}, f32[2,2,20,2]{2,3,1,0:T(2,128)S(1)}, u32[]{:S(2)}, u32[]{:S(2)}) %collective-permute-start.6) | collective-permute-done | bytes 672 | tf_op jit(solution)/shard_map/ppermute | solution.py:33
  209.0 1.3 collective-permute-start.7
  210.3 1.1 copy.147
  211.5 1.2 collective-permute-done.7
  212.7 2.1 collective-permute-start.8
  215.4 2.0 collective-permute-done.8
  217.6 2.4 convert_element_type.152
  220.0 4.9 %all-to-all-start = ((bf16[16,64,320]{2,1,0:T(8,128)(2,1)}), bf16[16,64,320]{2,1,0:T(8,128)(2,1)S(1)}, u32[]{:S(2)}, u32[]{:S(2)}) async-start(bf16[16,64,320]{2,1,0:T(8,128)(2,1)} %convert_element_type.152), calls=%async_computation.1 | async-start | bytes 1572864 | tf_op jit(solution)/shard_map/all_to_all | solution.py:232
  224.9 0.9 broadcast_subtract_fusion
  225.7 15.2 %all-to-all-done = bf16[16,64,320]{2,1,0:T(8,128)(2,1)S(1)} async-done(((bf16[16,64,320]{2,1,0:T(8,128)(2,1)}), bf16[16,64,320]{2,1,0:T(8,128)(2,1)S(1)}, u32[]{:S(2)}, u32[]{:S(2)}) %all-to-all-start) | async-done | bytes 655392 | tf_op jit(solution)/shard_map/all_to_all | solution.py:232
  240.9 4.4 %all_to_all.17 = bf16[16,64,320]{2,1,0:T(8,128)(2,1)S(1)} all-to-all(bf16[16,64,320]{2,1,0:T(8,128)(2,1)S(1)} %all-to-all-done), channel_id=1, replica_groups=mesh['seq'=16,'tp'=2] {'tp'}, dimensions={0} | all-to-all | bytes 1310720 | tf_op jit(solution)/shard_map/all_to_all | solution.py:235
  245.6 1.5 copy.173
  247.1 1.6 fusion.16
  248.7 1.1 copy.175
  (109 shorter events, 13.0 us)
Async XLA Ops:
  7.2 101.7 %copy-start = (bf16[2560,320]{0,1:T(8,128)(2,1)S(1)}, bf16[2560,320]{0,1:T(8,128)(2,1)}, u32[]{:S(2)}) copy-start(bf16[2560,320]{0,1:T(8,128)(2,1)} %param.25) | copy-start | bytes 4915204
  7.2 183.2 %all-gather.4.cloned.1.call-start = ((), (), s32[]{:S(2)}) async-start(), calls=%async_computation.3 | async-start | bytes 11141120 | tf_op jit(solution)/shard_map/all_gather | solution.py:156
  15.4 4.3 %copy-start.2 = (bf16[768,4,128]{2,0,1:T(8,128)(2,1)S(1)}, bf16[768,4,128]{2,0,1:T(8,128)(2,1)}, u32[]{:S(2)}) copy-start(bf16[768,4,128]{2,0,1:T(8,128)(2,1)} %copy.152) | copy-start | bytes 2359300
  30.5 1.4 copy-start.7
  31.7 185.9 %reduce-scatter.2.cloned.1.call-start = ((), (), s32[]{:S(2)}) async-start(), calls=%async_computation.4 | async-start | bytes 4718592 | tf_op jit(solution)/shard_map/reduce_scatter | solution.py:231
  34.0 2.3 copy-start.4
  34.1 2.3 copy-start.8
  40.1 10.7 %collective-permute-start = (bf16[1,11,2560]{2,1,0:T(8,128)(2,1)S(1)}, bf16[1,11,2560]{2,1,0:T(8,128)(2,1)S(1)}, u32[]{:S(2)}, u32[]{:S(2)}) collective-permute-start(bf16[1,11,2560]{2,1,0:T(8,128)(2,1)S(1)} %maximum_bitcast_fusion.9), channel_id=1, source_target_pairs={{0,16},{2,18},{4,20},{6,22},{8,24},{10,26},{12,28},{14,30},{16,0},... | collective-permute-start | bytes 168968 | tf_op jit(solution)/shard_map/ppermute | solution.py:33
  44.3 34.1 %copy-start.6 = (bf16[2,4,512]{2,1,0:T(4,128)(2,1)S(1)}, bf16[2,4,512]{2,1,0:T(4,128)(2,1)}, u32[]{:S(2)}) copy-start(bf16[2,4,512]{2,1,0:T(4,128)(2,1)} %param.21) | copy-start | bytes 24580
  50.9 27.6 %copy-start.5 = (bf16[5120]{0:T(1024)(128)(2,1)S(1)}, bf16[5120]{0:T(1024)(128)(2,1)}, u32[]{:S(2)}) copy-start(bf16[5120]{0:T(1024)(128)(2,1)} %param.26) | copy-start | bytes 30724
  50.9 14.0 %collective-permute-start.1 = (bf16[2,11,2560]{2,1,0:T(8,128)(2,1)S(1)}, bf16[2,11,2560]{2,1,0:T(8,128)(2,1)S(1)}, u32[]{:S(2)}, u32[]{:S(2)}) collective-permute-start(bf16[2,11,2560]{2,1,0:T(8,128)(2,1)S(1)} %maximum_select_fusion.3), channel_id=1, source_target_pairs={{0,8},{2,10},{4,12},{6,14},{8,0},{10,2},{12,4},{14,6},{16,24},{18,... | collective-permute-start | bytes 337928 | tf_op jit(solution)/shard_map/ppermute | solution.py:33
  64.9 11.4 %collective-permute-start.2 = (bf16[4,11,2560]{2,1,0:T(8,128)(2,1)S(1)}, bf16[4,11,2560]{2,1,0:T(8,128)(2,1)S(1)}, u32[]{:S(2)}, u32[]{:S(2)}) collective-permute-start(bf16[4,11,2560]{2,1,0:T(8,128)(2,1)S(1)} %maximum_select_fusion.2), channel_id=1, source_target_pairs={{0,4},{2,6},{4,0},{6,2},{8,12},{10,14},{12,8},{14,10},{16,20},{18,... | collective-permute-start | bytes 675848 | tf_op jit(solution)/shard_map/ppermute | solution.py:33
  76.7 21.8 %collective-permute-start.3 = (bf16[8,11,2560]{2,0,1:T(8,128)(2,1)S(1)}, bf16[8,11,2560]{2,0,1:T(8,128)(2,1)S(1)}, u32[]{:S(2)}, u32[]{:S(2)}) collective-permute-start(bf16[8,11,2560]{2,0,1:T(8,128)(2,1)S(1)} %copy.162), channel_id=1, source_target_pairs={{0,2},{2,0},{4,6},{6,4},{8,10},{10,8},{12,14},{14,12},{16,18},{18,... | collective-permute-start | bytes 1351688 | tf_op jit(solution)/shard_map/ppermute | solution.py:33
  100.4 0.9 copy-start.1
  200.5 9.8 %copy-start.3 = (bf16[128,2560]{1,0:T(8,128)(2,1)S(1)}, bf16[128,2560]{1,0:T(8,128)(2,1)}, u32[]{:S(2)}) copy-start(bf16[128,2560]{1,0:T(8,128)(2,1)} %param.14) | copy-start | bytes 1966084
  200.5 1.2 collective-permute-start.4
  201.8 3.6 %collective-permute-start.5 = (f32[1,2,20,2]{2,3,1,0:T(2,128)S(1)}, f32[1,2,20,2]{2,3,1,0:T(2,128)S(1)}, u32[]{:S(2)}, u32[]{:S(2)}) collective-permute-start(f32[1,2,20,2]{2,3,1,0:T(2,128)S(1)} %maximum_select_fusion.8), channel_id=1, source_target_pairs={{0,2},{2,0},{4,6},{6,4},{8,10},{10,8},{12,14},{14,12},{16,18},{18,... | collective-permute-start | bytes 968 | tf_op jit(solution)/shard_map/ppermute | solution.py:33
  205.4 3.6 %collective-permute-start.6 = (f32[2,2,20,2]{2,3,1,0:T(2,128)S(1)}, f32[2,2,20,2]{2,3,1,0:T(2,128)S(1)}, u32[]{:S(2)}, u32[]{:S(2)}) collective-permute-start(f32[2,2,20,2]{2,3,1,0:T(2,128)S(1)} %maximum_select_fusion.7), channel_id=1, source_target_pairs={{0,4},{2,6},{4,0},{6,2},{8,12},{10,14},{12,8},{14,10},{16,20},{18,... | collective-permute-start | bytes 1928 | tf_op jit(solution)/shard_map/ppermute | solution.py:33
  209.0 3.7 %collective-permute-start.7 = (f32[4,2,20,2]{2,3,1,0:T(2,128)S(1)}, f32[4,2,20,2]{2,3,1,0:T(2,128)S(1)}, u32[]{:S(2)}, u32[]{:S(2)}) collective-permute-start(f32[4,2,20,2]{2,3,1,0:T(2,128)S(1)} %maximum_select_fusion.6), channel_id=1, source_target_pairs={{0,8},{2,10},{4,12},{6,14},{8,0},{10,2},{12,4},{14,6},{16,24},{18,... | collective-permute-start | bytes 3848 | tf_op jit(solution)/shard_map/ppermute | solution.py:33
  212.7 4.7 %collective-permute-start.8 = (f32[8,2,20,2]{2,3,1,0:T(2,128)S(1)}, f32[8,2,20,2]{2,3,1,0:T(2,128)S(1)}, u32[]{:S(2)}, u32[]{:S(2)}) collective-permute-start(f32[8,2,20,2]{2,3,1,0:T(2,128)S(1)} %maximum_select_fusion.5), channel_id=1, source_target_pairs={{0,16},{2,18},{4,20},{6,22},{8,24},{10,26},{12,28},{14,30},{16,0},... | collective-permute-start | bytes 7688 | tf_op jit(solution)/shard_map/ppermute | solution.py:33
  220.0 20.9 %all-to-all-start = ((bf16[16,64,320]{2,1,0:T(8,128)(2,1)}), bf16[16,64,320]{2,1,0:T(8,128)(2,1)S(1)}, u32[]{:S(2)}, u32[]{:S(2)}) async-start(bf16[16,64,320]{2,1,0:T(8,128)(2,1)} %convert_element_type.152), calls=%async_computation.1 | async-start | bytes 1572864 | tf_op jit(solution)/shard_map/all_to_all | solution.py:232
Sparse Core Ops, SparseCore 0:
  31.8 158.6 all-gather.3
  200.7 10.2 reduce-scatter.1

commit v12 on v11

--- a/solution.py
+++ b/solution.py
@@ -131,7 +131,6 @@
     sum_high = decode_sum.astype(jnp.bfloat16)
     sum_low = (decode_sum - sum_high.astype(jnp.float32)).astype(jnp.bfloat16)
     mixed_high = decode_mixed.astype(jnp.bfloat16)
-    mixed_low = (decode_mixed - mixed_high.astype(jnp.float32)).astype(jnp.bfloat16)
     stat_count = decode_sum.size
     decode_flat = jnp.concatenate(
         [
@@ -139,7 +138,6 @@
             sum_high.reshape(-1),
             sum_low.reshape(-1),
             mixed_high.reshape(-1),
-            mixed_low.reshape(-1),
         ]
     )
     extra_rows = -(-decode_flat.size // feature_width)
@@ -165,7 +163,6 @@
     mixed_at = 3 * stat_count
     part_mixed = (
         every_flat[:, mixed_at : mixed_at + mixed_count]
-        + every_flat[:, mixed_at + mixed_count : mixed_at + 2 * mixed_count]
     ).reshape((n_seq,) + decode_mixed.shape)
 
     best = jnp.max(part_max, axis=0)

time: 258 us -> 249 us (0.965)
  waiting for transfers between devices: 77.3 us -> 63.1 us
  blocking collectives: 58.4 us -> 63.2 us
    ppermute x9, waiting for transfers between devices: 55.7 us -> 31.3 us  [doubling_gather(): other = lax.ppermute(block, axis, pairs)]
    all_gather x1, waiting for transfers between devices: 6.28 us -> 16.6 us  [local(): lax.all_gather(prefill_attention, 'seq', axis=0)]
    all_gather x1, blocking collectives: 54.1 us -> 58.8 us  [local(): head_all = lax.all_gather(head_part, ('seq', 'tp'), axis=0)]
    unnamed x23 -> x29, local copies, waits for them, and re-layouts: 6.87 us -> 6.29 us
where the time goes in v12:
time: 249 us; the launch traced here: 248 us
  blocking collectives  63.2 us (25%)
  waiting for transfers between devices  63.1 us (25%)
  matrix products  43.2 us (17%)
  local copies, waits for them, and re-layouts  30.2 us (12%)
  starting transfers between devices  21.5 us (9%)
  between operations  14.6 us (6%)
  other arithmetic  12.1 us (5%)
    all_gather x1, blocking collectives, local(): head_all = lax.all_gather(head_part, ('seq', 'tp'), axis=0)  58.8 us
    ppermute x9, waiting for transfers between devices, doubling_gather(): other = lax.ppermute(block, axis, pairs)  31.3 us
    dot_general x1, matrix products, local(): logits = jnp.dot(normed, head_weight, preferred_element_type=jnp.float32)  19.8 us
    all_gather x1, waiting for transfers between devices, local(): lax.all_gather(prefill_attention, 'seq', axis=0)  16.6 us
    ppermute x9, starting transfers between devices, doubling_gather(): other = lax.ppermute(block, axis, pairs)  15.9 us
    all_to_all x1, waiting for transfers between devices, local(): lax.all_to_all(summed_rows.astype(jnp.bfloat16), 'seq', split_axis=0, con...  15.2 us
    reshape x1, matrix products, local(): prefill_block = column_block.reshape(n_seq, span_len, column_width)  10.1 us
    sub x1, matrix products, local(): weights = jnp.where(live_mask, jnp.exp(masked - row_max), 0.0)  7.45 us
  transfers between devices with their start and end apart: 12, of which 11 were waited for; matrix products, arithmetic and copies ran while one was open for 17% of the time, Pallas kernels for 0%

profile of v12, /device:TPU:0, one launch (start us, length us, event | category | flops | bytes accessed | tf_op | source)
XLA Modules:
  0.0 247.9 jit_solution(8680109107527782118)
XLA Ops:
  7.2 1.4 dynamic_slice.14
  9.3 2.4 fusion.59
  11.6 1.4 copy.178
  13.0 1.2 copy.146
  14.2 1.0 fusion.63
  16.1 2.2 copy.148
  18.3 1.2 copy.142
  20.2 1.4 fusion.25
  21.6 7.4 %fusion.66 = (f32[4,5,128]{2,1,0:T(8,128)S(1)}, bf16[4,5,128,896]{2,3,1,0:T(8,128)(2,1)}) fusion(pred[128,896]{0,1:T(8,128)(4,1)} %fusion.25, bf16[128,4,5,128]{0,3,2,1:T(8,128)(2,1)} %bitcast.126, bf16[128,4,128]{2,0,1:T(8,128)(2,1)S(1)} %copy-done.5, bf16[768,4,128]{2,0,1:T(8,128)(2,1)S(1)} %copy-done.2), kind=kOutput, calls=%fused_computation.110 | convolution fusion | flops 602801024 | bytes 6285312 | tf_op jit(solution)/shard_map/sub | solution.py:120
  29.0 3.3 %fusion.13 = bf16[128,4,5,128]{0,3,2,1:T(8,128)(2,1)S(1)} fusion(bf16[4,5,128,896]{2,3,1,0:T(8,128)(2,1)} %get-tuple-element.47, bf16[128,4,128]{0,2,1:T(8,128)(2,1)S(1)} %bitcast.131, bf16[768,4,128]{0,2,1:T(8,128)(2,1)S(1)} %bitcast.125, f32[128,4,5]{0,2,1:T(8,128)S(1)} %bitcast.141), kind=kOutput, calls=%fused_computation.13 | convolution fusion | flops 589692928 | bytes 6170624 | tf_op jit(solution)/shard_map/kgrs,skh->rkgh/dot_general | solution.py:123
  32.3 1.1 copy.151
  33.7 1.9 gather_fusion
  35.9 0.9 fusion.60
  36.8 1.3 copy.152
  39.0 1.0 convolution_convert_fusion
  41.8 4.1 %collective-permute-start = (bf16[1,7,2560]{2,1,0:T(8,128)(2,1)S(1)}, bf16[1,7,2560]{2,1,0:T(8,128)(2,1)S(1)}, u32[]{:S(2)}, u32[]{:S(2)}) collective-permute-start(bf16[1,7,2560]{2,1,0:T(8,128)(2,1)S(1)} %maximum_bitcast_fusion.9), channel_id=1, source_target_pairs={{0,16},{2,18},{4,20},{6,22},{8,24},{10,26},{12,28},{14,30},{16,0},... | collective-permute-start | bytes 107528 | tf_op jit(solution)/shard_map/ppermute | solution.py:33
  45.9 2.5 %collective-permute-done = bf16[1,7,2560]{2,1,0:T(8,128)(2,1)S(1)} collective-permute-done((bf16[1,7,2560]{2,1,0:T(8,128)(2,1)S(1)}, bf16[1,7,2560]{2,1,0:T(8,128)(2,1)S(1)}, u32[]{:S(2)}, u32[]{:S(2)}) %collective-permute-start) | collective-permute-done | bytes 35872 | tf_op jit(solution)/shard_map/ppermute | solution.py:33
  48.5 3.2 %collective-permute-start.1 = (bf16[2,7,2560]{2,1,0:T(8,128)(2,1)S(1)}, bf16[2,7,2560]{2,1,0:T(8,128)(2,1)S(1)}, u32[]{:S(2)}, u32[]{:S(2)}) collective-permute-start(bf16[2,7,2560]{2,1,0:T(8,128)(2,1)S(1)} %maximum_select_fusion.3), channel_id=1, source_target_pairs={{0,8},{2,10},{4,12},{6,14},{8,0},{10,2},{12,4},{14,6},{16,24},{18,... | collective-permute-start | bytes 215048 | tf_op jit(solution)/shard_map/ppermute | solution.py:33
  51.7 7.9 %collective-permute-done.1 = bf16[2,7,2560]{2,1,0:T(8,128)(2,1)S(1)} collective-permute-done((bf16[2,7,2560]{2,1,0:T(8,128)(2,1)S(1)}, bf16[2,7,2560]{2,1,0:T(8,128)(2,1)S(1)}, u32[]{:S(2)}, u32[]{:S(2)}) %collective-permute-start.1) | collective-permute-done | bytes 71712 | tf_op jit(solution)/shard_map/ppermute | solution.py:33
  59.6 1.7 collective-permute-start.2
  61.4 3.6 %collective-permute-done.2 = bf16[4,7,2560]{2,1,0:T(8,128)(2,1)S(1)} collective-permute-done((bf16[4,7,2560]{2,1,0:T(8,128)(2,1)S(1)}, bf16[4,7,2560]{2,1,0:T(8,128)(2,1)S(1)}, u32[]{:S(2)}, u32[]{:S(2)}) %collective-permute-start.2) | collective-permute-done | bytes 143392 | tf_op jit(solution)/shard_map/ppermute | solution.py:33
  65.1 1.6 collective-permute-start.3
  68.2 7.6 %collective-permute-done.3 = bf16[8,7,2560]{2,1,0:T(8,128)(2,1)S(1)} collective-permute-done((bf16[8,7,2560]{2,1,0:T(8,128)(2,1)S(1)}, bf16[8,7,2560]{2,1,0:T(8,128)(2,1)S(1)}, u32[]{:S(2)}, u32[]{:S(2)}) %collective-permute-start.3) | collective-permute-done | bytes 286752 | tf_op jit(solution)/shard_map/ppermute | solution.py:33
  78.6 1.2 mul.107
  79.8 1.1 mul.108
  80.9 1.3 fusion.23
  83.5 0.9 fusion.62
  85.1 58.8 %all-gather.1 = f32[32,20,320]{2,1,0:T(8,128)S(1)} all-gather(f32[1,20,320]{2,1,0:T(8,128)S(1)} %fusion.35), channel_id=2, replica_groups=mesh['seq'=16,'tp'=2] {'seq','tp'}, dimensions={0}, use_global_device_ids=true | all-gather | bytes 844800 | tf_op jit(solution)/shard_map/all_gather | solution.py:198
  144.5 19.8 %fusion.67 = (f32[20]{0:T(128)S(1)}, f32[20,4752]{1,0:T(8,128)S(1)}) fusion(bf16[5120,4752]{0,1:T(8,128)(2,1)} %param.27, f32[20,5120]{1,0:T(8,128)S(1)} %reshape.249, f32[5120]{0:T(1024)S(1)} %convert_element_type.142, f32[20]{0:T(128)S(1)} %add_rsqrt_fusion), kind=kOutput, calls=%fused_computation.111 | convolution fusion | flops 973611840 | bytes 49470880 | tf_op jit(solution)/shard_map/dot_general | solution.py:213
  164.6 16.6 %all-gather.4.cloned.1.call-done = bf16[16,128,2560]{2,1,0:T(8,128)(2,1)} async-done(((bf16[1,128,2560]{2,1,0:T(8,128)(2,1)}), bf16[16,128,2560]{2,1,0:T(8,128)(2,1)}) %all-gather.4.cloned.1.call-update) | async-done | bytes 10485776 | tf_op jit(solution)/shard_map/all_gather | solution.py:154
  181.2 10.1 %fusion.69 = f32[2048,320]{1,0:T(8,128)} fusion(bf16[2048,2560]{1,0:T(8,128)(2,1)} %bitcast.140, bf16[2560,320]{0,1:T(8,128)(2,1)S(1)} %copy-done), kind=kOutput, calls=%fused_computation.113 | convolution fusion | flops 3355443200 | bytes 14745600 | tf_op jit(solution)/shard_map/reshape | solution.py:226
  191.3 1.1 collective-permute-done.4
  192.5 1.6 collective-permute-start.5
  194.1 2.0 collective-permute-done.5
  196.6 3.1 %collective-permute-done.6 = f32[2,2,20,2]{2,3,1,0:T(2,128)S(1)} collective-permute-done((f32[2,2,20,2]{2,3,1,0:T(2,128)S(1)}, f32[2,2,20,2]{2,3,1,0:T(2,128)S(1)}, u32[]{:S(2)}, u32[]{:S(2)}) %collective-permute-start.6) | collective-permute-done | bytes 672 | tf_op jit(solution)/shard_map/ppermute | solution.py:33
  199.7 1.3 collective-permute-start.7
  201.0 1.1 copy.141
  202.2 1.2 collective-permute-done.7
  203.4 1.9 collective-permute-start.8
  205.9 2.2 collective-permute-done.8
  208.3 2.4 convert_element_type.144
  210.7 5.4 %all-to-all-start = ((bf16[16,64,320]{2,1,0:T(8,128)(2,1)}), bf16[16,64,320]{2,1,0:T(8,128)(2,1)S(1)}, u32[]{:S(2)}, u32[]{:S(2)}) async-start(bf16[16,64,320]{2,1,0:T(8,128)(2,1)} %convert_element_type.144), calls=%async_computation.1 | async-start | bytes 1572864 | tf_op jit(solution)/shard_map/all_to_all | solution.py:229
  216.1 0.9 broadcast_subtract_fusion
  217.0 15.2 %all-to-all-done = bf16[16,64,320]{2,1,0:T(8,128)(2,1)S(1)} async-done(((bf16[16,64,320]{2,1,0:T(8,128)(2,1)}), bf16[16,64,320]{2,1,0:T(8,128)(2,1)S(1)}, u32[]{:S(2)}, u32[]{:S(2)}) %all-to-all-start) | async-done | bytes 655392 | tf_op jit(solution)/shard_map/all_to_all | solution.py:229
  232.2 4.4 %all_to_all.17 = bf16[16,64,320]{2,1,0:T(8,128)(2,1)S(1)} all-to-all(bf16[16,64,320]{2,1,0:T(8,128)(2,1)S(1)} %all-to-all-done), channel_id=1, replica_groups=mesh['seq'=16,'tp'=2] {'tp'}, dimensions={0} | all-to-all | bytes 1310720 | tf_op jit(solution)/shard_map/all_to_all | solution.py:232
  236.8 1.5 copy.164
  238.4 1.6 fusion.16
  240.0 1.1 copy.166
  (112 shorter events, 14.4 us)
Async XLA Ops:
  7.2 77.4 %copy-start = (bf16[2560,320]{0,1:T(8,128)(2,1)S(1)}, bf16[2560,320]{0,1:T(8,128)(2,1)}, u32[]{:S(2)}) copy-start(bf16[2560,320]{0,1:T(8,128)(2,1)} %param.25) | copy-start | bytes 4915204
  7.2 174.0 %all-gather.4.cloned.1.call-start = ((), (), s32[]{:S(2)}) async-start(), calls=%async_computation.3 | async-start | bytes 11141120 | tf_op jit(solution)/shard_map/all_gather | solution.py:154
  15.3 6.3 %copy-start.2 = (bf16[768,4,128]{2,0,1:T(8,128)(2,1)S(1)}, bf16[768,4,128]{2,0,1:T(8,128)(2,1)}, u32[]{:S(2)}) copy-start(bf16[768,4,128]{2,0,1:T(8,128)(2,1)} %copy.146) | copy-start | bytes 2359300
  16.1 5.5 %copy-start.5 = (bf16[128,4,128]{2,0,1:T(8,128)(2,1)S(1)}, bf16[128,4,128]{2,0,1:T(8,128)(2,1)}, u32[]{:S(2)}) copy-start(bf16[128,4,128]{2,0,1:T(8,128)(2,1)} %copy.147) | copy-start | bytes 393220
  21.6 7.5 %copy-start.3 = (bf16[1,1,768,512]{2,3,1,0:T(8,128)(2,1)S(1)}, bf16[1,1,768,512]{2,3,1,0:T(8,128)(2,1)}, u32[]{:S(2)}) copy-start(bf16[1,1,768,512]{2,3,1,0:T(8,128)(2,1)} %copy.142) | copy-start | bytes 2359300
  21.6 7.5 %copy-start.6 = (bf16[1,128,512]{1,2,0:T(8,128)(2,1)S(1)}, bf16[1,128,512]{1,2,0:T(8,128)(2,1)}, u32[]{:S(2)}) copy-start(bf16[1,128,512]{1,2,0:T(8,128)(2,1)} %copy.143) | copy-start | bytes 393220
  32.3 1.4 copy-start.10
  33.4 174.8 %reduce-scatter.2.cloned.1.call-start = ((), (), s32[]{:S(2)}) async-start(), calls=%async_computation.4 | async-start | bytes 4718592 | tf_op jit(solution)/shard_map/reduce_scatter | solution.py:228
  35.8 2.3 copy-start.7
  35.8 2.3 copy-start.11
  38.6 22.7 %copy-start.9 = (bf16[2,4,512]{2,1,0:T(4,128)(2,1)S(1)}, bf16[2,4,512]{2,1,0:T(4,128)(2,1)}, u32[]{:S(2)}) copy-start(bf16[2,4,512]{2,1,0:T(4,128)(2,1)} %param.21) | copy-start | bytes 24580
  38.6 22.8 %copy-start.8 = (bf16[5120]{0:T(1024)(128)(2,1)S(1)}, bf16[5120]{0:T(1024)(128)(2,1)}, u32[]{:S(2)}) copy-start(bf16[5120]{0:T(1024)(128)(2,1)} %param.26) | copy-start | bytes 30724
  41.8 6.7 %collective-permute-start = (bf16[1,7,2560]{2,1,0:T(8,128)(2,1)S(1)}, bf16[1,7,2560]{2,1,0:T(8,128)(2,1)S(1)}, u32[]{:S(2)}, u32[]{:S(2)}) collective-permute-start(bf16[1,7,2560]{2,1,0:T(8,128)(2,1)S(1)} %maximum_bitcast_fusion.9), channel_id=1, source_target_pairs={{0,16},{2,18},{4,20},{6,22},{8,24},{10,26},{12,28},{14,30},{16,0},... | collective-permute-start | bytes 107528 | tf_op jit(solution)/shard_map/ppermute | solution.py:33
  48.5 11.1 %collective-permute-start.1 = (bf16[2,7,2560]{2,1,0:T(8,128)(2,1)S(1)}, bf16[2,7,2560]{2,1,0:T(8,128)(2,1)S(1)}, u32[]{:S(2)}, u32[]{:S(2)}) collective-permute-start(bf16[2,7,2560]{2,1,0:T(8,128)(2,1)S(1)} %maximum_select_fusion.3), channel_id=1, source_target_pairs={{0,8},{2,10},{4,12},{6,14},{8,0},{10,2},{12,4},{14,6},{16,24},{18,... | collective-permute-start | bytes 215048 | tf_op jit(solution)/shard_map/ppermute | solution.py:33
  59.6 5.4 %collective-permute-start.2 = (bf16[4,7,2560]{2,1,0:T(8,128)(2,1)S(1)}, bf16[4,7,2560]{2,1,0:T(8,128)(2,1)S(1)}, u32[]{:S(2)}, u32[]{:S(2)}) collective-permute-start(bf16[4,7,2560]{2,1,0:T(8,128)(2,1)S(1)} %maximum_select_fusion.2), channel_id=1, source_target_pairs={{0,4},{2,6},{4,0},{6,2},{8,12},{10,14},{12,8},{14,10},{16,20},{18,... | collective-permute-start | bytes 430088 | tf_op jit(solution)/shard_map/ppermute | solution.py:33
  65.1 10.6 %collective-permute-start.3 = (bf16[8,7,2560]{2,1,0:T(8,128)(2,1)S(1)}, bf16[8,7,2560]{2,1,0:T(8,128)(2,1)S(1)}, u32[]{:S(2)}, u32[]{:S(2)}) collective-permute-start(bf16[8,7,2560]{2,1,0:T(8,128)(2,1)S(1)} %maximum_select_fusion.1), channel_id=1, source_target_pairs={{0,2},{2,0},{4,6},{6,4},{8,10},{10,8},{12,14},{14,12},{16,18},{18,... | collective-permute-start | bytes 860168 | tf_op jit(solution)/shard_map/ppermute | solution.py:33
  76.9 0.8 copy-start.1
  191.2 9.8 %copy-start.4 = (bf16[128,2560]{1,0:T(8,128)(2,1)S(1)}, bf16[128,2560]{1,0:T(8,128)(2,1)}, u32[]{:S(2)}) copy-start(bf16[128,2560]{1,0:T(8,128)(2,1)} %param.14) | copy-start | bytes 1966084
  191.3 1.2 collective-permute-start.4
  192.5 3.6 %collective-permute-start.5 = (f32[1,2,20,2]{2,3,1,0:T(2,128)S(1)}, f32[1,2,20,2]{2,3,1,0:T(2,128)S(1)}, u32[]{:S(2)}, u32[]{:S(2)}) collective-permute-start(f32[1,2,20,2]{2,3,1,0:T(2,128)S(1)} %maximum_select_fusion.8), channel_id=1, source_target_pairs={{0,2},{2,0},{4,6},{6,4},{8,10},{10,8},{12,14},{14,12},{16,18},{18,... | collective-permute-start | bytes 968 | tf_op jit(solution)/shard_map/ppermute | solution.py:33
  196.1 3.6 %collective-permute-start.6 = (f32[2,2,20,2]{2,3,1,0:T(2,128)S(1)}, f32[2,2,20,2]{2,3,1,0:T(2,128)S(1)}, u32[]{:S(2)}, u32[]{:S(2)}) collective-permute-start(f32[2,2,20,2]{2,3,1,0:T(2,128)S(1)} %maximum_select_fusion.7), channel_id=1, source_target_pairs={{0,4},{2,6},{4,0},{6,2},{8,12},{10,14},{12,8},{14,10},{16,20},{18,... | collective-permute-start | bytes 1928 | tf_op jit(solution)/shard_map/ppermute | solution.py:33
  199.7 3.7 %collective-permute-start.7 = (f32[4,2,20,2]{2,3,1,0:T(2,128)S(1)}, f32[4,2,20,2]{2,3,1,0:T(2,128)S(1)}, u32[]{:S(2)}, u32[]{:S(2)}) collective-permute-start(f32[4,2,20,2]{2,3,1,0:T(2,128)S(1)} %maximum_select_fusion.6), channel_id=1, source_target_pairs={{0,8},{2,10},{4,12},{6,14},{8,0},{10,2},{12,4},{14,6},{16,24},{18,... | collective-permute-start | bytes 3848 | tf_op jit(solution)/shard_map/ppermute | solution.py:33
  203.4 4.7 %collective-permute-start.8 = (f32[8,2,20,2]{2,3,1,0:T(2,128)S(1)}, f32[8,2,20,2]{2,3,1,0:T(2,128)S(1)}, u32[]{:S(2)}, u32[]{:S(2)}) collective-permute-start(f32[8,2,20,2]{2,3,1,0:T(2,128)S(1)} %maximum_select_fusion.5), channel_id=1, source_target_pairs={{0,16},{2,18},{4,20},{6,22},{8,24},{10,26},{12,28},{14,30},{16,0},... | collective-permute-start | bytes 7688 | tf_op jit(solution)/shard_map/ppermute | solution.py:33
  210.7 21.5 %all-to-all-start = ((bf16[16,64,320]{2,1,0:T(8,128)(2,1)}), bf16[16,64,320]{2,1,0:T(8,128)(2,1)S(1)}, u32[]{:S(2)}, u32[]{:S(2)}) async-start(bf16[16,64,320]{2,1,0:T(8,128)(2,1)} %convert_element_type.144), calls=%async_computation.1 | async-start | bytes 1572864 | tf_op jit(solution)/shard_map/all_to_all | solution.py:229
Sparse Core Ops, SparseCore 0:
  33.6 147.5 all-gather.3
  191.4 10.8 reduce-scatter.1
